TPU v7x, 256 devices: a whole 4x4x8 slice. The times are simulated.
256 devices in a mesh: space: 64 (over x, y, z_hi), chan: 4 (over z_lo, core).
Axes of the slice: x: 4, y: 4, z: 8 (z_hi: 4, z_lo: 2; z = z_hi * 2 + z_lo), core: 2. Of those that a mesh axis runs over, the one named last changes fastest.
Arguments:
- voxels: bfloat16 [32, 128, 16, 512], P(None, 'space'), may hold values from -6 to 6
- first_filters: bfloat16 [3, 3, 3, 64, 32], P(None, None, None, 'chan'), may hold values from -0.21875 to 0.21875
- second_filters: bfloat16 [3, 3, 3, 64, 64], P(None, None, None, 'chan'), may hold values from -0.15625 to 0.15625
Outputs:
- filtered: bfloat16 [64, 128, 16, 512], P('chan', 'space')
All inputs are finite; a program needn't handle non-finite values.
Results may differ from a plain program's by a relative error of at most 0.0049.
Values may be sent and summed in bfloat16 or wider, within the bound.
No kernel may reach another device: no remote copies, remote signals or barrier semaphores. Data moves between devices by JAX's collectives and lax.ppermute only.
A program may use at most 64 MiB of HBM per device.

v0:
```python
import jax
import jax.numpy as jnp
from jax import lax
from jax.sharding import PartitionSpec as P

GH = 8


def passed_along(value, axis, steps):
    count = lax.axis_size(axis)
    pairs = [(source, (source + steps) % count) for source in range(count)]
    return lax.ppermute(value, axis, pairs)


def widen(volume_tile):
    zero_col = jnp.zeros(volume_tile.shape[:3] + (1,), volume_tile.dtype)
    left_shift = jnp.concatenate([zero_col, volume_tile[..., :-1]], 3)
    right_shift = jnp.concatenate([volume_tile[..., 1:], zero_col], 3)
    return jnp.concatenate([left_shift, volume_tile, right_shift], 0)


def tile_border(volume_tile, above, below, front, back):
    tile_count = lax.axis_size("space")
    position = (lax.axis_index("space") + GH + GH // 4) % tile_count
    tile_row = position % GH
    depth_tile = position // GH
    grid_depth = tile_count // GH
    above_rim = above(volume_tile[:, :, -1:, :])
    below_rim = below(volume_tile[:, :, :1, :])
    above_rim = jnp.where(tile_row > 0, above_rim, jnp.zeros_like(above_rim))
    below_rim = jnp.where(tile_row < GH - 1, below_rim, jnp.zeros_like(below_rim))
    taller = jnp.concatenate([above_rim, volume_tile, below_rim], 2)
    front_rim = front(taller[:, -1:])
    back_rim = back(taller[:, :1])
    front_rim = jnp.where(depth_tile > 0, front_rim, jnp.zeros_like(front_rim))
    back_rim = jnp.where(depth_tile < grid_depth - 1, back_rim, jnp.zeros_like(back_rim))
    return jnp.concatenate([front_rim, taller, back_rim], 1)


def input_above(rim_cells):
    return passed_along(rim_cells, "space", 1)


def input_below(rim_cells):
    return passed_along(rim_cells, "space", -1)


def input_front(rim_cells):
    return passed_along(rim_cells, "space", GH)


def input_back(rim_cells):
    return passed_along(rim_cells, "space", -GH)


def hidden_above(rim_cells):
    return passed_along(rim_cells, "space", 1)


def hidden_below(rim_cells):
    return passed_along(rim_cells, "space", -1)


def hidden_front(rim_cells):
    return passed_along(rim_cells, "space", GH)


def hidden_back(rim_cells):
    return passed_along(rim_cells, "space", -GH)


def correlate(stacked, filters, depth_rows, height_rows):
    out_count = filters.shape[3]
    running = jnp.zeros((out_count, depth_rows, height_rows, stacked.shape[3]), jnp.float32)
    for depth_tap in range(3):
        for height_tap in range(3):
            matrix = filters[depth_tap, height_tap].transpose(1, 0, 2).reshape(out_count, -1)
            window = stacked[
                :, depth_tap : depth_tap + depth_rows, height_tap : height_tap + height_rows, :
            ]
            running = running + jnp.einsum(
                "ok,kdhw->odhw", matrix, window, preferred_element_type=jnp.float32
            )
    return running


def local(voxels, first_filters, second_filters):
    depth_rows = voxels.shape[1]
    height_rows = voxels.shape[2]
    padded = tile_border(voxels, input_above, input_below, input_front, input_back)
    hidden = jax.nn.relu(correlate(widen(padded), first_filters, depth_rows, height_rows)).astype(
        jnp.bfloat16
    )
    hidden_pad = tile_border(hidden, hidden_above, hidden_below, hidden_front, hidden_back)
    summed = correlate(
        widen(lax.all_gather(hidden_pad, "chan", axis=0, tiled=True)),
        second_filters,
        depth_rows,
        height_rows,
    )
    return jax.nn.relu(summed).astype(jnp.bfloat16)


def solution(mesh):
    return jax.shard_map(
        local,
        mesh=mesh,
        in_specs=(
            P(None, "space", None, None),
            P(None, None, None, "chan", None),
            P(None, None, None, "chan", None),
        ),
        out_specs=P("chan", "space", None, None),
        check_vma=False,
    )
```

profile of v0, /device:TPU:1, one launch (start us, length us, event | category | flops | bytes accessed | tf_op | source)
XLA Modules:
  0.0 173.7 jit_solution(5258099566370104163)
XLA Ops:
  6.5 1.8 %copy.26 = bf16[32,2,16,512]{3,0,2,1:T(8,128)(2,1)S(1)} copy(bf16[32,2,16,512]{3,2,1,0:T(8,128)(2,1)} %param.3) | data formatting | bytes 2097152 | tf_op args[0]
  8.4 3.9 %collective-permute-start = (bf16[32,2,1,512]{3,0,2,1:T(8,128)(2,1)S(1)}, bf16[32,2,1,512]{3,0,2,1:T(8,128)(2,1)S(1)}, u32[]{:S(2)}, u32[]{:S(2)}) collective-permute-start(bf16[32,2,1,512]{3,0,2,1:T(8,128)(2,1)S(1)} %get-tuple-element.11), channel_id=1, source_target_pairs={{0,4},{4,8},{8,12},{12,16},{16,20},{20,24},{24,28},{28,32},{32,36}... | collective-permute-start | bytes 196616 | tf_op jit(solution)/shard_map/ppermute | solution.py:12
  12.2 7.8 %collective-permute-start.1 = (bf16[32,2,1,512]{3,0,2,1:T(8,128)(2,1)S(1)}, bf16[32,2,1,512]{3,0,2,1:T(8,128)(2,1)S(1)}, u32[]{:S(2)}, u32[]{:S(2)}) collective-permute-start(bf16[32,2,1,512]{3,0,2,1:T(8,128)(2,1)S(1)} %get-tuple-element.12), channel_id=1, source_target_pairs={{0,252},{4,0},{8,4},{12,8},{16,12},{20,16},{24,20},{28,24},{32,28}... | collective-permute-start | bytes 196616 | tf_op jit(solution)/shard_map/ppermute | solution.py:12
  20.0 1.7 collective-permute-done
  22.5 4.6 %collective-permute-start.3 = (bf16[32,1,18,512]{3,0,2,1:T(8,128)(2,1)S(1)}, bf16[32,1,18,512]{3,0,2,1:T(8,128)(2,1)S(1)}, u32[]{:S(2)}, u32[]{:S(2)}) collective-permute-start(bf16[32,1,18,512]{3,0,2,1:T(8,128)(2,1)S(1)} %get-tuple-element.10), channel_id=1, source_target_pairs={{0,224},{4,228},{8,232},{12,236},{16,240},{20,244},{24,248},{28,25... | collective-permute-start | bytes 1769480 | tf_op jit(solution)/shard_map/ppermute | solution.py:12
  27.1 1.5 slice_bitcast_fusion.17
  40.4 5.7 %collective-permute-done.2 = bf16[32,1,18,512]{3,0,2,1:T(8,128)(2,1)S(1)} collective-permute-done((bf16[32,1,18,512]{3,0,2,1:T(8,128)(2,1)S(1)}, bf16[32,1,18,512]{3,0,2,1:T(8,128)(2,1)S(1)}, u32[]{:S(2)}, u32[]{:S(2)}) %collective-permute-start.2) | collective-permute-done | bytes 589856 | tf_op jit(solution)/shard_map/ppermute | solution.py:12
  46.2 4.0 %collective-permute-done.3 = bf16[32,1,18,512]{3,0,2,1:T(8,128)(2,1)S(1)} collective-permute-done((bf16[32,1,18,512]{3,0,2,1:T(8,128)(2,1)S(1)}, bf16[32,1,18,512]{3,0,2,1:T(8,128)(2,1)S(1)}, u32[]{:S(2)}, u32[]{:S(2)}) %collective-permute-start.3) | collective-permute-done | bytes 589856 | tf_op jit(solution)/shard_map/ppermute | solution.py:12
  50.7 1.6 fusion.129
  52.3 2.9 %fusion.6 = bf16[96,4,18,512]{3,0,2,1:T(8,128)(2,1)S(1)} fusion(bf16[32,4,18,511]{3,0,2,1:T(8,128)(2,1)S(1)} %get-tuple-element.8, bf16[32,4,18,511]{3,0,2,1:T(8,128)(2,1)S(1)} %get-tuple-element.7, bf16[32,1,18,512]{3,0,2,1:T(8,128)(2,1)S(1)} %broadcast_select_fusion, bf16[32,2,1,512]{3,0,2,1:T(8,128)(2,1)S(1)} %broadcast_select_fusion.4, ...), kind=kLoop, calls=%fused_computation.10 | loop fusion | flops 63700992 | bytes 14146560 | tf_op jit(solution)/shard_map/concatenate | solution.py:19
  60.2 4.0 %collective-permute-start.4 = (bf16[16,2,1,512]{3,0,2,1:T(8,128)(2,1)S(1)}, bf16[16,2,1,512]{3,0,2,1:T(8,128)(2,1)S(1)}, u32[]{:S(2)}, u32[]{:S(2)}) collective-permute-start(bf16[16,2,1,512]{3,0,2,1:T(8,128)(2,1)S(1)} %get-tuple-element.15), channel_id=1, source_target_pairs={{0,4},{4,8},{8,12},{12,16},{16,20},{20,24},{24,28},{28,32},{32,36}... | collective-permute-start | bytes 98312 | tf_op jit(solution)/shard_map/ppermute | solution.py:12
  64.1 4.5 %collective-permute-start.5 = (bf16[16,2,1,512]{3,0,2,1:T(8,128)(2,1)S(1)}, bf16[16,2,1,512]{3,0,2,1:T(8,128)(2,1)S(1)}, u32[]{:S(2)}, u32[]{:S(2)}) collective-permute-start(bf16[16,2,1,512]{3,0,2,1:T(8,128)(2,1)S(1)} %get-tuple-element.16), channel_id=1, source_target_pairs={{0,252},{4,0},{8,4},{12,8},{16,12},{20,16},{24,20},{28,24},{32,28}... | collective-permute-start | bytes 98312 | tf_op jit(solution)/shard_map/ppermute | solution.py:12
  68.6 1.0 collective-permute-done.4
  69.9 5.1 %collective-permute-start.7 = (bf16[16,1,18,512]{3,0,2,1:T(8,128)(2,1)S(1)}, bf16[16,1,18,512]{3,0,2,1:T(8,128)(2,1)S(1)}, u32[]{:S(2)}, u32[]{:S(2)}) collective-permute-start(bf16[16,1,18,512]{3,0,2,1:T(8,128)(2,1)S(1)} %get-tuple-element.14), channel_id=1, source_target_pairs={{0,224},{4,228},{8,232},{12,236},{16,240},{20,244},{24,248},{28,25... | collective-permute-start | bytes 884744 | tf_op jit(solution)/shard_map/ppermute | solution.py:12
  75.0 4.2 %collective-permute-done.6 = bf16[16,1,18,512]{3,0,2,1:T(8,128)(2,1)S(1)} collective-permute-done((bf16[16,1,18,512]{3,0,2,1:T(8,128)(2,1)S(1)}, bf16[16,1,18,512]{3,0,2,1:T(8,128)(2,1)S(1)}, u32[]{:S(2)}, u32[]{:S(2)}) %collective-permute-start.6) | collective-permute-done | bytes 294944 | tf_op jit(solution)/shard_map/ppermute | solution.py:12
  79.2 5.5 %collective-permute-done.7 = bf16[16,1,18,512]{3,0,2,1:T(8,128)(2,1)S(1)} collective-permute-done((bf16[16,1,18,512]{3,0,2,1:T(8,128)(2,1)S(1)}, bf16[16,1,18,512]{3,0,2,1:T(8,128)(2,1)S(1)}, u32[]{:S(2)}, u32[]{:S(2)}) %collective-permute-start.7) | collective-permute-done | bytes 294944 | tf_op jit(solution)/shard_map/ppermute | solution.py:12
  84.8 1.2 pad_maximum_fusion.2
  86.9 54.6 %all-gather.2.cloned.1.call-done = bf16[64,4,18,512]{3,0,2,1:T(8,128)(2,1)} async-done(((bf16[16,4,18,512]{3,0,2,1:T(8,128)(2,1)}), bf16[64,4,18,512]{3,0,2,1:T(8,128)(2,1)}) %all-gather.2.cloned.1.call-update) | async-done | bytes 4718608 | tf_op jit(solution)/shard_map/all_gather | solution.py:96
  141.6 9.0 %fusion.128 = (bf16[64,4,18,511]{3,0,2,1:T(8,128)(2,1)S(1)}, bf16[64,4,18,511]{3,0,2,1:T(8,128)(2,1)}) fusion(bf16[64,4,18,512]{3,0,2,1:T(8,128)(2,1)} %all-gather.2.cloned.1.call-done), kind=kLoop, calls=%fused_computation.118 | loop fusion | bytes 18837504 | tf_op jit(solution)/shard_map/slice | solution.py:17
  150.6 6.7 %fusion.2 = bf16[192,4,18,512]{3,0,2,1:T(8,128)(2,1)S(1)} fusion(bf16[64,4,18,511]{3,0,2,1:T(8,128)(2,1)} %get-tuple-element.6, bf16[64,4,18,511]{3,0,2,1:T(8,128)(2,1)S(1)} %get-tuple-element.5, bf16[64,4,18,512]{3,0,2,1:T(8,128)(2,1)S(1)} %copy-done), kind=kLoop, calls=%fused_computation.4 | loop fusion | flops 70778880 | bytes 28293120 | tf_op jit(solution)/shard_map/concatenate | solution.py:19
  158.2 0.9 fusion.59
  162.0 0.9 fusion.71
  164.8 0.9 fusion.107
  165.7 1.1 copy.47
  (95 shorter events, 24.8 us)
Async XLA Ops:
  6.5 135.0 %all-gather.2.cloned.1.call-start = ((), (), s32[]{:S(2)}) async-start(), calls=%async_computation | async-start | bytes 5898240 | tf_op jit(solution)/shard_map/all_gather | solution.py:96
  8.4 13.3 %collective-permute-start = (bf16[32,2,1,512]{3,0,2,1:T(8,128)(2,1)S(1)}, bf16[32,2,1,512]{3,0,2,1:T(8,128)(2,1)S(1)}, u32[]{:S(2)}, u32[]{:S(2)}) collective-permute-start(bf16[32,2,1,512]{3,0,2,1:T(8,128)(2,1)S(1)} %get-tuple-element.11), channel_id=1, source_target_pairs={{0,4},{4,8},{8,12},{12,16},{16,20},{20,24},{24,28},{28,32},{32,36}... | collective-permute-start | bytes 196616 | tf_op jit(solution)/shard_map/ppermute | solution.py:12
  12.2 9.4 %collective-permute-start.1 = (bf16[32,2,1,512]{3,0,2,1:T(8,128)(2,1)S(1)}, bf16[32,2,1,512]{3,0,2,1:T(8,128)(2,1)S(1)}, u32[]{:S(2)}, u32[]{:S(2)}) collective-permute-start(bf16[32,2,1,512]{3,0,2,1:T(8,128)(2,1)S(1)} %get-tuple-element.12), channel_id=1, source_target_pairs={{0,252},{4,0},{8,4},{12,8},{16,12},{20,16},{24,20},{28,24},{32,28}... | collective-permute-start | bytes 196616 | tf_op jit(solution)/shard_map/ppermute | solution.py:12
  22.0 24.2 %collective-permute-start.2 = (bf16[32,1,18,512]{3,0,2,1:T(8,128)(2,1)S(1)}, bf16[32,1,18,512]{3,0,2,1:T(8,128)(2,1)S(1)}, u32[]{:S(2)}, u32[]{:S(2)}) collective-permute-start(bf16[32,1,18,512]{3,0,2,1:T(8,128)(2,1)S(1)} %get-tuple-element.9), channel_id=1, source_target_pairs={{0,32},{4,36},{8,40},{12,44},{16,48},{20,52},{24,56},{28,60},{32,6... | collective-permute-start | bytes 1769480 | tf_op jit(solution)/shard_map/ppermute | solution.py:12
  22.5 27.7 %collective-permute-start.3 = (bf16[32,1,18,512]{3,0,2,1:T(8,128)(2,1)S(1)}, bf16[32,1,18,512]{3,0,2,1:T(8,128)(2,1)S(1)}, u32[]{:S(2)}, u32[]{:S(2)}) collective-permute-start(bf16[32,1,18,512]{3,0,2,1:T(8,128)(2,1)S(1)} %get-tuple-element.10), channel_id=1, source_target_pairs={{0,224},{4,228},{8,232},{12,236},{16,240},{20,244},{24,248},{28,25... | collective-permute-start | bytes 1769480 | tf_op jit(solution)/shard_map/ppermute | solution.py:12
  52.3 2.9 %copy-start.2 = (bf16[16,96,1,1]{1,0,2,3:T(8,128)(2,1)S(1)}, bf16[16,96,1,1]{1,0,2,3:T(8,128)(2,1)}, u32[]{:S(2)}) copy-start(bf16[16,96,1,1]{1,0,2,3:T(8,128)(2,1)} %reshape.80) | copy-start | bytes 9220
  52.3 3.5 %copy-start.3 = (bf16[16,96,1,1]{1,0,2,3:T(8,128)(2,1)S(1)}, bf16[16,96,1,1]{1,0,2,3:T(8,128)(2,1)}, u32[]{:S(2)}) copy-start(bf16[16,96,1,1]{1,0,2,3:T(8,128)(2,1)} %reshape.79) | copy-start | bytes 9220
  55.2 1.1 copy-start.4
  55.2 1.6 copy-start.5
  55.8 1.6 copy-start.6
  56.3 1.6 copy-start.7
  56.8 1.6 copy-start.8
  57.4 1.6 copy-start.9
  57.9 1.6 copy-start.10
  59.5 26.5 %copy-start.1 = (bf16[3,3,3,16,64]{4,3,2,1,0:T(8,128)(2,1)S(1)}, bf16[3,3,3,16,64]{4,3,2,1,0:T(8,128)(2,1)}, u32[]{:S(2)}) copy-start(bf16[3,3,3,16,64]{4,3,2,1,0:T(8,128)(2,1)} %param.5) | copy-start | bytes 165892
  60.2 9.5 %collective-permute-start.4 = (bf16[16,2,1,512]{3,0,2,1:T(8,128)(2,1)S(1)}, bf16[16,2,1,512]{3,0,2,1:T(8,128)(2,1)S(1)}, u32[]{:S(2)}, u32[]{:S(2)}) collective-permute-start(bf16[16,2,1,512]{3,0,2,1:T(8,128)(2,1)S(1)} %get-tuple-element.15), channel_id=1, source_target_pairs={{0,4},{4,8},{8,12},{12,16},{16,20},{20,24},{24,28},{28,32},{32,36}... | collective-permute-start | bytes 98312 | tf_op jit(solution)/shard_map/ppermute | solution.py:12
  64.1 5.6 %collective-permute-start.5 = (bf16[16,2,1,512]{3,0,2,1:T(8,128)(2,1)S(1)}, bf16[16,2,1,512]{3,0,2,1:T(8,128)(2,1)S(1)}, u32[]{:S(2)}, u32[]{:S(2)}) collective-permute-start(bf16[16,2,1,512]{3,0,2,1:T(8,128)(2,1)S(1)} %get-tuple-element.16), channel_id=1, source_target_pairs={{0,252},{4,0},{8,4},{12,8},{16,12},{20,16},{24,20},{28,24},{32,28}... | collective-permute-start | bytes 98312 | tf_op jit(solution)/shard_map/ppermute | solution.py:12
  69.8 9.4 %collective-permute-start.6 = (bf16[16,1,18,512]{3,0,2,1:T(8,128)(2,1)S(1)}, bf16[16,1,18,512]{3,0,2,1:T(8,128)(2,1)S(1)}, u32[]{:S(2)}, u32[]{:S(2)}) collective-permute-start(bf16[16,1,18,512]{3,0,2,1:T(8,128)(2,1)S(1)} %get-tuple-element.13), channel_id=1, source_target_pairs={{0,32},{4,36},{8,40},{12,44},{16,48},{20,52},{24,56},{28,60},{32,6... | collective-permute-start | bytes 884744 | tf_op jit(solution)/shard_map/ppermute | solution.py:12
  69.9 14.8 %collective-permute-start.7 = (bf16[16,1,18,512]{3,0,2,1:T(8,128)(2,1)S(1)}, bf16[16,1,18,512]{3,0,2,1:T(8,128)(2,1)S(1)}, u32[]{:S(2)}, u32[]{:S(2)}) collective-permute-start(bf16[16,1,18,512]{3,0,2,1:T(8,128)(2,1)S(1)} %get-tuple-element.14), channel_id=1, source_target_pairs={{0,224},{4,228},{8,232},{12,236},{16,240},{20,244},{24,248},{28,25... | collective-permute-start | bytes 884744 | tf_op jit(solution)/shard_map/ppermute | solution.py:12
  141.6 9.1 %copy-start = (bf16[64,4,18,512]{3,0,2,1:T(8,128)(2,1)S(1)}, bf16[64,4,18,512]{3,0,2,1:T(8,128)(2,1)}, u32[]{:S(2)}) copy-start(bf16[64,4,18,512]{3,0,2,1:T(8,128)(2,1)} %all-gather.2.cloned.1.call-done) | copy-start | bytes 14155780
Sparse Core Ops, SparseCore 0:
  86.1 55.3 all-gather.1
where the time goes:
time: 174 us
  waiting for transfers between devices  76.8 us (44%)
  starting transfers between devices  30.5 us (18%)
  local copies, waits for them, and re-layouts  27.9 us (16%)
  between operations  13.6 us (8%)
  matrix products  13.3 us (8%)
  other arithmetic  11.6 us (7%)
    all_gather x1, waiting for transfers between devices, local(): lax.all_gather(hidden_pad, 'chan', axis=0, tiled=True)  54.6 us
    ppermute x8, starting transfers between devices, passed_along(): return lax.ppermute(value, axis, pairs)  30.4 us
    ppermute x8, waiting for transfers between devices, passed_along(): return lax.ppermute(value, axis, pairs)  22.2 us
    dot_general x18, matrix products, correlate(): jnp.einsum('ok,kdhw->odhw', matrix, window, preferred_element_type=jnp.fl...  13.3 us
    slice x2, local copies, waits for them, and re-layouts, widen(): left_shift = jnp.concatenate([zero_col, volume_tile[..., :-1]], 3)  10.6 us
    concatenate x2, other arithmetic, widen(): return jnp.concatenate([left_shift, volume_tile, right_shift], 0)  9.59 us
    transpose x20, local copies, waits for them, and re-layouts, correlate(): filters[depth_tap, height_tap].transpose(1, 0, 2).reshape(out_count, -1)  7.27 us
    reshape x18, local copies, waits for them, and re-layouts, correlate(): filters[depth_tap, height_tap].transpose(1, 0, 2).reshape(out_count, -1)  6.94 us
  transfers between devices with their start and end apart: 9, of which 7 were waited for; matrix products, arithmetic and copies ran while one was open for 8% of the time, Pallas kernels for 0%

commit v1 on v0

v1 whole, which is shorter than its diff:
```python
import jax
import jax.numpy as jnp
from jax import lax
from jax.sharding import PartitionSpec as P

GH = 8


def passed_along(value, axis, steps):
    count = lax.axis_size(axis)
    pairs = [(source, (source + steps) % count) for source in range(count)]
    return lax.ppermute(value, axis, pairs)


def tile_place():
    tile_count = lax.axis_size("space")
    position = (lax.axis_index("space") + GH + GH // 4) % tile_count
    return position % GH, position // GH, tile_count // GH


def wide_border(volume_tile, rim):
    tile_row, depth_tile, grid_depth = tile_place()
    above_rim = passed_along(volume_tile[:, :, -rim:, :], "space", 1)
    below_rim = passed_along(volume_tile[:, :, :rim, :], "space", -1)
    above_rim = jnp.where(tile_row > 0, above_rim, jnp.zeros_like(above_rim))
    below_rim = jnp.where(tile_row < GH - 1, below_rim, jnp.zeros_like(below_rim))
    taller = jnp.concatenate([above_rim, volume_tile, below_rim], 2)
    front_rim = passed_along(taller[:, -rim:], "space", GH)
    back_rim = passed_along(taller[:, :rim], "space", -GH)
    front_rim = jnp.where(depth_tile > 0, front_rim, jnp.zeros_like(front_rim))
    back_rim = jnp.where(depth_tile < grid_depth - 1, back_rim, jnp.zeros_like(back_rim))
    return jnp.concatenate([front_rim, taller, back_rim], 1)


def conv_valid(stacked, filters):
    kernel = filters.transpose(3, 4, 0, 1, 2)
    result = lax.conv_general_dilated(
        stacked[None], kernel, (1, 1, 1), ((0, 0), (0, 0), (1, 1)),
        dimension_numbers=("NCDHW", "OIDHW", "NCDHW"), preferred_element_type=jnp.float32)
    return result[0]


def inside_mask(depth_rows, height_rows):
    tile_row, depth_tile, grid_depth = tile_place()
    d = lax.broadcasted_iota(jnp.int32, (depth_rows, height_rows, 1), 0)
    h = lax.broadcasted_iota(jnp.int32, (depth_rows, height_rows, 1), 1)
    keep = (d > 0) | (depth_tile > 0)
    keep &= (d < depth_rows - 1) | (depth_tile < grid_depth - 1)
    keep &= (h > 0) | (tile_row > 0)
    keep &= (h < height_rows - 1) | (tile_row < GH - 1)
    return keep


def local(voxels, first_filters, second_filters):
    all_first = lax.all_gather(first_filters, "chan", axis=3, tiled=True)
    padded = wide_border(voxels, 2)
    hidden = jax.nn.relu(conv_valid(padded, all_first))
    keep = inside_mask(hidden.shape[1], hidden.shape[2])
    hidden = jnp.where(keep[None], hidden, 0.0).astype(jnp.bfloat16)
    summed = conv_valid(hidden, second_filters)
    return jax.nn.relu(summed).astype(jnp.bfloat16)


def solution(mesh):
    return jax.shard_map(
        local,
        mesh=mesh,
        in_specs=(
            P(None, "space", None, None),
            P(None, None, None, "chan", None),
            P(None, None, None, "chan", None),
        ),
        out_specs=P("chan", "space", None, None),
        check_vma=False,
    )
```

time: 174 us -> 202 us (1.16); the launches traced: 174 us -> 198 us
  matrix products: 13.3 us -> 73.2 us
  waiting for transfers between devices: 76.8 us -> 48.3 us
  local copies, waits for them, and re-layouts: 27.9 us -> 47.6 us
  starting transfers between devices: 30.5 us -> 15.9 us
  between operations: 13.6 us -> 0.13 us
  blocking collectives: 0 us -> 9.16 us
  other arithmetic: 11.6 us -> 4.07 us
    conv_general_dilated x0 -> x2, matrix products: none -> 73.2 us  [conv_valid(): lax.conv_general_dilated(stacked[None], kernel, (1, 1, 1), ((0, 0), (0, 0...]
    all_gather x1 -> x0, waiting for transfers between devices: 54.6 us -> none  [local(): lax.all_gather(hidden_pad, 'chan', axis=0, tiled=True)]
    conv_general_dilated x0 -> x4, local copies, waits for them, and re-layouts: none -> 38.4 us  [conv_valid(): lax.conv_general_dilated(stacked[None], kernel, (1, 1, 1), ((0, 0), (0, 0...]
    ppermute x8 -> x4, waiting for transfers between devices: 22.2 us -> 48.3 us  [passed_along(): return lax.ppermute(value, axis, pairs)]
    ppermute x8 -> x4, starting transfers between devices: 30.4 us -> 15.9 us  [passed_along(): return lax.ppermute(value, axis, pairs)]
    dot_general x18 -> x0, matrix products: 13.3 us -> none  [correlate(): jnp.einsum('ok,kdhw->odhw', matrix, window, preferred_element_type=jnp.fl...]
    concatenate x6 -> x1, other arithmetic: 11.4 us -> 0.16 us  [wide_border(): taller = jnp.concatenate([above_rim, volume_tile, below_rim], 2)]
    slice x6 -> x1, local copies, waits for them, and re-layouts: 10.8 us -> 0.02 us  [wide_border(): above_rim = passed_along(volume_tile[:, :, -rim:, :], 'space', 1)]
  transfers between devices with their start and end apart: 9 -> 4, of which waited for: 7 -> 3; matrix products, arithmetic and copies ran while one was open for 8% -> 1% of each run, Pallas kernels for 0% -> 0%
where the time goes in v1:
time: 202 us; the launch traced here: 198 us
  matrix products  73.2 us (36%)
  waiting for transfers between devices  48.3 us (24%)
  local copies, waits for them, and re-layouts  47.6 us (24%)
  starting transfers between devices  15.9 us (8%)
  blocking collectives  9.16 us (5%)
  other arithmetic  4.07 us (2%)
    conv_general_dilated x2, matrix products, conv_valid(): lax.conv_general_dilated(stacked[None], kernel, (1, 1, 1), ((0, 0), (0, 0...  73.2 us
    ppermute x4, waiting for transfers between devices, passed_along(): return lax.ppermute(value, axis, pairs)  48.3 us
    conv_general_dilated x4, local copies, waits for them, and re-layouts, conv_valid(): lax.conv_general_dilated(stacked[None], kernel, (1, 1, 1), ((0, 0), (0, 0...  38.4 us
    ppermute x4, starting transfers between devices, passed_along(): return lax.ppermute(value, axis, pairs)  15.9 us
    all_gather x1, blocking collectives, local(): all_first = lax.all_gather(first_filters, 'chan', axis=3, tiled=True)  9.16 us
    broadcast_in_dim x1, local copies, waits for them, and re-layouts, conv_valid(): stacked[None]  4.97 us
  transfers between devices with their start and end apart: 4, of which 3 were waited for; matrix products, arithmetic and copies ran while one was open for 1% of the time, Pallas kernels for 0%

profile of v1, /device:TPU:1, one launch (start us, length us, event | category | flops | bytes accessed | tf_op | source)
XLA Modules:
  0.0 198.3 jit_solution(11501891564249158995)
XLA Ops:
  0.0 1.8 copy.24
  1.9 3.9 %collective-permute-start = (bf16[32,2,2,512]{3,0,2,1:T(8,128)(2,1)S(1)}, bf16[32,2,2,512]{3,0,2,1:T(8,128)(2,1)S(1)}, u32[]{:S(2)}, u32[]{:S(2)}) collective-permute-start(bf16[32,2,2,512]{3,0,2,1:T(8,128)(2,1)S(1)} %get-tuple-element.7), channel_id=1, source_target_pairs={{0,4},{4,8},{8,12},{12,16},{16,20},{20,24},{24,28},{28,32},{32,36}... | collective-permute-start | bytes 393224 | tf_op jit(solution)/shard_map/ppermute | solution.py:12
  5.8 7.8 %collective-permute-start.1 = (bf16[32,2,2,512]{3,0,2,1:T(8,128)(2,1)S(1)}, bf16[32,2,2,512]{3,0,2,1:T(8,128)(2,1)S(1)}, u32[]{:S(2)}, u32[]{:S(2)}) collective-permute-start(bf16[32,2,2,512]{3,0,2,1:T(8,128)(2,1)S(1)} %get-tuple-element.8), channel_id=1, source_target_pairs={{0,252},{4,0},{8,4},{12,8},{16,12},{20,16},{24,20},{28,24},{32,28}... | collective-permute-start | bytes 393224 | tf_op jit(solution)/shard_map/ppermute | solution.py:12
  13.5 3.7 %collective-permute-done = bf16[32,2,2,512]{3,0,2,1:T(8,128)(2,1)S(1)} collective-permute-done((bf16[32,2,2,512]{3,0,2,1:T(8,128)(2,1)S(1)}, bf16[32,2,2,512]{3,0,2,1:T(8,128)(2,1)S(1)}, u32[]{:S(2)}, u32[]{:S(2)}) %collective-permute-start) | collective-permute-done | bytes 131104 | tf_op jit(solution)/shard_map/ppermute | solution.py:12
  17.3 0.2 pad_maximum_fusion
  17.4 4.2 %collective-permute-start.3 = (bf16[32,2,20,512]{3,0,2,1:T(8,128)(2,1)S(1)}, bf16[32,2,20,512]{3,0,2,1:T(8,128)(2,1)}, u32[]{:S(2)}, u32[]{:S(2)}) collective-permute-start(bf16[32,2,20,512]{3,0,2,1:T(8,128)(2,1)S(1)} %pad_maximum_fusion), channel_id=1, source_target_pairs={{0,224},{4,228},{8,232},{12,236},{16,240},{20,244},{24,248},{28,25... | collective-permute-start | bytes 3932168 | tf_op jit(solution)/shard_map/ppermute | solution.py:12
  21.6 9.2 %all_gather.3 = bf16[3,3,3,64,32]{4,3,2,1,0:T(8,128)(2,1)S(1)} all-gather(bf16[3,3,3,16,32]{4,3,2,1,0:T(8,128)(2,1)} %param.4), channel_id=1, replica_groups=mesh['space'=64,'chan'=4] {'chan'}, dimensions={3}, use_global_device_ids=true | all-gather | bytes 138240 | tf_op jit(solution)/shard_map/all_gather | solution.py:55
  30.8 0.1 and_and_fusion
  30.9 43.8 %collective-permute-done.3 = bf16[32,2,20,512]{3,0,2,1:T(8,128)(2,1)} collective-permute-done((bf16[32,2,20,512]{3,0,2,1:T(8,128)(2,1)S(1)}, bf16[32,2,20,512]{3,0,2,1:T(8,128)(2,1)}, u32[]{:S(2)}, u32[]{:S(2)}) %collective-permute-start.3) | collective-permute-done | bytes 1310752 | tf_op jit(solution)/shard_map/ppermute | solution.py:12
  74.7 1.4 broadcast_select_fusion
  76.1 0.8 collective-permute-done.2
  76.9 1.4 broadcast_select_fusion.1
  78.3 0.7 maximum_bitcast_fusion
  79.1 5.0 %pad = bf16[32,6,20,1,520]{4,0,2,1,3:T(8,128)(2,1)} pad(bf16[32,6,20,1,512]{4,0,2,1,3:T(8,128)(2,1)S(1)} %maximum_bitcast_fusion, bf16[]{:T(256)} %constant.64.clone.1), padding=0_0x0_0x0_0x0_0x1_7 | pad | bytes 7925762 | tf_op jit(solution)/shard_map/broadcast_in_dim | solution.py:38
  84.0 12.9 %reshape.61 = bf16[32,6,20,1,8,65]{5,4,0,2,1,3:T(8,128)(2,1)} reshape(bf16[32,6,20,1,520]{4,0,2,1,3:T(8,128)(2,1)} %pad) | data formatting | bytes 7987200 | tf_op jit(solution)/shard_map/conv_general_dilated | solution.py:37
  96.9 20.2 %copy.28 = bf16[32,6,20,1,8,65]{0,4,5,2,1,3:T(8,128)(2,1)} copy(bf16[32,6,20,1,8,65]{5,4,0,2,1,3:T(8,128)(2,1)} %reshape.61) | data formatting | bytes 7987200 | tf_op jit(solution)/shard_map/conv_general_dilated | solution.py:37
  117.1 1.2 slice.14
  118.3 41.5 %fusion.22 = bf16[4,18,1,8,65,64]{5,3,4,1,0,2:T(8,128)(2,1)S(1)} fusion(pred[8,65]{0,1:T(8,128)(4,1)S(1)} %copy-done.1, pred[4,18]{1,0:T(4,128)(4,1)S(1)} %and_and_fusion, bf16[3,3,3,64,32]{4,3,2,1,0:T(8,128)(2,1)S(1)} %all_gather.3, bf16[32,6,20,1,7,2]{0,4,5,2,1,3:T(8,128)(2,1)S(1)} %slice.14, bf16[32,6,20,1,8,65]{0,4,5,2,1,3:T(8,128)(2,1)} %copy.28), kind=kOutput, calls=%fused_computation.23 | convolution fusion | flops 4164894720 | bytes 9004624 | tf_op jit(solution)/shard_map/conv_general_dilated | solution.py:37
  159.9 31.7 %fusion.12 = bf16[2,16,8,65,16]{4,2,3,1,0:T(8,128)(2,1)} fusion(bf16[3,3,3,16,64]{4,3,2,1,0:T(8,128)(2,1)S(1)} %copy-done, bf16[4,18,1,7,1,64]{5,3,4,1,0,2:T(8,128)(2,1)S(1)} %get-tuple-element.6, bf16[4,18,1,7,1,64]{5,3,4,1,0,2:T(8,128)(2,1)S(1)} %get-tuple-element.5, bf16[4,18,1,8,65,64]{5,3,4,1,0,2:T(8,128)(2,1)S(1)} %fusion.22), kind=kOutput, calls=%fused_computation.15 | convolution fusion | flops 944824320 | bytes 5509120 | tf_op jit(solution)/shard_map/conv_general_dilated | solution.py:37
  191.5 4.2 %copy.29 = bf16[2,16,8,65,16]{3,4,2,1,0:T(8,128)(2,1)S(1)} copy(bf16[2,16,8,65,16]{4,2,3,1,0:T(8,128)(2,1)} %fusion.12) | data formatting | bytes 1064960 | tf_op jit(solution)/shard_map/conv_general_dilated | solution.py:37
  195.7 0.3 maximum_convert_fusion
  196.0 0.3 copy.30
  196.3 0.8 reshape.68
  197.2 1.1 copy.31
  (13 shorter events, 0.2 us)
Async XLA Ops:
  0.0 159.8 %copy-start = (bf16[3,3,3,16,64]{4,3,2,1,0:T(8,128)(2,1)S(1)}, bf16[3,3,3,16,64]{4,3,2,1,0:T(8,128)(2,1)}, u32[]{:S(2)}) copy-start(bf16[3,3,3,16,64]{4,3,2,1,0:T(8,128)(2,1)} %param.5) | copy-start | bytes 165892
  1.9 15.3 %collective-permute-start = (bf16[32,2,2,512]{3,0,2,1:T(8,128)(2,1)S(1)}, bf16[32,2,2,512]{3,0,2,1:T(8,128)(2,1)S(1)}, u32[]{:S(2)}, u32[]{:S(2)}) collective-permute-start(bf16[32,2,2,512]{3,0,2,1:T(8,128)(2,1)S(1)} %get-tuple-element.7), channel_id=1, source_target_pairs={{0,4},{4,8},{8,12},{12,16},{16,20},{20,24},{24,28},{28,32},{32,36}... | collective-permute-start | bytes 393224 | tf_op jit(solution)/shard_map/ppermute | solution.py:12
  5.8 11.5 %collective-permute-start.1 = (bf16[32,2,2,512]{3,0,2,1:T(8,128)(2,1)S(1)}, bf16[32,2,2,512]{3,0,2,1:T(8,128)(2,1)S(1)}, u32[]{:S(2)}, u32[]{:S(2)}) collective-permute-start(bf16[32,2,2,512]{3,0,2,1:T(8,128)(2,1)S(1)} %get-tuple-element.8), channel_id=1, source_target_pairs={{0,252},{4,0},{8,4},{12,8},{16,12},{20,16},{24,20},{28,24},{32,28}... | collective-permute-start | bytes 393224 | tf_op jit(solution)/shard_map/ppermute | solution.py:12
  17.4 57.3 %collective-permute-start.3 = (bf16[32,2,20,512]{3,0,2,1:T(8,128)(2,1)S(1)}, bf16[32,2,20,512]{3,0,2,1:T(8,128)(2,1)}, u32[]{:S(2)}, u32[]{:S(2)}) collective-permute-start(bf16[32,2,20,512]{3,0,2,1:T(8,128)(2,1)S(1)} %pad_maximum_fusion), channel_id=1, source_target_pairs={{0,224},{4,228},{8,232},{12,236},{16,240},{20,244},{24,248},{28,25... | collective-permute-start | bytes 3932168 | tf_op jit(solution)/shard_map/ppermute | solution.py:12
  21.6 55.3 %collective-permute-start.2 = (bf16[32,2,20,512]{3,0,2,1:T(8,128)(2,1)S(1)}, bf16[32,2,20,512]{3,0,2,1:T(8,128)(2,1)}, u32[]{:S(2)}, u32[]{:S(2)}) collective-permute-start(bf16[32,2,20,512]{3,0,2,1:T(8,128)(2,1)S(1)} %pad_maximum_fusion), channel_id=1, source_target_pairs={{0,32},{4,36},{8,40},{12,44},{16,48},{20,52},{24,56},{28,60},{32,6... | collective-permute-start | bytes 3932168 | tf_op jit(solution)/shard_map/ppermute | solution.py:12
  96.9 21.4 %copy-start.1 = (pred[8,65]{0,1:T(8,128)(4,1)S(1)}, pred[8,65]{0,1:T(8,128)(4,1)}, u32[]{:S(2)}) copy-start(pred[8,65]{0,1:T(8,128)(4,1)} %constant.74) | copy-start | bytes 1564

commit v2 on v1

v2 whole, which is shorter than its diff:
```python
import functools

import jax
import jax.numpy as jnp
from jax import lax
from jax.experimental import pallas as pl
from jax.experimental.pallas import tpu as pltpu
from jax.sharding import PartitionSpec as P

GH = 8


def passed_along(value, axis, steps):
    count = lax.axis_size(axis)
    pairs = [(source, (source + steps) % count) for source in range(count)]
    return lax.ppermute(value, axis, pairs)


def tile_place():
    tile_count = lax.axis_size("space")
    position = (lax.axis_index("space") + GH + GH // 4) % tile_count
    return position % GH, position // GH, tile_count // GH


def wide_border(volume_tile, rim):
    tile_row, depth_tile, grid_depth = tile_place()
    above_rim = passed_along(volume_tile[:, -rim:], "space", 1)
    below_rim = passed_along(volume_tile[:, :rim], "space", -1)
    above_rim = jnp.where(tile_row > 0, above_rim, jnp.zeros_like(above_rim))
    below_rim = jnp.where(tile_row < GH - 1, below_rim, jnp.zeros_like(below_rim))
    taller = jnp.concatenate([above_rim, volume_tile, below_rim], 1)
    front_rim = passed_along(taller[-rim:], "space", GH)
    back_rim = passed_along(taller[:rim], "space", -GH)
    front_rim = jnp.where(depth_tile > 0, front_rim, jnp.zeros_like(front_rim))
    back_rim = jnp.where(depth_tile < grid_depth - 1, back_rim, jnp.zeros_like(back_rim))
    return jnp.concatenate([front_rim, taller, back_rim], 0)


def width_taps(acc, out_count):
    width = acc.shape[1]
    col = lax.broadcasted_iota(jnp.int32, (out_count, width), 1)
    left = pltpu.roll(acc[:out_count], 1, 1)
    right = pltpu.roll(acc[2 * out_count :], width - 1, 1)
    left = jnp.where(col > 0, left, 0.0)
    right = jnp.where(col < width - 1, right, 0.0)
    return left + acc[out_count : 2 * out_count] + right


def conv_rows(src_ref, w_ref, d, h, out_count):
    windows = []
    for a in range(3):
        window = src_ref[d + a, pl.ds(h, 3)]
        windows.append(window.reshape(-1, window.shape[-1]))
    acc = jnp.dot(w_ref[...], jnp.concatenate(windows, 0), preferred_element_type=jnp.float32)
    return width_taps(acc, out_count)


def two_layers_kernel(keep_ref, x_ref, w1_ref, w2_ref, o_ref, hid_ref):
    mid_count = w1_ref.shape[0] // 3
    out_count = w2_ref.shape[0] // 3
    hid_depth, hid_height = hid_ref.shape[0], hid_ref.shape[1]
    out_depth, out_height = o_ref.shape[0], o_ref.shape[1]

    for d in range(hid_depth):
        def first(h, carry, d=d):
            y = jnp.maximum(conv_rows(x_ref, w1_ref, d, h, mid_count), 0.0)
            y = jnp.where(keep_ref[d * hid_height + h] > 0, y, 0.0)
            hid_ref[d, h] = y.astype(hid_ref.dtype)
            return carry

        lax.fori_loop(0, hid_height, first, 0)

    for d in range(out_depth):
        def second(h, carry, d=d):
            y = jnp.maximum(conv_rows(hid_ref, w2_ref, d, h, out_count), 0.0)
            o_ref[d, h] = y.astype(o_ref.dtype)
            return carry

        lax.fori_loop(0, out_height, second, 0)


def two_layers(keep, padded, w1, w2):
    in_depth, in_height, _, width = padded.shape
    mid_count = w1.shape[0] // 3
    out_count = w2.shape[0] // 3
    vmem = pltpu.MemorySpace.VMEM
    return pl.pallas_call(
        two_layers_kernel,
        out_shape=jax.ShapeDtypeStruct((in_depth - 4, in_height - 4, out_count, width), jnp.bfloat16),
        in_specs=[
            pl.BlockSpec(memory_space=pltpu.SMEM),
            pl.BlockSpec(memory_space=vmem),
            pl.BlockSpec(memory_space=vmem),
            pl.BlockSpec(memory_space=vmem),
        ],
        out_specs=pl.BlockSpec(memory_space=vmem),
        scratch_shapes=[pltpu.VMEM((in_depth - 2, in_height - 2, mid_count, width), jnp.bfloat16)],
    )(keep, padded, w1, w2)


def tap_matrices(filters):
    a, b, e, o, c = filters.shape
    return filters.transpose(2, 3, 0, 1, 4).reshape(e * o, a * b * c)


def inside_flags(depth_rows, height_rows):
    tile_row, depth_tile, grid_depth = tile_place()
    d = lax.broadcasted_iota(jnp.int32, (depth_rows, height_rows), 0)
    h = lax.broadcasted_iota(jnp.int32, (depth_rows, height_rows), 1)
    keep = (d > 0) | (depth_tile > 0)
    keep &= (d < depth_rows - 1) | (depth_tile < grid_depth - 1)
    keep &= (h > 0) | (tile_row > 0)
    keep &= (h < height_rows - 1) | (tile_row < GH - 1)
    return keep.astype(jnp.int32).reshape(-1)


def local(voxels, first_filters, second_filters):
    all_first = lax.all_gather(first_filters, "chan", axis=3, tiled=True)
    tile = voxels.transpose(1, 2, 0, 3)
    padded = wide_border(tile, 2)
    keep = inside_flags(padded.shape[0] - 2, padded.shape[1] - 2)
    out = two_layers(keep, padded, tap_matrices(all_first), tap_matrices(second_filters))
    return out.transpose(2, 0, 1, 3)


def solution(mesh):
    return jax.shard_map(
        local,
        mesh=mesh,
        in_specs=(
            P(None, "space", None, None),
            P(None, None, None, "chan", None),
            P(None, None, None, "chan", None),
        ),
        out_specs=P("chan", "space", None, None),
        check_vma=False,
    )
```

time: 202 us -> 131 us (0.65)
  matrix products: 73.2 us -> 0 us
  local copies, waits for them, and re-layouts: 47.6 us -> 6.72 us
  Pallas kernels: 0 us -> 37.9 us
  waiting for transfers between devices: 48.3 us -> 54.7 us
    conv_general_dilated x2 -> x0, matrix products: 73.2 us -> none  [conv_valid(): lax.conv_general_dilated(stacked[None], kernel, (1, 1, 1), ((0, 0), (0, 0...]
    conv_general_dilated x4 -> x0, local copies, waits for them, and re-layouts: 38.4 us -> none  [conv_valid(): lax.conv_general_dilated(stacked[None], kernel, (1, 1, 1), ((0, 0), (0, 0...]
    pallas_call x0 -> x1, Pallas kernels: none -> 37.9 us  [two_layers(): pl.pallas_call(two_layers_kernel, out_shape=jax.ShapeDtypeStruct((in_dept...]
    ppermute x4, waiting for transfers between devices: 48.3 us -> 54.7 us  [passed_along(): return lax.ppermute(value, axis, pairs)]
    broadcast_in_dim x1 -> x0, local copies, waits for them, and re-layouts: 4.97 us -> none  [conv_valid(): stacked[None]]
    transpose x0 -> x3, local copies, waits for them, and re-layouts: none -> 2.46 us  [the longest x1 2.13 us: local(): return out.transpose(2, 0, 1, 3)]
    concatenate x1 -> x2, other arithmetic: 0.16 us -> 2.33 us  [the longest x1 2.17 us: wide_border(): return jnp.concatenate([front_rim, taller, back_rim], 0)]
  transfers between devices with their start and end apart: 4 -> 4, of which waited for: 3 -> 3; matrix products, arithmetic and copies ran while one was open for 1% -> 3% of each run, Pallas kernels for 0% -> 0%
where the time goes in v2:
time: 131 us; the launch traced here: 129 us
  waiting for transfers between devices  54.7 us (42%)
  Pallas kernels  37.9 us (29%)
  starting transfers between devices  14.6 us (11%)
  blocking collectives  9.94 us (8%)
  local copies, waits for them, and re-layouts  6.72 us (5%)
  other arithmetic  5.27 us (4%)
    ppermute x4, waiting for transfers between devices, passed_along(): return lax.ppermute(value, axis, pairs)  54.7 us
    pallas_call x1, Pallas kernels, two_layers(): pl.pallas_call(two_layers_kernel, out_shape=jax.ShapeDtypeStruct((in_dept...  37.9 us
    ppermute x4, starting transfers between devices, passed_along(): return lax.ppermute(value, axis, pairs)  14.6 us
    all_gather x1, blocking collectives, local(): all_first = lax.all_gather(first_filters, 'chan', axis=3, tiled=True)  9.94 us
  transfers between devices with their start and end apart: 4, of which 3 were waited for; matrix products, arithmetic and copies ran while one was open for 3% of the time, Pallas kernels for 0%

profile of v2, /device:TPU:1, one launch (start us, length us, event | category | flops | bytes accessed | tf_op | source)
XLA Modules:
  0.0 129.2 jit_solution(13024349037711589844)
XLA Ops:
  0.0 1.8 %copy.14 = bf16[32,2,16,512]{3,0,2,1:T(8,128)(2,1)S(1)} copy(bf16[32,2,16,512]{3,2,1,0:T(8,128)(2,1)} %param.3) | data formatting | bytes 2097152 | tf_op args[0]
  1.8 11.6 %collective-permute-start.1 = (bf16[2,2,32,512]{3,2,1,0:T(8,128)(2,1)S(1)}, bf16[2,2,32,512]{3,2,1,0:T(8,128)(2,1)S(1)}, u32[]{:S(2)}, u32[]{:S(2)}) collective-permute-start(bf16[2,2,32,512]{3,2,1,0:T(8,128)(2,1)S(1)} %get-tuple-element.6), channel_id=1, source_target_pairs={{0,252},{4,0},{8,4},{12,8},{16,12},{20,16},{24,20},{28,24},{32,28}... | collective-permute-start | bytes 393224 | tf_op jit(solution)/shard_map/ppermute | solution.py:16
  13.4 0.0 collective-permute-start
  13.4 5.6 %collective-permute-done.1 = bf16[2,2,32,512]{3,2,1,0:T(8,128)(2,1)S(1)} collective-permute-done((bf16[2,2,32,512]{3,2,1,0:T(8,128)(2,1)S(1)}, bf16[2,2,32,512]{3,2,1,0:T(8,128)(2,1)S(1)}, u32[]{:S(2)}, u32[]{:S(2)}) %collective-permute-start.1) | collective-permute-done | bytes 131104 | tf_op jit(solution)/shard_map/ppermute | solution.py:16
  19.0 6.2 %collective-permute-done = bf16[2,2,32,512]{3,2,1,0:T(8,128)(2,1)S(1)} collective-permute-done((bf16[2,2,32,512]{3,2,1,0:T(8,128)(2,1)S(1)}, bf16[2,2,32,512]{3,2,1,0:T(8,128)(2,1)S(1)}, u32[]{:S(2)}, u32[]{:S(2)}) %collective-permute-start) | collective-permute-done | bytes 131104 | tf_op jit(solution)/shard_map/ppermute | solution.py:16
  25.2 0.0 copy-start.1
  25.2 0.2 pad_maximum_fusion.1
  25.3 0.0 copy-start
  25.3 0.1 collective-permute-start.3
  25.4 3.0 %collective-permute-start.2 = (bf16[2,20,32,512]{3,2,1,0:T(8,128)(2,1)S(1)}, bf16[2,20,32,512]{3,2,1,0:T(8,128)(2,1)}, u32[]{:S(2)}, u32[]{:S(2)}) collective-permute-start(bf16[2,20,32,512]{3,2,1,0:T(8,128)(2,1)S(1)} %pad_maximum_fusion.1), channel_id=1, source_target_pairs={{0,32},{4,36},{8,40},{12,44},{16,48},{20,52},{24,56},{28,60},{32,6... | collective-permute-start | bytes 3932168 | tf_op jit(solution)/shard_map/ppermute | solution.py:16
  28.4 0.1 and_convert_fusion
  28.5 0.7 reshape.20.keep_ref
  29.2 9.9 %all_gather.3 = bf16[3,3,3,64,32]{4,3,2,1,0:T(8,128)(2,1)S(1)} all-gather(bf16[3,3,3,16,32]{4,3,2,1,0:T(8,128)(2,1)S(1)} %copy-done.1), channel_id=1, replica_groups=mesh['space'=64,'chan'=4] {'chan'}, dimensions={3}, use_global_device_ids=true | all-gather | bytes 138240 | tf_op jit(solution)/shard_map/all_gather | solution.py:118
  39.1 0.3 copy.9
  39.4 0.2 reshape.18
  39.6 0.8 copy.11.w1_ref
  40.4 0.1 copy.10
  40.4 0.8 reshape.19.w2_ref
  41.2 43.0 %collective-permute-done.3 = bf16[2,20,32,512]{3,2,1,0:T(8,128)(2,1)} collective-permute-done((bf16[2,20,32,512]{3,2,1,0:T(8,128)(2,1)S(1)}, bf16[2,20,32,512]{3,2,1,0:T(8,128)(2,1)}, u32[]{:S(2)}, u32[]{:S(2)}) %collective-permute-start.3) | collective-permute-done | bytes 1310752 | tf_op jit(solution)/shard_map/ppermute | solution.py:16
  84.2 1.4 %broadcast_select_fusion = bf16[2,20,32,512]{3,2,1,0:T(8,128)(2,1)S(1)} fusion(bf16[2,20,32,512]{3,2,1,0:T(8,128)(2,1)} %collective-permute-done.3, pred[]{:T(512)S(6)} %lt.39), kind=kLoop, calls=%fused_computation.2 | loop fusion | flops 655360 | bytes 2621441 | tf_op jit(solution)/shard_map/jit(_where)/select_n | solution.py:35
  85.6 1.4 %broadcast_select_fusion.1 = bf16[2,20,32,512]{3,2,1,0:T(8,128)(2,1)S(1)} fusion(bf16[2,20,32,512]{3,2,1,0:T(8,128)(2,1)} %collective-permute-done.2, pred[]{:T(512)S(6)} %gt.17), kind=kLoop, calls=%fused_computation.3 | loop fusion | flops 655360 | bytes 2621441 | tf_op jit(solution)/shard_map/jit(_where)/select_n | solution.py:34
  87.1 2.2 %pad_maximum_fusion.x_ref = bf16[6,20,32,512]{3,2,1,0:T(8,128)(2,1)} fusion(bf16[2,20,32,512]{3,2,1,0:T(8,128)(2,1)S(1)} %broadcast_select_fusion, bf16[2,2,32,512]{3,2,1,0:T(8,128)(2,1)S(1)} %broadcast_select_fusion.2, bf16[2,16,32,512]{3,2,1,0:T(8,128)(2,1)S(1)} %bitcast.10, bf16[2,2,32,512]{3,2,1,0:T(8,128)(2,1)S(1)} %broadcast_select_fusion.3, ...), kind=kLoop, calls=%fused_computation | loop fusion | flops 7864320 | bytes 7864320 | tf_op jit(solution)/shard_map/concatenate | solution.py:36
  89.2 37.9 %shard_map.37 = bf16[2,16,16,512]{3,2,1,0:T(8,128)(2,1)} custom-call(s32[72]{0:T(128)} %reshape.20.keep_ref, bf16[6,20,32,512]{3,2,1,0:T(8,128)(2,1)} %pad_maximum_fusion.x_ref, bf16[192,288]{1,0:T(8,128)(2,1)} %copy.11.w1_ref, bf16[48,576]{1,0:T(8,128)(2,1)} %reshape.19.w2_ref), custom_call_target="tpu_custom_call" | custom-call | tf_op jit(solution)/shard_map/pallas_call | solution.py:87
  127.1 2.1 %copy.12 = bf16[16,2,16,512]{3,2,1,0:T(8,128)(2,1)} copy(bf16[16,2,16,512]{3,0,2,1:T(8,128)(2,1)} %bitcast.11) | data formatting | bytes 1048576 | tf_op jit(solution)/shard_map/transpose | solution.py:123
  (8 shorter events, 0.1 us)
Async XLA Ops:
  1.8 17.1 %collective-permute-start.1 = (bf16[2,2,32,512]{3,2,1,0:T(8,128)(2,1)S(1)}, bf16[2,2,32,512]{3,2,1,0:T(8,128)(2,1)S(1)}, u32[]{:S(2)}, u32[]{:S(2)}) collective-permute-start(bf16[2,2,32,512]{3,2,1,0:T(8,128)(2,1)S(1)} %get-tuple-element.6), channel_id=1, source_target_pairs={{0,252},{4,0},{8,4},{12,8},{16,12},{20,16},{24,20},{28,24},{32,28}... | collective-permute-start | bytes 393224 | tf_op jit(solution)/shard_map/ppermute | solution.py:16
  13.4 11.7 %collective-permute-start = (bf16[2,2,32,512]{3,2,1,0:T(8,128)(2,1)S(1)}, bf16[2,2,32,512]{3,2,1,0:T(8,128)(2,1)S(1)}, u32[]{:S(2)}, u32[]{:S(2)}) collective-permute-start(bf16[2,2,32,512]{3,2,1,0:T(8,128)(2,1)S(1)} %get-tuple-element.5), channel_id=1, source_target_pairs={{0,4},{4,8},{8,12},{12,16},{16,20},{20,24},{24,28},{28,32},{32,36}... | collective-permute-start | bytes 393224 | tf_op jit(solution)/shard_map/ppermute | solution.py:16
  25.2 4.0 %copy-start.1 = (bf16[3,3,3,16,32]{4,3,2,1,0:T(8,128)(2,1)S(1)}, bf16[3,3,3,16,32]{4,3,2,1,0:T(8,128)(2,1)}, u32[]{:S(2)}) copy-start(bf16[3,3,3,16,32]{4,3,2,1,0:T(8,128)(2,1)} %param.4) | copy-start | bytes 82948
  25.3 15.0 %copy-start = (bf16[3,3,3,16,64]{4,3,2,1,0:T(8,128)(2,1)S(1)}, bf16[3,3,3,16,64]{4,3,2,1,0:T(8,128)(2,1)}, u32[]{:S(2)}) copy-start(bf16[3,3,3,16,64]{4,3,2,1,0:T(8,128)(2,1)} %param.5) | copy-start | bytes 165892
  25.3 58.9 %collective-permute-start.3 = (bf16[2,20,32,512]{3,2,1,0:T(8,128)(2,1)S(1)}, bf16[2,20,32,512]{3,2,1,0:T(8,128)(2,1)}, u32[]{:S(2)}, u32[]{:S(2)}) collective-permute-start(bf16[2,20,32,512]{3,2,1,0:T(8,128)(2,1)S(1)} %pad_maximum_fusion.1), channel_id=1, source_target_pairs={{0,224},{4,228},{8,232},{12,236},{16,240},{20,244},{24,248},{28,25... | collective-permute-start | bytes 3932168 | tf_op jit(solution)/shard_map/ppermute | solution.py:16
  25.4 60.2 %collective-permute-start.2 = (bf16[2,20,32,512]{3,2,1,0:T(8,128)(2,1)S(1)}, bf16[2,20,32,512]{3,2,1,0:T(8,128)(2,1)}, u32[]{:S(2)}, u32[]{:S(2)}) collective-permute-start(bf16[2,20,32,512]{3,2,1,0:T(8,128)(2,1)S(1)} %pad_maximum_fusion.1), channel_id=1, source_target_pairs={{0,32},{4,36},{8,40},{12,44},{16,48},{20,52},{24,56},{28,60},{32,6... | collective-permute-start | bytes 3932168 | tf_op jit(solution)/shard_map/ppermute | solution.py:16

commit v3 on v2

--- a/solution.py
+++ b/solution.py
@@ -22,6 +22,16 @@
     return position % GH, position // GH, tile_count // GH
 
 
+def shared_along(value, steps):
+    core = lax.axis_index("chan") % 2
+    half = value.shape[1] // 2
+    mine = lax.dynamic_slice_in_dim(value, core * half, half, 1)
+    mine = passed_along(mine, "space", steps)
+    count = lax.axis_size("chan")
+    theirs = lax.ppermute(mine, "chan", [(source, source ^ 1) for source in range(count)])
+    return jnp.where(core == 0, jnp.concatenate([mine, theirs], 1), jnp.concatenate([theirs, mine], 1))
+
+
 def wide_border(volume_tile, rim):
     tile_row, depth_tile, grid_depth = tile_place()
     above_rim = passed_along(volume_tile[:, -rim:], "space", 1)
@@ -29,8 +39,8 @@
     above_rim = jnp.where(tile_row > 0, above_rim, jnp.zeros_like(above_rim))
     below_rim = jnp.where(tile_row < GH - 1, below_rim, jnp.zeros_like(below_rim))
     taller = jnp.concatenate([above_rim, volume_tile, below_rim], 1)
-    front_rim = passed_along(taller[-rim:], "space", GH)
-    back_rim = passed_along(taller[:rim], "space", -GH)
+    front_rim = shared_along(taller[-rim:], GH)
+    back_rim = shared_along(taller[:rim], -GH)
     front_rim = jnp.where(depth_tile > 0, front_rim, jnp.zeros_like(front_rim))
     back_rim = jnp.where(depth_tile < grid_depth - 1, back_rim, jnp.zeros_like(back_rim))
     return jnp.concatenate([front_rim, taller, back_rim], 0)

time: 131 us -> 108 us (0.82); the launches traced: 129 us -> 108 us
  waiting for transfers between devices: 54.7 us -> 28.7 us
  starting transfers between devices: 14.6 us -> 19.5 us
    ppermute x4, waiting for transfers between devices: 54.7 us -> 28.7 us  [passed_along(): return lax.ppermute(value, axis, pairs)]
    ppermute x0 -> x2, starting transfers between devices: none -> 3.69 us  [shared_along(): lax.ppermute(mine, 'chan', [(source, source ^ 1) for source in range(coun...]
  transfers between devices with their start and end apart: 4 -> 6, of which waited for: 3 -> 2; matrix products, arithmetic and copies ran while one was open for 3% -> 4% of each run, Pallas kernels for 0% -> 0%
where the time goes in v3:
time: 108 us
  Pallas kernels  37.9 us (35%)
  waiting for transfers between devices  28.7 us (27%)
  starting transfers between devices  19.5 us (18%)
  blocking collectives  9.11 us (8%)
  local copies, waits for them, and re-layouts  6.72 us (6%)
  other arithmetic  6.05 us (6%)
    pallas_call x1, Pallas kernels, two_layers(): pl.pallas_call(two_layers_kernel, out_shape=jax.ShapeDtypeStruct((in_dept...  37.9 us
    ppermute x4, waiting for transfers between devices, passed_along(): return lax.ppermute(value, axis, pairs)  28.7 us
    ppermute x4, starting transfers between devices, passed_along(): return lax.ppermute(value, axis, pairs)  15.9 us
    all_gather x1, blocking collectives, local(): all_first = lax.all_gather(first_filters, 'chan', axis=3, tiled=True)  9.11 us
    ppermute x2, starting transfers between devices, shared_along(): lax.ppermute(mine, 'chan', [(source, source ^ 1) for source in range(coun...  3.69 us
    concatenate x1, other arithmetic, wide_border(): return jnp.concatenate([front_rim, taller, back_rim], 0)  2.17 us
  transfers between devices with their start and end apart: 6, of which 2 were waited for; matrix products, arithmetic and copies ran while one was open for 4% of the time, Pallas kernels for 0%

profile of v3, /device:TPU:1, one launch (start us, length us, event | category | flops | bytes accessed | tf_op | source)
XLA Modules:
  0.0 108.1 jit_solution(4280559159657298990)
XLA Ops:
  0.0 1.8 %copy.14 = bf16[32,2,16,512]{3,0,2,1:T(8,128)(2,1)S(1)} copy(bf16[32,2,16,512]{3,2,1,0:T(8,128)(2,1)} %param.3) | data formatting | bytes 2097152 | tf_op args[0]
  1.8 0.0 copy-start.1
  1.8 3.9 %collective-permute-start = (bf16[2,2,32,512]{3,2,1,0:T(8,128)(2,1)S(1)}, bf16[2,2,32,512]{3,2,1,0:T(8,128)(2,1)S(1)}, u32[]{:S(2)}, u32[]{:S(2)}) collective-permute-start(bf16[2,2,32,512]{3,2,1,0:T(8,128)(2,1)S(1)} %get-tuple-element.6), channel_id=1, source_target_pairs={{0,4},{4,8},{8,12},{12,16},{16,20},{20,24},{24,28},{28,32},{32,36}... | collective-permute-start | bytes 393224 | tf_op jit(solution)/shard_map/ppermute | solution.py:16
  5.7 7.8 %collective-permute-start.1 = (bf16[2,2,32,512]{3,2,1,0:T(8,128)(2,1)S(1)}, bf16[2,2,32,512]{3,2,1,0:T(8,128)(2,1)S(1)}, u32[]{:S(2)}, u32[]{:S(2)}) collective-permute-start(bf16[2,2,32,512]{3,2,1,0:T(8,128)(2,1)S(1)} %get-tuple-element.5), channel_id=1, source_target_pairs={{0,252},{4,0},{8,4},{12,8},{16,12},{20,16},{24,20},{28,24},{32,28}... | collective-permute-start | bytes 393224 | tf_op jit(solution)/shard_map/ppermute | solution.py:16
  13.5 3.7 %collective-permute-done = bf16[2,2,32,512]{3,2,1,0:T(8,128)(2,1)S(1)} collective-permute-done((bf16[2,2,32,512]{3,2,1,0:T(8,128)(2,1)S(1)}, bf16[2,2,32,512]{3,2,1,0:T(8,128)(2,1)S(1)}, u32[]{:S(2)}, u32[]{:S(2)}) %collective-permute-start) | collective-permute-done | bytes 131104 | tf_op jit(solution)/shard_map/ppermute | solution.py:16
  17.2 0.2 fusion.3
  17.5 0.0 copy-start
  17.5 4.2 %collective-permute-start.4 = (bf16[2,10,32,512]{3,2,1,0:T(8,128)(2,1)S(1)}, bf16[2,10,32,512]{3,2,1,0:T(8,128)(2,1)}, u32[]{:S(2)}, u32[]{:S(2)}) collective-permute-start(bf16[2,10,32,512]{3,2,1,0:T(8,128)(2,1)S(1)} %fusion.3), channel_id=1, source_target_pairs={{0,224},{4,228},{8,232},{12,236},{16,240},{20,244},{24,248},{28,25... | collective-permute-start | bytes 1966088 | tf_op jit(solution)/shard_map/ppermute | solution.py:16
  21.7 25.0 %collective-permute-done.4 = bf16[2,10,32,512]{3,2,1,0:T(8,128)(2,1)} collective-permute-done((bf16[2,10,32,512]{3,2,1,0:T(8,128)(2,1)S(1)}, bf16[2,10,32,512]{3,2,1,0:T(8,128)(2,1)}, u32[]{:S(2)}, u32[]{:S(2)}) %collective-permute-start.4) | collective-permute-done | bytes 655392 | tf_op jit(solution)/shard_map/ppermute | solution.py:16
  46.7 3.7 %collective-permute-start.5 = (bf16[2,10,32,512]{3,2,1,0:T(8,128)(2,1)}, bf16[2,10,32,512]{3,2,1,0:T(8,128)(2,1)}, u32[]{:S(2)}, u32[]{:S(2)}) collective-permute-start(bf16[2,10,32,512]{3,2,1,0:T(8,128)(2,1)} %collective-permute-done.4), channel_id=1, source_target_pairs={{0,1},{1,0},{2,3},{3,2},{4,5},{5,4},{6,7},{7,6},{8,9},{9,8},{10,11... | collective-permute-start | bytes 1966088 | tf_op jit(solution)/shard_map/ppermute | solution.py:31
  50.4 0.0 collective-permute-start.3
  50.4 0.1 and_convert_fusion
  50.5 0.7 reshape.20.keep_ref
  51.1 9.1 %all_gather.3 = bf16[3,3,3,64,32]{4,3,2,1,0:T(8,128)(2,1)S(1)} all-gather(bf16[3,3,3,16,32]{4,3,2,1,0:T(8,128)(2,1)S(1)} %copy-done.1), channel_id=1, replica_groups=mesh['space'=64,'chan'=4] {'chan'}, dimensions={3}, use_global_device_ids=true | all-gather | bytes 138240 | tf_op jit(solution)/shard_map/all_gather | solution.py:128
  60.3 0.3 copy.9
  60.5 0.2 reshape.18
  60.8 0.8 copy.11.w1_ref
  61.5 0.1 copy.10
  61.6 0.8 reshape.19.w2_ref
  62.4 1.9 %fusion.1 = bf16[2,20,32,512]{3,2,1,0:T(8,128)(2,1)S(1)} fusion(bf16[2,10,32,512]{3,2,1,0:T(8,128)(2,1)} %collective-permute-done.5, bf16[2,10,32,512]{3,2,1,0:T(8,128)(2,1)} %collective-permute-done.4, pred[]{:T(512)S(6)} %lt.49, pred[]{:T(512)S(6)} %eq.11), kind=kLoop, calls=%fused_computation.7 | loop fusion | flops 2621440 | bytes 2621442 | tf_op jit(solution)/shard_map/jit(_where)/select_n | solution.py:45
  64.3 1.6 %fusion = bf16[2,20,32,512]{3,2,1,0:T(8,128)(2,1)S(1)} fusion(bf16[2,10,32,512]{3,2,1,0:T(8,128)(2,1)} %collective-permute-done.3, bf16[2,10,32,512]{3,2,1,0:T(8,128)(2,1)S(1)} %collective-permute-done.2, pred[]{:T(512)S(6)} %eq.11, pred[]{:T(512)S(6)} %gt.17), kind=kLoop, calls=%fused_computation.5 | loop fusion | flops 2621440 | bytes 2621442 | tf_op jit(solution)/shard_map/jit(_where)/select_n | solution.py:44
  65.9 2.2 %pad_maximum_fusion.x_ref = bf16[6,20,32,512]{3,2,1,0:T(8,128)(2,1)} fusion(bf16[2,20,32,512]{3,2,1,0:T(8,128)(2,1)S(1)} %fusion.1, bf16[2,2,32,512]{3,2,1,0:T(8,128)(2,1)S(1)} %broadcast_select_fusion, bf16[2,16,32,512]{3,2,1,0:T(8,128)(2,1)S(1)} %bitcast.10, bf16[2,2,32,512]{3,2,1,0:T(8,128)(2,1)S(1)} %broadcast_select_fusion.1, ...), kind=kLoop, calls=%fused_computation | loop fusion | flops 7864320 | bytes 7864320 | tf_op jit(solution)/shard_map/concatenate | solution.py:46
  68.1 37.9 %shard_map.37 = bf16[2,16,16,512]{3,2,1,0:T(8,128)(2,1)} custom-call(s32[72]{0:T(128)} %reshape.20.keep_ref, bf16[6,20,32,512]{3,2,1,0:T(8,128)(2,1)} %pad_maximum_fusion.x_ref, bf16[192,288]{1,0:T(8,128)(2,1)} %copy.11.w1_ref, bf16[48,576]{1,0:T(8,128)(2,1)} %reshape.19.w2_ref), custom_call_target="tpu_custom_call" | custom-call | tf_op jit(solution)/shard_map/pallas_call | solution.py:97
  106.0 2.1 %copy.12 = bf16[16,2,16,512]{3,2,1,0:T(8,128)(2,1)} copy(bf16[16,2,16,512]{3,0,2,1:T(8,128)(2,1)} %bitcast.11) | data formatting | bytes 1048576 | tf_op jit(solution)/shard_map/transpose | solution.py:133
  (12 shorter events, 0.1 us)
Async XLA Ops:
  1.8 49.3 %copy-start.1 = (bf16[3,3,3,16,32]{4,3,2,1,0:T(8,128)(2,1)S(1)}, bf16[3,3,3,16,32]{4,3,2,1,0:T(8,128)(2,1)}, u32[]{:S(2)}) copy-start(bf16[3,3,3,16,32]{4,3,2,1,0:T(8,128)(2,1)} %param.4) | copy-start | bytes 82948
  1.8 15.3 %collective-permute-start = (bf16[2,2,32,512]{3,2,1,0:T(8,128)(2,1)S(1)}, bf16[2,2,32,512]{3,2,1,0:T(8,128)(2,1)S(1)}, u32[]{:S(2)}, u32[]{:S(2)}) collective-permute-start(bf16[2,2,32,512]{3,2,1,0:T(8,128)(2,1)S(1)} %get-tuple-element.6), channel_id=1, source_target_pairs={{0,4},{4,8},{8,12},{12,16},{16,20},{20,24},{24,28},{28,32},{32,36}... | collective-permute-start | bytes 393224 | tf_op jit(solution)/shard_map/ppermute | solution.py:16
  5.7 11.5 %collective-permute-start.1 = (bf16[2,2,32,512]{3,2,1,0:T(8,128)(2,1)S(1)}, bf16[2,2,32,512]{3,2,1,0:T(8,128)(2,1)S(1)}, u32[]{:S(2)}, u32[]{:S(2)}) collective-permute-start(bf16[2,2,32,512]{3,2,1,0:T(8,128)(2,1)S(1)} %get-tuple-element.5), channel_id=1, source_target_pairs={{0,252},{4,0},{8,4},{12,8},{16,12},{20,16},{24,20},{28,24},{32,28}... | collective-permute-start | bytes 393224 | tf_op jit(solution)/shard_map/ppermute | solution.py:16
  17.5 44.1 %copy-start = (bf16[3,3,3,16,64]{4,3,2,1,0:T(8,128)(2,1)S(1)}, bf16[3,3,3,16,64]{4,3,2,1,0:T(8,128)(2,1)}, u32[]{:S(2)}) copy-start(bf16[3,3,3,16,64]{4,3,2,1,0:T(8,128)(2,1)} %param.5) | copy-start | bytes 165892
  17.5 29.2 %collective-permute-start.4 = (bf16[2,10,32,512]{3,2,1,0:T(8,128)(2,1)S(1)}, bf16[2,10,32,512]{3,2,1,0:T(8,128)(2,1)}, u32[]{:S(2)}, u32[]{:S(2)}) collective-permute-start(bf16[2,10,32,512]{3,2,1,0:T(8,128)(2,1)S(1)} %fusion.3), channel_id=1, source_target_pairs={{0,224},{4,228},{8,232},{12,236},{16,240},{20,244},{24,248},{28,25... | collective-permute-start | bytes 1966088 | tf_op jit(solution)/shard_map/ppermute | solution.py:16
  21.7 28.7 %collective-permute-start.2 = (bf16[2,10,32,512]{3,2,1,0:T(8,128)(2,1)S(1)}, bf16[2,10,32,512]{3,2,1,0:T(8,128)(2,1)S(1)}, u32[]{:S(2)}, u32[]{:S(2)}) collective-permute-start(bf16[2,10,32,512]{3,2,1,0:T(8,128)(2,1)S(1)} %fusion.3), channel_id=1, source_target_pairs={{0,32},{4,36},{8,40},{12,44},{16,48},{20,52},{24,56},{28,60},{32,6... | collective-permute-start | bytes 1966088 | tf_op jit(solution)/shard_map/ppermute | solution.py:16
  46.7 15.7 %collective-permute-start.5 = (bf16[2,10,32,512]{3,2,1,0:T(8,128)(2,1)}, bf16[2,10,32,512]{3,2,1,0:T(8,128)(2,1)}, u32[]{:S(2)}, u32[]{:S(2)}) collective-permute-start(bf16[2,10,32,512]{3,2,1,0:T(8,128)(2,1)} %collective-permute-done.4), channel_id=1, source_target_pairs={{0,1},{1,0},{2,3},{3,2},{4,5},{5,4},{6,7},{7,6},{8,9},{9,8},{10,11... | collective-permute-start | bytes 1966088 | tf_op jit(solution)/shard_map/ppermute | solution.py:31
  50.4 13.9 %collective-permute-start.3 = (bf16[2,10,32,512]{3,2,1,0:T(8,128)(2,1)S(1)}, bf16[2,10,32,512]{3,2,1,0:T(8,128)(2,1)}, u32[]{:S(2)}, u32[]{:S(2)}) collective-permute-start(bf16[2,10,32,512]{3,2,1,0:T(8,128)(2,1)S(1)} %collective-permute-done.2), channel_id=1, source_target_pairs={{0,1},{1,0},{2,3},{3,2},{4,5},{5,4},{6,7},{7,6},{8,9},{9,8},{10,11... | collective-permute-start | bytes 1966088 | tf_op jit(solution)/shard_map/ppermute | solution.py:31

commit v4 on v3

--- a/solution.py
+++ b/solution.py
@@ -124,8 +124,21 @@
     return keep.astype(jnp.int32).reshape(-1)
 
 
+def gathered_filters(first_filters, second_filters):
+    count = lax.axis_size("chan")
+    own = lax.axis_index("chan")
+    pieces = [first_filters]
+    for steps in range(1, count):
+        pieces.append(passed_along(first_filters, "chan", -steps))
+    all_first = jnp.concatenate(pieces, 3)
+    block = first_filters.shape[3]
+    doubled = jnp.concatenate([second_filters, second_filters], 4)
+    all_second = lax.dynamic_slice_in_dim(doubled, own * block, second_filters.shape[4], 4)
+    return all_first, all_second
+
+
 def local(voxels, first_filters, second_filters):
-    all_first = lax.all_gather(first_filters, "chan", axis=3, tiled=True)
+    all_first, second_filters = gathered_filters(first_filters, second_filters)
     tile = voxels.transpose(1, 2, 0, 3)
     padded = wide_border(tile, 2)
     keep = inside_flags(padded.shape[0] - 2, padded.shape[1] - 2)

time: 108 us -> 101 us (0.935)
  blocking collectives: 9.11 us -> 0 us
  starting transfers between devices: 19.5 us -> 23.6 us
  waiting for transfers between devices: 28.7 us -> 24.8 us
  other arithmetic: 6.05 us -> 7.14 us
    all_gather x1 -> x0, blocking collectives: 9.11 us -> none  [local(): all_first = lax.all_gather(first_filters, 'chan', axis=3, tiled=True)]
    ppermute x4 -> x7, waiting for transfers between devices: 28.7 us -> 24.8 us  [passed_along(): return lax.ppermute(value, axis, pairs)]
    ppermute x4 -> x7, starting transfers between devices: 15.9 us -> 19.8 us  [passed_along(): return lax.ppermute(value, axis, pairs)]
    transpose x0 -> x2, other arithmetic: none -> 1.17 us  [tap_matrices(): return filters.transpose(2, 3, 0, 1, 4).reshape(e * o, a * b * c)]
  transfers between devices with their start and end apart: 6 -> 9, of which waited for: 2 -> 2; matrix products, arithmetic and copies ran while one was open for 4% -> 6% of each run, Pallas kernels for 0% -> 0%
where the time goes in v4:
time: 101 us; the launch traced here: 100 us
  Pallas kernels  37.9 us (38%)
  waiting for transfers between devices  24.8 us (25%)
  starting transfers between devices  23.6 us (23%)
  other arithmetic  7.14 us (7%)
  local copies, waits for them, and re-layouts  6.73 us (7%)
    pallas_call x1, Pallas kernels, two_layers(): pl.pallas_call(two_layers_kernel, out_shape=jax.ShapeDtypeStruct((in_dept...  37.9 us
    ppermute x7, waiting for transfers between devices, passed_along(): return lax.ppermute(value, axis, pairs)  24.8 us
    ppermute x7, starting transfers between devices, passed_along(): return lax.ppermute(value, axis, pairs)  19.8 us
    ppermute x2, starting transfers between devices, shared_along(): lax.ppermute(mine, 'chan', [(source, source ^ 1) for source in range(coun...  3.79 us
    concatenate x1, other arithmetic, wide_border(): return jnp.concatenate([front_rim, taller, back_rim], 0)  2.16 us
    transpose x1, local copies, waits for them, and re-layouts, local(): return out.transpose(2, 0, 1, 3)  2.13 us
  transfers between devices with their start and end apart: 9, of which 2 were waited for; matrix products, arithmetic and copies ran while one was open for 6% of the time, Pallas kernels for 0%

profile of v4, /device:TPU:1, one launch (start us, length us, event | category | flops | bytes accessed | tf_op | source)
XLA Modules:
  0.0 100.2 jit_solution(6088240726079104231)
XLA Ops:
  0.0 1.8 %copy.14 = bf16[32,2,16,512]{3,0,2,1:T(8,128)(2,1)S(1)} copy(bf16[32,2,16,512]{3,2,1,0:T(8,128)(2,1)} %param.3) | data formatting | bytes 2097152 | tf_op args[0]
  1.8 3.9 %collective-permute-start = (bf16[2,2,32,512]{3,2,1,0:T(8,128)(2,1)S(1)}, bf16[2,2,32,512]{3,2,1,0:T(8,128)(2,1)S(1)}, u32[]{:S(2)}, u32[]{:S(2)}) collective-permute-start(bf16[2,2,32,512]{3,2,1,0:T(8,128)(2,1)S(1)} %get-tuple-element.6), channel_id=1, source_target_pairs={{0,4},{4,8},{8,12},{12,16},{16,20},{20,24},{24,28},{28,32},{32,36}... | collective-permute-start | bytes 393224 | tf_op jit(solution)/shard_map/ppermute | solution.py:16
  5.7 7.8 %collective-permute-start.1 = (bf16[2,2,32,512]{3,2,1,0:T(8,128)(2,1)S(1)}, bf16[2,2,32,512]{3,2,1,0:T(8,128)(2,1)S(1)}, u32[]{:S(2)}, u32[]{:S(2)}) collective-permute-start(bf16[2,2,32,512]{3,2,1,0:T(8,128)(2,1)S(1)} %get-tuple-element.5), channel_id=1, source_target_pairs={{0,252},{4,0},{8,4},{12,8},{16,12},{20,16},{24,20},{28,24},{32,28}... | collective-permute-start | bytes 393224 | tf_op jit(solution)/shard_map/ppermute | solution.py:16
  13.5 3.7 %collective-permute-done = bf16[2,2,32,512]{3,2,1,0:T(8,128)(2,1)S(1)} collective-permute-done((bf16[2,2,32,512]{3,2,1,0:T(8,128)(2,1)S(1)}, bf16[2,2,32,512]{3,2,1,0:T(8,128)(2,1)S(1)}, u32[]{:S(2)}, u32[]{:S(2)}) %collective-permute-start) | collective-permute-done | bytes 131104 | tf_op jit(solution)/shard_map/ppermute | solution.py:16
  17.2 0.2 fusion.3
  17.5 4.2 %collective-permute-start.4 = (bf16[2,10,32,512]{3,2,1,0:T(8,128)(2,1)S(1)}, bf16[2,10,32,512]{3,2,1,0:T(8,128)(2,1)}, u32[]{:S(2)}, u32[]{:S(2)}) collective-permute-start(bf16[2,10,32,512]{3,2,1,0:T(8,128)(2,1)S(1)} %fusion.3), channel_id=1, source_target_pairs={{0,224},{4,228},{8,232},{12,236},{16,240},{20,244},{24,248},{28,25... | collective-permute-start | bytes 1966088 | tf_op jit(solution)/shard_map/ppermute | solution.py:16
  21.7 3.5 %collective-permute-start.8 = (bf16[3,3,3,16,32]{4,3,2,1,0:T(8,128)(2,1)S(1)}, bf16[3,3,3,16,32]{4,3,2,1,0:T(8,128)(2,1)S(1)}, u32[]{:S(2)}, u32[]{:S(2)}) collective-permute-start(bf16[3,3,3,16,32]{4,3,2,1,0:T(8,128)(2,1)S(1)} %copy-done.1), channel_id=1, source_target_pairs={{0,1},{1,2},{2,3},{3,0},{4,5},{5,6},{6,7},{7,4},{8,9},{9,10},{10,1... | collective-permute-start | bytes 82952 | tf_op jit(solution)/shard_map/ppermute | solution.py:16
  25.2 0.1 collective-permute-start.7
  25.3 0.3 collective-permute-start.6
  25.6 21.1 %collective-permute-done.4 = bf16[2,10,32,512]{3,2,1,0:T(8,128)(2,1)} collective-permute-done((bf16[2,10,32,512]{3,2,1,0:T(8,128)(2,1)S(1)}, bf16[2,10,32,512]{3,2,1,0:T(8,128)(2,1)}, u32[]{:S(2)}, u32[]{:S(2)}) %collective-permute-start.4) | collective-permute-done | bytes 655392 | tf_op jit(solution)/shard_map/ppermute | solution.py:16
  46.7 3.7 %collective-permute-start.5 = (bf16[2,10,32,512]{3,2,1,0:T(8,128)(2,1)}, bf16[2,10,32,512]{3,2,1,0:T(8,128)(2,1)}, u32[]{:S(2)}, u32[]{:S(2)}) collective-permute-start(bf16[2,10,32,512]{3,2,1,0:T(8,128)(2,1)} %collective-permute-done.4), channel_id=1, source_target_pairs={{0,1},{1,0},{2,3},{3,2},{4,5},{5,4},{6,7},{7,6},{8,9},{9,8},{10,11... | collective-permute-start | bytes 1966088 | tf_op jit(solution)/shard_map/ppermute | solution.py:31
  50.4 0.1 collective-permute-start.3
  50.6 0.2 fusion.4
  50.7 0.7 reshape.20.keep_ref
  51.5 0.8 reshape.19.w2_ref
  52.2 1.0 %maximum_bitcast_fusion = bf16[3,64,3,3,32]{4,1,0,3,2:T(8,128)(2,1)S(1)} fusion(bf16[3,3,3,16,32]{4,3,2,1,0:T(8,128)(2,1)S(1)} %collective-permute-done.8, bf16[3,3,3,16,32]{4,3,2,1,0:T(8,128)(2,1)S(1)} %collective-permute-done.7, bf16[3,3,3,16,32]{4,3,2,1,0:T(8,128)(2,1)} %collective-permute-done.6, bf16[3,3,3,16,32]{4,3,2,1,0:T(8,128)(2,1)S(1)} %copy-done.1), kind=kLoop, calls=%fused_computation.11 | loop fusion | flops 442368 | bytes 221184 | tf_op jit(solution)/shard_map/transpose | solution.py:113
  53.3 0.3 copy.9
  53.6 0.2 reshape.18
  53.8 0.8 copy.11.w1_ref
  54.6 1.9 %fusion.1 = bf16[2,20,32,512]{3,2,1,0:T(8,128)(2,1)S(1)} fusion(bf16[2,10,32,512]{3,2,1,0:T(8,128)(2,1)} %collective-permute-done.5, bf16[2,10,32,512]{3,2,1,0:T(8,128)(2,1)} %collective-permute-done.4, pred[]{:T(512)S(6)} %lt.52, pred[]{:T(512)S(6)} %eq.11), kind=kLoop, calls=%fused_computation.7 | loop fusion | flops 2621440 | bytes 2621442 | tf_op jit(solution)/shard_map/jit(_where)/select_n | solution.py:45
  56.5 1.5 %fusion = bf16[2,20,32,512]{3,2,1,0:T(8,128)(2,1)S(1)} fusion(bf16[2,10,32,512]{3,2,1,0:T(8,128)(2,1)} %collective-permute-done.3, bf16[2,10,32,512]{3,2,1,0:T(8,128)(2,1)S(1)} %collective-permute-done.2, pred[]{:T(512)S(6)} %eq.11, pred[]{:T(512)S(6)} %gt.17), kind=kLoop, calls=%fused_computation.5 | loop fusion | flops 2621440 | bytes 2621442 | tf_op jit(solution)/shard_map/jit(_where)/select_n | solution.py:44
  58.0 2.2 %pad_maximum_fusion.x_ref = bf16[6,20,32,512]{3,2,1,0:T(8,128)(2,1)} fusion(bf16[2,20,32,512]{3,2,1,0:T(8,128)(2,1)S(1)} %fusion.1, bf16[2,2,32,512]{3,2,1,0:T(8,128)(2,1)S(1)} %broadcast_select_fusion, bf16[2,16,32,512]{3,2,1,0:T(8,128)(2,1)S(1)} %bitcast.12, bf16[2,2,32,512]{3,2,1,0:T(8,128)(2,1)S(1)} %broadcast_select_fusion.1, ...), kind=kLoop, calls=%fused_computation | loop fusion | flops 7864320 | bytes 7864320 | tf_op jit(solution)/shard_map/concatenate | solution.py:46
  60.2 37.9 %shard_map.37 = bf16[2,16,16,512]{3,2,1,0:T(8,128)(2,1)} custom-call(s32[72]{0:T(128)} %reshape.20.keep_ref, bf16[6,20,32,512]{3,2,1,0:T(8,128)(2,1)} %pad_maximum_fusion.x_ref, bf16[192,288]{1,0:T(8,128)(2,1)} %copy.11.w1_ref, bf16[48,576]{1,0:T(8,128)(2,1)} %reshape.19.w2_ref), custom_call_target="tpu_custom_call" | custom-call | tf_op jit(solution)/shard_map/pallas_call | solution.py:97
  98.1 2.1 %copy.12 = bf16[16,2,16,512]{3,2,1,0:T(8,128)(2,1)} copy(bf16[16,2,16,512]{3,0,2,1:T(8,128)(2,1)} %bitcast.13) | data formatting | bytes 1048576 | tf_op jit(solution)/shard_map/transpose | solution.py:146
  (19 shorter events, 0.2 us)
Async XLA Ops:
  1.8 19.9 %copy-start.1 = (bf16[3,3,3,16,32]{4,3,2,1,0:T(8,128)(2,1)S(1)}, bf16[3,3,3,16,32]{4,3,2,1,0:T(8,128)(2,1)}, u32[]{:S(2)}) copy-start(bf16[3,3,3,16,32]{4,3,2,1,0:T(8,128)(2,1)} %param.4) | copy-start | bytes 82948
  1.8 15.3 %collective-permute-start = (bf16[2,2,32,512]{3,2,1,0:T(8,128)(2,1)S(1)}, bf16[2,2,32,512]{3,2,1,0:T(8,128)(2,1)S(1)}, u32[]{:S(2)}, u32[]{:S(2)}) collective-permute-start(bf16[2,2,32,512]{3,2,1,0:T(8,128)(2,1)S(1)} %get-tuple-element.6), channel_id=1, source_target_pairs={{0,4},{4,8},{8,12},{12,16},{16,20},{20,24},{24,28},{28,32},{32,36}... | collective-permute-start | bytes 393224 | tf_op jit(solution)/shard_map/ppermute | solution.py:16
  5.7 44.8 %copy-start = (bf16[3,3,3,16,64]{4,3,2,1,0:T(8,128)(2,1)S(1)}, bf16[3,3,3,16,64]{4,3,2,1,0:T(8,128)(2,1)}, u32[]{:S(2)}) copy-start(bf16[3,3,3,16,64]{4,3,2,1,0:T(8,128)(2,1)} %param.5) | copy-start | bytes 165892
  5.7 11.5 %collective-permute-start.1 = (bf16[2,2,32,512]{3,2,1,0:T(8,128)(2,1)S(1)}, bf16[2,2,32,512]{3,2,1,0:T(8,128)(2,1)S(1)}, u32[]{:S(2)}, u32[]{:S(2)}) collective-permute-start(bf16[2,2,32,512]{3,2,1,0:T(8,128)(2,1)S(1)} %get-tuple-element.5), channel_id=1, source_target_pairs={{0,252},{4,0},{8,4},{12,8},{16,12},{20,16},{24,20},{28,24},{32,28}... | collective-permute-start | bytes 393224 | tf_op jit(solution)/shard_map/ppermute | solution.py:16
  17.5 29.2 %collective-permute-start.4 = (bf16[2,10,32,512]{3,2,1,0:T(8,128)(2,1)S(1)}, bf16[2,10,32,512]{3,2,1,0:T(8,128)(2,1)}, u32[]{:S(2)}, u32[]{:S(2)}) collective-permute-start(bf16[2,10,32,512]{3,2,1,0:T(8,128)(2,1)S(1)} %fusion.3), channel_id=1, source_target_pairs={{0,224},{4,228},{8,232},{12,236},{16,240},{20,244},{24,248},{28,25... | collective-permute-start | bytes 1966088 | tf_op jit(solution)/shard_map/ppermute | solution.py:16
  21.7 28.7 %collective-permute-start.2 = (bf16[2,10,32,512]{3,2,1,0:T(8,128)(2,1)S(1)}, bf16[2,10,32,512]{3,2,1,0:T(8,128)(2,1)S(1)}, u32[]{:S(2)}, u32[]{:S(2)}) collective-permute-start(bf16[2,10,32,512]{3,2,1,0:T(8,128)(2,1)S(1)} %fusion.3), channel_id=1, source_target_pairs={{0,32},{4,36},{8,40},{12,44},{16,48},{20,52},{24,56},{28,60},{32,6... | collective-permute-start | bytes 1966088 | tf_op jit(solution)/shard_map/ppermute | solution.py:16
  21.7 30.5 %collective-permute-start.8 = (bf16[3,3,3,16,32]{4,3,2,1,0:T(8,128)(2,1)S(1)}, bf16[3,3,3,16,32]{4,3,2,1,0:T(8,128)(2,1)S(1)}, u32[]{:S(2)}, u32[]{:S(2)}) collective-permute-start(bf16[3,3,3,16,32]{4,3,2,1,0:T(8,128)(2,1)S(1)} %copy-done.1), channel_id=1, source_target_pairs={{0,1},{1,2},{2,3},{3,0},{4,5},{5,6},{6,7},{7,4},{8,9},{9,10},{10,1... | collective-permute-start | bytes 82952 | tf_op jit(solution)/shard_map/ppermute | solution.py:16
  25.2 27.0 %collective-permute-start.7 = (bf16[3,3,3,16,32]{4,3,2,1,0:T(8,128)(2,1)S(1)}, bf16[3,3,3,16,32]{4,3,2,1,0:T(8,128)(2,1)S(1)}, u32[]{:S(2)}, u32[]{:S(2)}) collective-permute-start(bf16[3,3,3,16,32]{4,3,2,1,0:T(8,128)(2,1)S(1)} %copy-done.1), channel_id=1, source_target_pairs={{0,2},{1,3},{2,0},{3,1},{4,6},{5,7},{6,4},{7,5},{8,10},{9,11},{10,... | collective-permute-start | bytes 82952 | tf_op jit(solution)/shard_map/ppermute | solution.py:16
  25.3 27.0 %collective-permute-start.6 = (bf16[3,3,3,16,32]{4,3,2,1,0:T(8,128)(2,1)S(1)}, bf16[3,3,3,16,32]{4,3,2,1,0:T(8,128)(2,1)}, u32[]{:S(2)}, u32[]{:S(2)}) collective-permute-start(bf16[3,3,3,16,32]{4,3,2,1,0:T(8,128)(2,1)S(1)} %copy-done.1), channel_id=1, source_target_pairs={{0,3},{1,0},{2,1},{3,2},{4,7},{5,4},{6,5},{7,6},{8,11},{9,8},{10,9... | collective-permute-start | bytes 82952 | tf_op jit(solution)/shard_map/ppermute | solution.py:16
  46.7 7.9 %collective-permute-start.5 = (bf16[2,10,32,512]{3,2,1,0:T(8,128)(2,1)}, bf16[2,10,32,512]{3,2,1,0:T(8,128)(2,1)}, u32[]{:S(2)}, u32[]{:S(2)}) collective-permute-start(bf16[2,10,32,512]{3,2,1,0:T(8,128)(2,1)} %collective-permute-done.4), channel_id=1, source_target_pairs={{0,1},{1,0},{2,3},{3,2},{4,5},{5,4},{6,7},{7,6},{8,9},{9,8},{10,11... | collective-permute-start | bytes 1966088 | tf_op jit(solution)/shard_map/ppermute | solution.py:31
  50.4 6.1 %collective-permute-start.3 = (bf16[2,10,32,512]{3,2,1,0:T(8,128)(2,1)S(1)}, bf16[2,10,32,512]{3,2,1,0:T(8,128)(2,1)}, u32[]{:S(2)}, u32[]{:S(2)}) collective-permute-start(bf16[2,10,32,512]{3,2,1,0:T(8,128)(2,1)S(1)} %collective-permute-done.2), channel_id=1, source_target_pairs={{0,1},{1,0},{2,3},{3,2},{4,5},{5,4},{6,7},{7,6},{8,9},{9,8},{10,11... | collective-permute-start | bytes 1966088 | tf_op jit(solution)/shard_map/ppermute | solution.py:31

commit v5 on v4

--- a/solution.py
+++ b/solution.py
@@ -78,7 +78,7 @@
             hid_ref[d, h] = y.astype(hid_ref.dtype)
             return carry
 
-        lax.fori_loop(0, hid_height, first, 0)
+        lax.fori_loop(0, hid_height, first, 0, unroll=True)
 
     for d in range(out_depth):
         def second(h, carry, d=d):
@@ -86,7 +86,7 @@
             o_ref[d, h] = y.astype(o_ref.dtype)
             return carry
 
-        lax.fori_loop(0, out_height, second, 0)
+        lax.fori_loop(0, out_height, second, 0, unroll=True)
 
 
 def two_layers(keep, padded, w1, w2):

time: 101 us -> 77.3 us (0.77)
  Pallas kernels: 37.9 us -> 13.7 us
    pallas_call x1, Pallas kernels: 37.9 us -> 13.7 us  [two_layers(): pl.pallas_call(two_layers_kernel, out_shape=jax.ShapeDtypeStruct((in_dept...]
  transfers between devices with their start and end apart: 9 -> 9, of which waited for: 2 -> 2; matrix products, arithmetic and copies ran while one was open for 6% -> 8% of each run, Pallas kernels for 0% -> 0%
where the time goes in v5:
time: 77.3 us; the launch traced here: 76.2 us
  waiting for transfers between devices  24.8 us (32%)
  starting transfers between devices  23.7 us (31%)
  Pallas kernels  13.7 us (18%)
  other arithmetic  7.14 us (9%)
  local copies, waits for them, and re-layouts  6.73 us (9%)
    ppermute x7, waiting for transfers between devices, passed_along(): return lax.ppermute(value, axis, pairs)  24.8 us
    ppermute x7, starting transfers between devices, passed_along(): return lax.ppermute(value, axis, pairs)  19.8 us
    pallas_call x1, Pallas kernels, two_layers(): pl.pallas_call(two_layers_kernel, out_shape=jax.ShapeDtypeStruct((in_dept...  13.7 us
    ppermute x2, starting transfers between devices, shared_along(): lax.ppermute(mine, 'chan', [(source, source ^ 1) for source in range(coun...  3.97 us
    concatenate x1, other arithmetic, wide_border(): return jnp.concatenate([front_rim, taller, back_rim], 0)  2.16 us
    transpose x1, local copies, waits for them, and re-layouts, local(): return out.transpose(2, 0, 1, 3)  2.13 us
    select_n x1, other arithmetic, wide_border(): jnp.where(depth_tile < grid_depth - 1, back_rim, jnp.zeros_like(back_rim))  1.93 us
    unnamed x5, local copies, waits for them, and re-layouts  1.81 us
  transfers between devices with their start and end apart: 9, of which 2 were waited for; matrix products, arithmetic and copies ran while one was open for 8% of the time, Pallas kernels for 0%

profile of v5, /device:TPU:1, one launch (start us, length us, event | category | flops | bytes accessed | tf_op | source)
XLA Modules:
  0.0 76.2 jit_solution(14088051291297507482)
XLA Ops:
  0.0 1.8 %copy.14 = bf16[32,2,16,512]{3,0,2,1:T(8,128)(2,1)S(1)} copy(bf16[32,2,16,512]{3,2,1,0:T(8,128)(2,1)} %param.3) | data formatting | bytes 2097152 | tf_op args[0]
  1.8 3.9 %collective-permute-start = (bf16[2,2,32,512]{3,2,1,0:T(8,128)(2,1)S(1)}, bf16[2,2,32,512]{3,2,1,0:T(8,128)(2,1)S(1)}, u32[]{:S(2)}, u32[]{:S(2)}) collective-permute-start(bf16[2,2,32,512]{3,2,1,0:T(8,128)(2,1)S(1)} %get-tuple-element.6), channel_id=1, source_target_pairs={{0,4},{4,8},{8,12},{12,16},{16,20},{20,24},{24,28},{28,32},{32,36}... | collective-permute-start | bytes 393224 | tf_op jit(solution)/shard_map/ppermute | solution.py:16
  5.7 7.8 %collective-permute-start.1 = (bf16[2,2,32,512]{3,2,1,0:T(8,128)(2,1)S(1)}, bf16[2,2,32,512]{3,2,1,0:T(8,128)(2,1)S(1)}, u32[]{:S(2)}, u32[]{:S(2)}) collective-permute-start(bf16[2,2,32,512]{3,2,1,0:T(8,128)(2,1)S(1)} %get-tuple-element.5), channel_id=1, source_target_pairs={{0,252},{4,0},{8,4},{12,8},{16,12},{20,16},{24,20},{28,24},{32,28}... | collective-permute-start | bytes 393224 | tf_op jit(solution)/shard_map/ppermute | solution.py:16
  13.5 3.7 %collective-permute-done = bf16[2,2,32,512]{3,2,1,0:T(8,128)(2,1)S(1)} collective-permute-done((bf16[2,2,32,512]{3,2,1,0:T(8,128)(2,1)S(1)}, bf16[2,2,32,512]{3,2,1,0:T(8,128)(2,1)S(1)}, u32[]{:S(2)}, u32[]{:S(2)}) %collective-permute-start) | collective-permute-done | bytes 131104 | tf_op jit(solution)/shard_map/ppermute | solution.py:16
  17.2 0.2 fusion.3
  17.5 4.2 %collective-permute-start.4 = (bf16[2,10,32,512]{3,2,1,0:T(8,128)(2,1)S(1)}, bf16[2,10,32,512]{3,2,1,0:T(8,128)(2,1)}, u32[]{:S(2)}, u32[]{:S(2)}) collective-permute-start(bf16[2,10,32,512]{3,2,1,0:T(8,128)(2,1)S(1)} %fusion.3), channel_id=1, source_target_pairs={{0,224},{4,228},{8,232},{12,236},{16,240},{20,244},{24,248},{28,25... | collective-permute-start | bytes 1966088 | tf_op jit(solution)/shard_map/ppermute | solution.py:16
  21.7 3.5 %collective-permute-start.8 = (bf16[3,3,3,16,32]{4,3,2,1,0:T(8,128)(2,1)S(1)}, bf16[3,3,3,16,32]{4,3,2,1,0:T(8,128)(2,1)S(1)}, u32[]{:S(2)}, u32[]{:S(2)}) collective-permute-start(bf16[3,3,3,16,32]{4,3,2,1,0:T(8,128)(2,1)S(1)} %copy-done.1), channel_id=1, source_target_pairs={{0,1},{1,2},{2,3},{3,0},{4,5},{5,6},{6,7},{7,4},{8,9},{9,10},{10,1... | collective-permute-start | bytes 82952 | tf_op jit(solution)/shard_map/ppermute | solution.py:16
  25.2 0.1 collective-permute-start.7
  25.3 0.3 collective-permute-start.6
  25.6 21.1 %collective-permute-done.4 = bf16[2,10,32,512]{3,2,1,0:T(8,128)(2,1)} collective-permute-done((bf16[2,10,32,512]{3,2,1,0:T(8,128)(2,1)S(1)}, bf16[2,10,32,512]{3,2,1,0:T(8,128)(2,1)}, u32[]{:S(2)}, u32[]{:S(2)}) %collective-permute-start.4) | collective-permute-done | bytes 655392 | tf_op jit(solution)/shard_map/ppermute | solution.py:16
  46.7 3.7 %collective-permute-start.5 = (bf16[2,10,32,512]{3,2,1,0:T(8,128)(2,1)}, bf16[2,10,32,512]{3,2,1,0:T(8,128)(2,1)}, u32[]{:S(2)}, u32[]{:S(2)}) collective-permute-start(bf16[2,10,32,512]{3,2,1,0:T(8,128)(2,1)} %collective-permute-done.4), channel_id=1, source_target_pairs={{0,1},{1,0},{2,3},{3,2},{4,5},{5,4},{6,7},{7,6},{8,9},{9,8},{10,11... | collective-permute-start | bytes 1966088 | tf_op jit(solution)/shard_map/ppermute | solution.py:31
  50.4 0.3 collective-permute-start.3
  50.8 0.2 fusion.4
  50.9 0.7 reshape.20.keep_ref
  51.6 0.8 %reshape.19.w2_ref = bf16[48,576]{1,0:T(8,128)(2,1)} reshape(bf16[3,16,3,3,64]{4,3,2,1,0:T(4,128)(2,1)S(1)} %copy.10) | data formatting | bytes 110592 | tf_op jit(solution)/shard_map/reshape | solution.py:113
  52.4 1.0 %maximum_bitcast_fusion = bf16[3,64,3,3,32]{4,1,0,3,2:T(8,128)(2,1)S(1)} fusion(bf16[3,3,3,16,32]{4,3,2,1,0:T(8,128)(2,1)S(1)} %collective-permute-done.8, bf16[3,3,3,16,32]{4,3,2,1,0:T(8,128)(2,1)S(1)} %collective-permute-done.7, bf16[3,3,3,16,32]{4,3,2,1,0:T(8,128)(2,1)} %collective-permute-done.6, bf16[3,3,3,16,32]{4,3,2,1,0:T(8,128)(2,1)S(1)} %copy-done.1), kind=kLoop, calls=%fused_computation.11 | loop fusion | flops 442368 | bytes 221184 | tf_op jit(solution)/shard_map/transpose | solution.py:113
  53.5 0.3 copy.9
  53.7 0.2 reshape.18
  53.9 0.8 %copy.11.w1_ref = bf16[192,288]{1,0:T(8,128)(2,1)} copy(bf16[192,288]{0,1:T(8,128)(2,1)S(1)} %reshape.18) | data formatting | bytes 221184 | tf_op jit(solution)/shard_map/reshape | solution.py:113
  54.7 1.9 %fusion.1 = bf16[2,20,32,512]{3,2,1,0:T(8,128)(2,1)S(1)} fusion(bf16[2,10,32,512]{3,2,1,0:T(8,128)(2,1)} %collective-permute-done.5, bf16[2,10,32,512]{3,2,1,0:T(8,128)(2,1)} %collective-permute-done.4, pred[]{:T(512)S(6)} %lt.52, pred[]{:T(512)S(6)} %eq.11), kind=kLoop, calls=%fused_computation.7 | loop fusion | flops 2621440 | bytes 2621442 | tf_op jit(solution)/shard_map/jit(_where)/select_n | solution.py:45
  56.7 1.5 %fusion = bf16[2,20,32,512]{3,2,1,0:T(8,128)(2,1)S(1)} fusion(bf16[2,10,32,512]{3,2,1,0:T(8,128)(2,1)} %collective-permute-done.3, bf16[2,10,32,512]{3,2,1,0:T(8,128)(2,1)S(1)} %collective-permute-done.2, pred[]{:T(512)S(6)} %eq.11, pred[]{:T(512)S(6)} %gt.17), kind=kLoop, calls=%fused_computation.5 | loop fusion | flops 2621440 | bytes 2621442 | tf_op jit(solution)/shard_map/jit(_where)/select_n | solution.py:44
  58.2 2.2 %pad_maximum_fusion.x_ref = bf16[6,20,32,512]{3,2,1,0:T(8,128)(2,1)} fusion(bf16[2,20,32,512]{3,2,1,0:T(8,128)(2,1)S(1)} %fusion.1, bf16[2,2,32,512]{3,2,1,0:T(8,128)(2,1)S(1)} %broadcast_select_fusion, bf16[2,16,32,512]{3,2,1,0:T(8,128)(2,1)S(1)} %bitcast.12, bf16[2,2,32,512]{3,2,1,0:T(8,128)(2,1)S(1)} %broadcast_select_fusion.1, ...), kind=kLoop, calls=%fused_computation | loop fusion | flops 7864320 | bytes 7864320 | tf_op jit(solution)/shard_map/concatenate | solution.py:46
  60.4 13.7 %shard_map.37 = bf16[2,16,16,512]{3,2,1,0:T(8,128)(2,1)} custom-call(s32[72]{0:T(128)} %reshape.20.keep_ref, bf16[6,20,32,512]{3,2,1,0:T(8,128)(2,1)} %pad_maximum_fusion.x_ref, bf16[192,288]{1,0:T(8,128)(2,1)} %copy.11.w1_ref, bf16[48,576]{1,0:T(8,128)(2,1)} %reshape.19.w2_ref), custom_call_target="tpu_custom_call" | custom-call | tf_op jit(solution)/shard_map/pallas_call | solution.py:97
  74.1 2.1 %copy.12 = bf16[16,2,16,512]{3,2,1,0:T(8,128)(2,1)} copy(bf16[16,2,16,512]{3,0,2,1:T(8,128)(2,1)} %bitcast.13) | data formatting | bytes 1048576 | tf_op jit(solution)/shard_map/transpose | solution.py:146
  (19 shorter events, 0.2 us)
Async XLA Ops:
  1.8 19.9 %copy-start.1 = (bf16[3,3,3,16,32]{4,3,2,1,0:T(8,128)(2,1)S(1)}, bf16[3,3,3,16,32]{4,3,2,1,0:T(8,128)(2,1)}, u32[]{:S(2)}) copy-start(bf16[3,3,3,16,32]{4,3,2,1,0:T(8,128)(2,1)} %param.4) | copy-start | bytes 82948
  1.8 15.3 %collective-permute-start = (bf16[2,2,32,512]{3,2,1,0:T(8,128)(2,1)S(1)}, bf16[2,2,32,512]{3,2,1,0:T(8,128)(2,1)S(1)}, u32[]{:S(2)}, u32[]{:S(2)}) collective-permute-start(bf16[2,2,32,512]{3,2,1,0:T(8,128)(2,1)S(1)} %get-tuple-element.6), channel_id=1, source_target_pairs={{0,4},{4,8},{8,12},{12,16},{16,20},{20,24},{24,28},{28,32},{32,36}... | collective-permute-start | bytes 393224 | tf_op jit(solution)/shard_map/ppermute | solution.py:16
  5.7 45.0 %copy-start = (bf16[3,3,3,16,64]{4,3,2,1,0:T(8,128)(2,1)S(1)}, bf16[3,3,3,16,64]{4,3,2,1,0:T(8,128)(2,1)}, u32[]{:S(2)}) copy-start(bf16[3,3,3,16,64]{4,3,2,1,0:T(8,128)(2,1)} %param.5) | copy-start | bytes 165892
  5.7 11.5 %collective-permute-start.1 = (bf16[2,2,32,512]{3,2,1,0:T(8,128)(2,1)S(1)}, bf16[2,2,32,512]{3,2,1,0:T(8,128)(2,1)S(1)}, u32[]{:S(2)}, u32[]{:S(2)}) collective-permute-start(bf16[2,2,32,512]{3,2,1,0:T(8,128)(2,1)S(1)} %get-tuple-element.5), channel_id=1, source_target_pairs={{0,252},{4,0},{8,4},{12,8},{16,12},{20,16},{24,20},{28,24},{32,28}... | collective-permute-start | bytes 393224 | tf_op jit(solution)/shard_map/ppermute | solution.py:16
  17.5 29.2 %collective-permute-start.4 = (bf16[2,10,32,512]{3,2,1,0:T(8,128)(2,1)S(1)}, bf16[2,10,32,512]{3,2,1,0:T(8,128)(2,1)}, u32[]{:S(2)}, u32[]{:S(2)}) collective-permute-start(bf16[2,10,32,512]{3,2,1,0:T(8,128)(2,1)S(1)} %fusion.3), channel_id=1, source_target_pairs={{0,224},{4,228},{8,232},{12,236},{16,240},{20,244},{24,248},{28,25... | collective-permute-start | bytes 1966088 | tf_op jit(solution)/shard_map/ppermute | solution.py:16
  21.7 28.7 %collective-permute-start.2 = (bf16[2,10,32,512]{3,2,1,0:T(8,128)(2,1)S(1)}, bf16[2,10,32,512]{3,2,1,0:T(8,128)(2,1)S(1)}, u32[]{:S(2)}, u32[]{:S(2)}) collective-permute-start(bf16[2,10,32,512]{3,2,1,0:T(8,128)(2,1)S(1)} %fusion.3), channel_id=1, source_target_pairs={{0,32},{4,36},{8,40},{12,44},{16,48},{20,52},{24,56},{28,60},{32,6... | collective-permute-start | bytes 1966088 | tf_op jit(solution)/shard_map/ppermute | solution.py:16
  21.7 30.7 %collective-permute-start.8 = (bf16[3,3,3,16,32]{4,3,2,1,0:T(8,128)(2,1)S(1)}, bf16[3,3,3,16,32]{4,3,2,1,0:T(8,128)(2,1)S(1)}, u32[]{:S(2)}, u32[]{:S(2)}) collective-permute-start(bf16[3,3,3,16,32]{4,3,2,1,0:T(8,128)(2,1)S(1)} %copy-done.1), channel_id=1, source_target_pairs={{0,1},{1,2},{2,3},{3,0},{4,5},{5,6},{6,7},{7,4},{8,9},{9,10},{10,1... | collective-permute-start | bytes 82952 | tf_op jit(solution)/shard_map/ppermute | solution.py:16
  25.2 27.2 %collective-permute-start.7 = (bf16[3,3,3,16,32]{4,3,2,1,0:T(8,128)(2,1)S(1)}, bf16[3,3,3,16,32]{4,3,2,1,0:T(8,128)(2,1)S(1)}, u32[]{:S(2)}, u32[]{:S(2)}) collective-permute-start(bf16[3,3,3,16,32]{4,3,2,1,0:T(8,128)(2,1)S(1)} %copy-done.1), channel_id=1, source_target_pairs={{0,2},{1,3},{2,0},{3,1},{4,6},{5,7},{6,4},{7,5},{8,10},{9,11},{10,... | collective-permute-start | bytes 82952 | tf_op jit(solution)/shard_map/ppermute | solution.py:16
  25.3 27.1 %collective-permute-start.6 = (bf16[3,3,3,16,32]{4,3,2,1,0:T(8,128)(2,1)S(1)}, bf16[3,3,3,16,32]{4,3,2,1,0:T(8,128)(2,1)}, u32[]{:S(2)}, u32[]{:S(2)}) collective-permute-start(bf16[3,3,3,16,32]{4,3,2,1,0:T(8,128)(2,1)S(1)} %copy-done.1), channel_id=1, source_target_pairs={{0,3},{1,0},{2,1},{3,2},{4,7},{5,4},{6,5},{7,6},{8,11},{9,8},{10,9... | collective-permute-start | bytes 82952 | tf_op jit(solution)/shard_map/ppermute | solution.py:16
  46.7 8.1 %collective-permute-start.5 = (bf16[2,10,32,512]{3,2,1,0:T(8,128)(2,1)}, bf16[2,10,32,512]{3,2,1,0:T(8,128)(2,1)}, u32[]{:S(2)}, u32[]{:S(2)}) collective-permute-start(bf16[2,10,32,512]{3,2,1,0:T(8,128)(2,1)} %collective-permute-done.4), channel_id=1, source_target_pairs={{0,1},{1,0},{2,3},{3,2},{4,5},{5,4},{6,7},{7,6},{8,9},{9,8},{10,11... | collective-permute-start | bytes 1966088 | tf_op jit(solution)/shard_map/ppermute | solution.py:31
  50.4 6.3 %collective-permute-start.3 = (bf16[2,10,32,512]{3,2,1,0:T(8,128)(2,1)S(1)}, bf16[2,10,32,512]{3,2,1,0:T(8,128)(2,1)}, u32[]{:S(2)}, u32[]{:S(2)}) collective-permute-start(bf16[2,10,32,512]{3,2,1,0:T(8,128)(2,1)S(1)} %collective-permute-done.2), channel_id=1, source_target_pairs={{0,1},{1,0},{2,3},{3,2},{4,5},{5,4},{6,7},{7,6},{8,9},{9,8},{10,11... | collective-permute-start | bytes 1966088 | tf_op jit(solution)/shard_map/ppermute | solution.py:31

commit v6 on v5

--- a/solution.py
+++ b/solution.py
@@ -1,11 +1,10 @@
-import functools
-
 import jax
 import jax.numpy as jnp
 from jax import lax
 from jax.experimental import pallas as pl
 from jax.experimental.pallas import tpu as pltpu
 from jax.sharding import PartitionSpec as P
+
 
 GH = 8
 
@@ -34,16 +33,16 @@
 
 def wide_border(volume_tile, rim):
     tile_row, depth_tile, grid_depth = tile_place()
-    above_rim = passed_along(volume_tile[:, -rim:], "space", 1)
-    below_rim = passed_along(volume_tile[:, :rim], "space", -1)
-    above_rim = jnp.where(tile_row > 0, above_rim, jnp.zeros_like(above_rim))
-    below_rim = jnp.where(tile_row < GH - 1, below_rim, jnp.zeros_like(below_rim))
-    taller = jnp.concatenate([above_rim, volume_tile, below_rim], 1)
-    front_rim = shared_along(taller[-rim:], GH)
-    back_rim = shared_along(taller[:rim], -GH)
-    front_rim = jnp.where(depth_tile > 0, front_rim, jnp.zeros_like(front_rim))
-    back_rim = jnp.where(depth_tile < grid_depth - 1, back_rim, jnp.zeros_like(back_rim))
-    return jnp.concatenate([front_rim, taller, back_rim], 0)
+
+    def kept(value, flag):
+        return jnp.where(flag, value, jnp.zeros_like(value))
+
+    above = kept(passed_along(volume_tile[:, -rim:], "space", 1), tile_row > 0)
+    below = kept(passed_along(volume_tile[:, :rim], "space", -1), tile_row < GH - 1)
+    taller = jnp.concatenate([above, volume_tile, below], 1)
+    front = kept(shared_along(taller, GH), depth_tile > 0)
+    back = kept(shared_along(taller, -GH), depth_tile < grid_depth - 1)
+    return jnp.concatenate([front, taller, back], 0)
 
 
 def width_taps(acc, out_count):
@@ -138,9 +137,9 @@
 
 
 def local(voxels, first_filters, second_filters):
-    all_first, second_filters = gathered_filters(first_filters, second_filters)
     tile = voxels.transpose(1, 2, 0, 3)
     padded = wide_border(tile, 2)
+    all_first, second_filters = gathered_filters(first_filters, second_filters)
     keep = inside_flags(padded.shape[0] - 2, padded.shape[1] - 2)
     out = two_layers(keep, padded, tap_matrices(all_first), tap_matrices(second_filters))
     return out.transpose(2, 0, 1, 3)

time: 77.3 us -> 77.3 us (level)
  no operation moved by 1% of the time
where the time goes in v6:
time: 77.3 us; the launch traced here: 76.2 us
  waiting for transfers between devices  24.8 us (32%)
  starting transfers between devices  23.7 us (31%)
  Pallas kernels  13.7 us (18%)
  other arithmetic  7.14 us (9%)
  local copies, waits for them, and re-layouts  6.73 us (9%)
    ppermute x7, waiting for transfers between devices, passed_along(): return lax.ppermute(value, axis, pairs)  24.8 us
    ppermute x7, starting transfers between devices, passed_along(): return lax.ppermute(value, axis, pairs)  19.8 us
    pallas_call x1, Pallas kernels, two_layers(): pl.pallas_call(two_layers_kernel, out_shape=jax.ShapeDtypeStruct((in_dept...  13.7 us
    ppermute x2, starting transfers between devices, shared_along(): lax.ppermute(mine, 'chan', [(source, source ^ 1) for source in range(coun...  3.97 us
    select_n x4, other arithmetic, kept(): return jnp.where(flag, value, jnp.zeros_like(value))  3.48 us
    concatenate x1, other arithmetic, wide_border(): return jnp.concatenate([front, taller, back], 0)  2.16 us
    transpose x1, local copies, waits for them, and re-layouts, local(): return out.transpose(2, 0, 1, 3)  2.13 us
    unnamed x5, local copies, waits for them, and re-layouts  1.81 us
  transfers between devices with their start and end apart: 9, of which 2 were waited for; matrix products, arithmetic and copies ran while one was open for 8% of the time, Pallas kernels for 0%

profile of v6, /device:TPU:1, one launch (start us, length us, event | category | flops | bytes accessed | tf_op | source)
XLA Modules:
  0.0 76.2 jit_solution(14088051291297507482)
XLA Ops:
  0.0 1.8 %copy.14 = bf16[32,2,16,512]{3,0,2,1:T(8,128)(2,1)S(1)} copy(bf16[32,2,16,512]{3,2,1,0:T(8,128)(2,1)} %param.3) | data formatting | bytes 2097152 | tf_op args[0]
  1.8 3.9 %collective-permute-start = (bf16[2,2,32,512]{3,2,1,0:T(8,128)(2,1)S(1)}, bf16[2,2,32,512]{3,2,1,0:T(8,128)(2,1)S(1)}, u32[]{:S(2)}, u32[]{:S(2)}) collective-permute-start(bf16[2,2,32,512]{3,2,1,0:T(8,128)(2,1)S(1)} %get-tuple-element.6), channel_id=1, source_target_pairs={{0,4},{4,8},{8,12},{12,16},{16,20},{20,24},{24,28},{28,32},{32,36}... | collective-permute-start | bytes 393224 | tf_op jit(solution)/shard_map/ppermute | solution.py:15
  5.7 7.8 %collective-permute-start.1 = (bf16[2,2,32,512]{3,2,1,0:T(8,128)(2,1)S(1)}, bf16[2,2,32,512]{3,2,1,0:T(8,128)(2,1)S(1)}, u32[]{:S(2)}, u32[]{:S(2)}) collective-permute-start(bf16[2,2,32,512]{3,2,1,0:T(8,128)(2,1)S(1)} %get-tuple-element.5), channel_id=1, source_target_pairs={{0,252},{4,0},{8,4},{12,8},{16,12},{20,16},{24,20},{28,24},{32,28}... | collective-permute-start | bytes 393224 | tf_op jit(solution)/shard_map/ppermute | solution.py:15
  13.5 3.7 %collective-permute-done = bf16[2,2,32,512]{3,2,1,0:T(8,128)(2,1)S(1)} collective-permute-done((bf16[2,2,32,512]{3,2,1,0:T(8,128)(2,1)S(1)}, bf16[2,2,32,512]{3,2,1,0:T(8,128)(2,1)S(1)}, u32[]{:S(2)}, u32[]{:S(2)}) %collective-permute-start) | collective-permute-done | bytes 131104 | tf_op jit(solution)/shard_map/ppermute | solution.py:15
  17.2 0.2 fusion.3
  17.5 4.2 %collective-permute-start.4 = (bf16[2,10,32,512]{3,2,1,0:T(8,128)(2,1)S(1)}, bf16[2,10,32,512]{3,2,1,0:T(8,128)(2,1)}, u32[]{:S(2)}, u32[]{:S(2)}) collective-permute-start(bf16[2,10,32,512]{3,2,1,0:T(8,128)(2,1)S(1)} %fusion.3), channel_id=1, source_target_pairs={{0,224},{4,228},{8,232},{12,236},{16,240},{20,244},{24,248},{28,25... | collective-permute-start | bytes 1966088 | tf_op jit(solution)/shard_map/ppermute | solution.py:15
  21.7 3.5 %collective-permute-start.8 = (bf16[3,3,3,16,32]{4,3,2,1,0:T(8,128)(2,1)S(1)}, bf16[3,3,3,16,32]{4,3,2,1,0:T(8,128)(2,1)S(1)}, u32[]{:S(2)}, u32[]{:S(2)}) collective-permute-start(bf16[3,3,3,16,32]{4,3,2,1,0:T(8,128)(2,1)S(1)} %copy-done.1), channel_id=1, source_target_pairs={{0,1},{1,2},{2,3},{3,0},{4,5},{5,6},{6,7},{7,4},{8,9},{9,10},{10,1... | collective-permute-start | bytes 82952 | tf_op jit(solution)/shard_map/ppermute | solution.py:15
  25.2 0.1 collective-permute-start.7
  25.3 0.3 collective-permute-start.6
  25.6 21.1 %collective-permute-done.4 = bf16[2,10,32,512]{3,2,1,0:T(8,128)(2,1)} collective-permute-done((bf16[2,10,32,512]{3,2,1,0:T(8,128)(2,1)S(1)}, bf16[2,10,32,512]{3,2,1,0:T(8,128)(2,1)}, u32[]{:S(2)}, u32[]{:S(2)}) %collective-permute-start.4) | collective-permute-done | bytes 655392 | tf_op jit(solution)/shard_map/ppermute | solution.py:15
  46.7 3.7 %collective-permute-start.5 = (bf16[2,10,32,512]{3,2,1,0:T(8,128)(2,1)}, bf16[2,10,32,512]{3,2,1,0:T(8,128)(2,1)}, u32[]{:S(2)}, u32[]{:S(2)}) collective-permute-start(bf16[2,10,32,512]{3,2,1,0:T(8,128)(2,1)} %collective-permute-done.4), channel_id=1, source_target_pairs={{0,1},{1,0},{2,3},{3,2},{4,5},{5,4},{6,7},{7,6},{8,9},{9,8},{10,11... | collective-permute-start | bytes 1966088 | tf_op jit(solution)/shard_map/ppermute | solution.py:30
  50.4 0.3 collective-permute-start.3
  50.8 0.2 fusion.4
  50.9 0.7 reshape.20.keep_ref
  51.6 0.8 %reshape.19.w2_ref = bf16[48,576]{1,0:T(8,128)(2,1)} reshape(bf16[3,16,3,3,64]{4,3,2,1,0:T(4,128)(2,1)S(1)} %copy.10) | data formatting | bytes 110592 | tf_op jit(solution)/shard_map/reshape | solution.py:112
  52.4 1.0 %maximum_bitcast_fusion = bf16[3,64,3,3,32]{4,1,0,3,2:T(8,128)(2,1)S(1)} fusion(bf16[3,3,3,16,32]{4,3,2,1,0:T(8,128)(2,1)S(1)} %collective-permute-done.8, bf16[3,3,3,16,32]{4,3,2,1,0:T(8,128)(2,1)S(1)} %collective-permute-done.7, bf16[3,3,3,16,32]{4,3,2,1,0:T(8,128)(2,1)} %collective-permute-done.6, bf16[3,3,3,16,32]{4,3,2,1,0:T(8,128)(2,1)S(1)} %copy-done.1), kind=kLoop, calls=%fused_computation.11 | loop fusion | flops 442368 | bytes 221184 | tf_op jit(solution)/shard_map/transpose | solution.py:112
  53.5 0.3 copy.9
  53.7 0.2 reshape.18
  53.9 0.8 %copy.11.w1_ref = bf16[192,288]{1,0:T(8,128)(2,1)} copy(bf16[192,288]{0,1:T(8,128)(2,1)S(1)} %reshape.18) | data formatting | bytes 221184 | tf_op jit(solution)/shard_map/reshape | solution.py:112
  54.7 1.9 %fusion.1 = bf16[2,20,32,512]{3,2,1,0:T(8,128)(2,1)S(1)} fusion(bf16[2,10,32,512]{3,2,1,0:T(8,128)(2,1)} %collective-permute-done.5, bf16[2,10,32,512]{3,2,1,0:T(8,128)(2,1)} %collective-permute-done.4, pred[]{:T(512)S(6)} %lt.52, pred[]{:T(512)S(6)} %eq.11), kind=kLoop, calls=%fused_computation.7 | loop fusion | flops 2621440 | bytes 2621442 | tf_op jit(solution)/shard_map/jit(_where)/select_n | solution.py:38
  56.7 1.5 %fusion = bf16[2,20,32,512]{3,2,1,0:T(8,128)(2,1)S(1)} fusion(bf16[2,10,32,512]{3,2,1,0:T(8,128)(2,1)} %collective-permute-done.3, bf16[2,10,32,512]{3,2,1,0:T(8,128)(2,1)S(1)} %collective-permute-done.2, pred[]{:T(512)S(6)} %eq.11, pred[]{:T(512)S(6)} %gt.17), kind=kLoop, calls=%fused_computation.5 | loop fusion | flops 2621440 | bytes 2621442 | tf_op jit(solution)/shard_map/jit(_where)/select_n | solution.py:38
  58.2 2.2 %pad_maximum_fusion.x_ref = bf16[6,20,32,512]{3,2,1,0:T(8,128)(2,1)} fusion(bf16[2,20,32,512]{3,2,1,0:T(8,128)(2,1)S(1)} %fusion.1, bf16[2,2,32,512]{3,2,1,0:T(8,128)(2,1)S(1)} %broadcast_select_fusion, bf16[2,16,32,512]{3,2,1,0:T(8,128)(2,1)S(1)} %bitcast.12, bf16[2,2,32,512]{3,2,1,0:T(8,128)(2,1)S(1)} %broadcast_select_fusion.1, ...), kind=kLoop, calls=%fused_computation | loop fusion | flops 7864320 | bytes 7864320 | tf_op jit(solution)/shard_map/concatenate | solution.py:45
  60.4 13.7 %shard_map.37 = bf16[2,16,16,512]{3,2,1,0:T(8,128)(2,1)} custom-call(s32[72]{0:T(128)} %reshape.20.keep_ref, bf16[6,20,32,512]{3,2,1,0:T(8,128)(2,1)} %pad_maximum_fusion.x_ref, bf16[192,288]{1,0:T(8,128)(2,1)} %copy.11.w1_ref, bf16[48,576]{1,0:T(8,128)(2,1)} %reshape.19.w2_ref), custom_call_target="tpu_custom_call" | custom-call | tf_op jit(solution)/shard_map/pallas_call | solution.py:96
  74.1 2.1 %copy.12 = bf16[16,2,16,512]{3,2,1,0:T(8,128)(2,1)} copy(bf16[16,2,16,512]{3,0,2,1:T(8,128)(2,1)} %bitcast.13) | data formatting | bytes 1048576 | tf_op jit(solution)/shard_map/transpose | solution.py:145
  (19 shorter events, 0.2 us)
Async XLA Ops:
  1.8 19.9 %copy-start.1 = (bf16[3,3,3,16,32]{4,3,2,1,0:T(8,128)(2,1)S(1)}, bf16[3,3,3,16,32]{4,3,2,1,0:T(8,128)(2,1)}, u32[]{:S(2)}) copy-start(bf16[3,3,3,16,32]{4,3,2,1,0:T(8,128)(2,1)} %param.4) | copy-start | bytes 82948
  1.8 15.3 %collective-permute-start = (bf16[2,2,32,512]{3,2,1,0:T(8,128)(2,1)S(1)}, bf16[2,2,32,512]{3,2,1,0:T(8,128)(2,1)S(1)}, u32[]{:S(2)}, u32[]{:S(2)}) collective-permute-start(bf16[2,2,32,512]{3,2,1,0:T(8,128)(2,1)S(1)} %get-tuple-element.6), channel_id=1, source_target_pairs={{0,4},{4,8},{8,12},{12,16},{16,20},{20,24},{24,28},{28,32},{32,36}... | collective-permute-start | bytes 393224 | tf_op jit(solution)/shard_map/ppermute | solution.py:15
  5.7 45.0 %copy-start = (bf16[3,3,3,16,64]{4,3,2,1,0:T(8,128)(2,1)S(1)}, bf16[3,3,3,16,64]{4,3,2,1,0:T(8,128)(2,1)}, u32[]{:S(2)}) copy-start(bf16[3,3,3,16,64]{4,3,2,1,0:T(8,128)(2,1)} %param.5) | copy-start | bytes 165892
  5.7 11.5 %collective-permute-start.1 = (bf16[2,2,32,512]{3,2,1,0:T(8,128)(2,1)S(1)}, bf16[2,2,32,512]{3,2,1,0:T(8,128)(2,1)S(1)}, u32[]{:S(2)}, u32[]{:S(2)}) collective-permute-start(bf16[2,2,32,512]{3,2,1,0:T(8,128)(2,1)S(1)} %get-tuple-element.5), channel_id=1, source_target_pairs={{0,252},{4,0},{8,4},{12,8},{16,12},{20,16},{24,20},{28,24},{32,28}... | collective-permute-start | bytes 393224 | tf_op jit(solution)/shard_map/ppermute | solution.py:15
  17.5 29.2 %collective-permute-start.4 = (bf16[2,10,32,512]{3,2,1,0:T(8,128)(2,1)S(1)}, bf16[2,10,32,512]{3,2,1,0:T(8,128)(2,1)}, u32[]{:S(2)}, u32[]{:S(2)}) collective-permute-start(bf16[2,10,32,512]{3,2,1,0:T(8,128)(2,1)S(1)} %fusion.3), channel_id=1, source_target_pairs={{0,224},{4,228},{8,232},{12,236},{16,240},{20,244},{24,248},{28,25... | collective-permute-start | bytes 1966088 | tf_op jit(solution)/shard_map/ppermute | solution.py:15
  21.7 28.7 %collective-permute-start.2 = (bf16[2,10,32,512]{3,2,1,0:T(8,128)(2,1)S(1)}, bf16[2,10,32,512]{3,2,1,0:T(8,128)(2,1)S(1)}, u32[]{:S(2)}, u32[]{:S(2)}) collective-permute-start(bf16[2,10,32,512]{3,2,1,0:T(8,128)(2,1)S(1)} %fusion.3), channel_id=1, source_target_pairs={{0,32},{4,36},{8,40},{12,44},{16,48},{20,52},{24,56},{28,60},{32,6... | collective-permute-start | bytes 1966088 | tf_op jit(solution)/shard_map/ppermute | solution.py:15
  21.7 30.7 %collective-permute-start.8 = (bf16[3,3,3,16,32]{4,3,2,1,0:T(8,128)(2,1)S(1)}, bf16[3,3,3,16,32]{4,3,2,1,0:T(8,128)(2,1)S(1)}, u32[]{:S(2)}, u32[]{:S(2)}) collective-permute-start(bf16[3,3,3,16,32]{4,3,2,1,0:T(8,128)(2,1)S(1)} %copy-done.1), channel_id=1, source_target_pairs={{0,1},{1,2},{2,3},{3,0},{4,5},{5,6},{6,7},{7,4},{8,9},{9,10},{10,1... | collective-permute-start | bytes 82952 | tf_op jit(solution)/shard_map/ppermute | solution.py:15
  25.2 27.2 %collective-permute-start.7 = (bf16[3,3,3,16,32]{4,3,2,1,0:T(8,128)(2,1)S(1)}, bf16[3,3,3,16,32]{4,3,2,1,0:T(8,128)(2,1)S(1)}, u32[]{:S(2)}, u32[]{:S(2)}) collective-permute-start(bf16[3,3,3,16,32]{4,3,2,1,0:T(8,128)(2,1)S(1)} %copy-done.1), channel_id=1, source_target_pairs={{0,2},{1,3},{2,0},{3,1},{4,6},{5,7},{6,4},{7,5},{8,10},{9,11},{10,... | collective-permute-start | bytes 82952 | tf_op jit(solution)/shard_map/ppermute | solution.py:15
  25.3 27.1 %collective-permute-start.6 = (bf16[3,3,3,16,32]{4,3,2,1,0:T(8,128)(2,1)S(1)}, bf16[3,3,3,16,32]{4,3,2,1,0:T(8,128)(2,1)}, u32[]{:S(2)}, u32[]{:S(2)}) collective-permute-start(bf16[3,3,3,16,32]{4,3,2,1,0:T(8,128)(2,1)S(1)} %copy-done.1), channel_id=1, source_target_pairs={{0,3},{1,0},{2,1},{3,2},{4,7},{5,4},{6,5},{7,6},{8,11},{9,8},{10,9... | collective-permute-start | bytes 82952 | tf_op jit(solution)/shard_map/ppermute | solution.py:15
  46.7 8.1 %collective-permute-start.5 = (bf16[2,10,32,512]{3,2,1,0:T(8,128)(2,1)}, bf16[2,10,32,512]{3,2,1,0:T(8,128)(2,1)}, u32[]{:S(2)}, u32[]{:S(2)}) collective-permute-start(bf16[2,10,32,512]{3,2,1,0:T(8,128)(2,1)} %collective-permute-done.4), channel_id=1, source_target_pairs={{0,1},{1,0},{2,3},{3,2},{4,5},{5,4},{6,7},{7,6},{8,9},{9,8},{10,11... | collective-permute-start | bytes 1966088 | tf_op jit(solution)/shard_map/ppermute | solution.py:30
  50.4 6.3 %collective-permute-start.3 = (bf16[2,10,32,512]{3,2,1,0:T(8,128)(2,1)S(1)}, bf16[2,10,32,512]{3,2,1,0:T(8,128)(2,1)}, u32[]{:S(2)}, u32[]{:S(2)}) collective-permute-start(bf16[2,10,32,512]{3,2,1,0:T(8,128)(2,1)S(1)} %collective-permute-done.2), channel_id=1, source_target_pairs={{0,1},{1,0},{2,3},{3,2},{4,5},{5,4},{6,7},{7,6},{8,9},{9,8},{10,11... | collective-permute-start | bytes 1966088 | tf_op jit(solution)/shard_map/ppermute | solution.py:30

commit v7 on v6

--- a/solution.py
+++ b/solution.py
@@ -28,21 +28,27 @@
     mine = passed_along(mine, "space", steps)
     count = lax.axis_size("chan")
     theirs = lax.ppermute(mine, "chan", [(source, source ^ 1) for source in range(count)])
-    return jnp.where(core == 0, jnp.concatenate([mine, theirs], 1), jnp.concatenate([theirs, mine], 1))
+    return mine, theirs
 
 
-def wide_border(volume_tile, rim):
+def halo_pieces(volume_tile, rim):
     tile_row, depth_tile, grid_depth = tile_place()
-
-    def kept(value, flag):
-        return jnp.where(flag, value, jnp.zeros_like(value))
-
-    above = kept(passed_along(volume_tile[:, -rim:], "space", 1), tile_row > 0)
-    below = kept(passed_along(volume_tile[:, :rim], "space", -1), tile_row < GH - 1)
-    taller = jnp.concatenate([above, volume_tile, below], 1)
-    front = kept(shared_along(taller, GH), depth_tile > 0)
-    back = kept(shared_along(taller, -GH), depth_tile < grid_depth - 1)
-    return jnp.concatenate([front, taller, back], 0)
+    top = volume_tile[:, -rim:]
+    bottom = volume_tile[:, :rim]
+    front = shared_along(volume_tile, GH)
+    back = shared_along(volume_tile, -GH)
+    above = passed_along(top, "space", 1)
+    below = passed_along(bottom, "space", -1)
+    front_above = passed_along(top, "space", GH + 1)
+    front_below = passed_along(bottom, "space", GH - 1)
+    back_above = passed_along(top, "space", 1 - GH)
+    back_below = passed_along(bottom, "space", -1 - GH)
+    place = jnp.stack([
+        tile_row > 0, tile_row < GH - 1, depth_tile > 0, depth_tile < grid_depth - 1,
+    ]).astype(jnp.int32)
+    place = jnp.concatenate([place, (lax.axis_index("chan") % 2).astype(jnp.int32)[None]])
+    pieces = (volume_tile, above, below) + front + back + (front_above, front_below, back_above, back_below)
+    return place, pieces
 
 
 def width_taps(acc, out_count):
@@ -64,7 +70,36 @@
     return width_taps(acc, out_count)
 
 
-def two_layers_kernel(keep_ref, x_ref, w1_ref, w2_ref, o_ref, hid_ref):
+def assemble(place_ref, own_ref, above_ref, below_ref, front_refs, back_refs, corner_refs, x_ref):
+    has_above, has_below = place_ref[0] > 0, place_ref[1] > 0
+    has_front, has_back = place_ref[2] > 0, place_ref[3] > 0
+    core = place_ref[4]
+    depth, height = own_ref.shape[0], own_ref.shape[1]
+    half = height // 2
+
+    def put(rows, cols, value, flag):
+        x_ref[rows, cols] = jnp.where(flag, value, jnp.zeros_like(value))
+
+    put(slice(2, 2 + depth), slice(2, 2 + height), own_ref[...], True)
+    put(slice(2, 2 + depth), slice(0, 2), above_ref[...], has_above)
+    put(slice(2, 2 + depth), slice(2 + height, 4 + height), below_ref[...], has_below)
+    for (mine_ref, theirs_ref), rows, flag in (
+        (front_refs, slice(0, 2), has_front),
+        (back_refs, slice(2 + depth, 4 + depth), has_back),
+    ):
+        put(rows, pl.ds(2 + core * half, half), mine_ref[...], flag)
+        put(rows, pl.ds(2 + (1 - core) * half, half), theirs_ref[...], flag)
+    fa_ref, fb_ref, ba_ref, bb_ref = corner_refs
+    put(slice(0, 2), slice(0, 2), fa_ref[...], has_front & has_above)
+    put(slice(0, 2), slice(2 + height, 4 + height), fb_ref[...], has_front & has_below)
+    put(slice(2 + depth, 4 + depth), slice(0, 2), ba_ref[...], has_back & has_above)
+    put(slice(2 + depth, 4 + depth), slice(2 + height, 4 + height), bb_ref[...], has_back & has_below)
+
+
+def two_layers_kernel(keep_ref, place_ref, own_ref, above_ref, below_ref, fm_ref, ft_ref, bm_ref, bt_ref,
+                      fa_ref, fb_ref, ba_ref, bb_ref, w1_ref, w2_ref, o_ref, x_ref, hid_ref):
+    assemble(place_ref, own_ref, above_ref, below_ref, (fm_ref, ft_ref), (bm_ref, bt_ref),
+             (fa_ref, fb_ref, ba_ref, bb_ref), x_ref)
     mid_count = w1_ref.shape[0] // 3
     out_count = w2_ref.shape[0] // 3
     hid_depth, hid_height = hid_ref.shape[0], hid_ref.shape[1]
@@ -88,23 +123,23 @@
         lax.fori_loop(0, out_height, second, 0, unroll=True)
 
 
-def two_layers(keep, padded, w1, w2):
-    in_depth, in_height, _, width = padded.shape
+def two_layers(keep, place, pieces, w1, w2):
+    own = pieces[0]
+    depth, height, in_count, width = own.shape
     mid_count = w1.shape[0] // 3
     out_count = w2.shape[0] // 3
     vmem = pltpu.MemorySpace.VMEM
+    smem = pl.BlockSpec(memory_space=pltpu.SMEM)
     return pl.pallas_call(
         two_layers_kernel,
-        out_shape=jax.ShapeDtypeStruct((in_depth - 4, in_height - 4, out_count, width), jnp.bfloat16),
-        in_specs=[
-            pl.BlockSpec(memory_space=pltpu.SMEM),
-            pl.BlockSpec(memory_space=vmem),
-            pl.BlockSpec(memory_space=vmem),
-            pl.BlockSpec(memory_space=vmem),
+        out_shape=jax.ShapeDtypeStruct((depth, height, out_count, width), jnp.bfloat16),
+        in_specs=[smem, smem] + [pl.BlockSpec(memory_space=vmem)] * (len(pieces) + 2),
+        out_specs=pl.BlockSpec(memory_space=vmem),
+        scratch_shapes=[
+            pltpu.VMEM((depth + 4, height + 4, in_count, width), jnp.bfloat16),
+            pltpu.VMEM((depth + 2, height + 2, mid_count, width), jnp.bfloat16),
         ],
-        out_specs=pl.BlockSpec(memory_space=vmem),
-        scratch_shapes=[pltpu.VMEM((in_depth - 2, in_height - 2, mid_count, width), jnp.bfloat16)],
-    )(keep, padded, w1, w2)
+    )(keep, place, *pieces, w1, w2)
 
 
 def tap_matrices(filters):
@@ -126,11 +161,12 @@
 def gathered_filters(first_filters, second_filters):
     count = lax.axis_size("chan")
     own = lax.axis_index("chan")
-    pieces = [first_filters]
+    a, b, e, block, c = first_filters.shape
+    own_block = first_filters.transpose(2, 3, 0, 1, 4).reshape(e, block, a * b * c)
+    pieces = [own_block]
     for steps in range(1, count):
-        pieces.append(passed_along(first_filters, "chan", -steps))
-    all_first = jnp.concatenate(pieces, 3)
-    block = first_filters.shape[3]
+        pieces.append(passed_along(own_block, "chan", -steps))
+    all_first = jnp.concatenate(pieces, 1).reshape(e * block * count, a * b * c)
     doubled = jnp.concatenate([second_filters, second_filters], 4)
     all_second = lax.dynamic_slice_in_dim(doubled, own * block, second_filters.shape[4], 4)
     return all_first, all_second
@@ -138,10 +174,10 @@
 
 def local(voxels, first_filters, second_filters):
     tile = voxels.transpose(1, 2, 0, 3)
-    padded = wide_border(tile, 2)
+    place, pieces = halo_pieces(tile, 2)
     all_first, second_filters = gathered_filters(first_filters, second_filters)
-    keep = inside_flags(padded.shape[0] - 2, padded.shape[1] - 2)
-    out = two_layers(keep, padded, tap_matrices(all_first), tap_matrices(second_filters))
+    keep = inside_flags(tile.shape[0] + 2, tile.shape[1] + 2)
+    out = two_layers(keep, place, pieces, all_first, tap_matrices(second_filters))
     return out.transpose(2, 0, 1, 3)
 
 

time: 77.3 us -> 93.5 us (1.21)
  starting transfers between devices: 23.7 us -> 37.8 us
  waiting for transfers between devices: 24.8 us -> 31.5 us
  other arithmetic: 7.14 us -> 1.58 us
  local copies, waits for them, and re-layouts: 6.73 us -> 8.26 us
    ppermute x7 -> x11, starting transfers between devices: 19.8 us -> 36.4 us  [passed_along(): return lax.ppermute(value, axis, pairs)]
    ppermute x7 -> x11, waiting for transfers between devices: 24.8 us -> 31.5 us  [passed_along(): return lax.ppermute(value, axis, pairs)]
    select_n x4 -> x0, other arithmetic: 3.48 us -> none  [kept(): return jnp.where(flag, value, jnp.zeros_like(value))]
    ppermute x2, starting transfers between devices: 3.97 us -> 1.35 us  [shared_along(): lax.ppermute(mine, 'chan', [(source, source ^ 1) for source in range(coun...]
    concatenate x2, other arithmetic: 2.4 us -> 1.25 us  [the longest x1 0.67 us: gathered_filters(): all_first = jnp.concatenate(pieces, 1).reshape(e * block * count, a * b * c)]
    reshape x3 -> x1, local copies, waits for them, and re-layouts: 1.77 us -> 0.76 us  [tap_matrices(): return filters.transpose(2, 3, 0, 1, 4).reshape(e * o, a * b * c)]
    transpose x2 -> x1, other arithmetic: 1.17 us -> 0.17 us  [tap_matrices(): return filters.transpose(2, 3, 0, 1, 4).reshape(e * o, a * b * c)]
    unnamed x5 -> x27, local copies, waits for them, and re-layouts: 1.81 us -> 2.8 us
  transfers between devices with their start and end apart: 9 -> 13, of which waited for: 2 -> 3; matrix products, arithmetic and copies ran while one was open for 8% -> 6% of each run, Pallas kernels for 0% -> 0%
where the time goes in v7:
time: 93.5 us; the launch traced here: 93.3 us
  starting transfers between devices  37.8 us (40%)
  waiting for transfers between devices  31.5 us (34%)
  Pallas kernels  14 us (15%)
  local copies, waits for them, and re-layouts  8.26 us (9%)
  other arithmetic  1.58 us (2%)
    ppermute x11, starting transfers between devices, passed_along(): return lax.ppermute(value, axis, pairs)  36.4 us
    ppermute x11, waiting for transfers between devices, passed_along(): return lax.ppermute(value, axis, pairs)  31.5 us
    pallas_call x1, Pallas kernels, two_layers(): pl.pallas_call(two_layers_kernel, out_shape=jax.ShapeDtypeStruct((depth,...  14 us
    unnamed x27, local copies, waits for them, and re-layouts  2.8 us
    transpose x1, local copies, waits for them, and re-layouts, local(): return out.transpose(2, 0, 1, 3)  2.13 us
  transfers between devices with their start and end apart: 13, of which 3 were waited for; matrix products, arithmetic and copies ran while one was open for 6% of the time, Pallas kernels for 0%

profile of v7, /device:TPU:1, one launch (start us, length us, event | category | flops | bytes accessed | tf_op | source)
XLA Modules:
  0.0 93.3 jit_solution(629882585435398229)
XLA Ops:
  0.0 1.0 %copy.10 = bf16[3,16,3,3,32]{4,3,2,1,0:T(4,128)(2,1)S(1)} copy(bf16[3,16,3,3,32]{4,1,0,3,2:T(8,128)(2,1)} %bitcast.18) | data formatting | bytes 55296 | tf_op jit(solution)/shard_map/transpose | solution.py:165
  1.1 3.1 %collective-permute-start.12 = (bf16[3,16,288]{2,1,0:T(8,128)(2,1)S(1)}, bf16[3,16,288]{2,1,0:T(8,128)(2,1)S(1)}, u32[]{:S(2)}, u32[]{:S(2)}) collective-permute-start(bf16[3,16,288]{2,1,0:T(8,128)(2,1)S(1)} %reshape.21), channel_id=1, source_target_pairs={{0,1},{1,2},{2,3},{3,0},{4,5},{5,6},{6,7},{7,4},{8,9},{9,10},{10,1... | collective-permute-start | bytes 82952 | tf_op jit(solution)/shard_map/ppermute | solution.py:15
  4.2 1.5 %collective-permute-start.11 = (bf16[3,16,288]{2,1,0:T(8,128)(2,1)S(1)}, bf16[3,16,288]{2,1,0:T(8,128)(2,1)S(1)}, u32[]{:S(2)}, u32[]{:S(2)}) collective-permute-start(bf16[3,16,288]{2,1,0:T(8,128)(2,1)S(1)} %reshape.21), channel_id=1, source_target_pairs={{0,2},{1,3},{2,0},{3,1},{4,6},{5,7},{6,4},{7,5},{8,10},{9,11},{10,... | collective-permute-start | bytes 82952 | tf_op jit(solution)/shard_map/ppermute | solution.py:15
  5.7 1.8 %copy.15 = bf16[32,2,16,512]{3,0,2,1:T(8,128)(2,1)S(1)} copy(bf16[32,2,16,512]{3,2,1,0:T(8,128)(2,1)} %param.3) | data formatting | bytes 2097152 | tf_op args[0]
  7.6 4.1 %collective-permute-start.4 = (bf16[2,8,32,512]{3,2,1,0:T(8,128)(2,1)S(1)}, bf16[2,8,32,512]{3,2,1,0:T(8,128)(2,1)S(1)}, u32[]{:S(2)}, u32[]{:S(2)}) collective-permute-start(bf16[2,8,32,512]{3,2,1,0:T(8,128)(2,1)S(1)} %dynamic-slice_bitcast_fusion), channel_id=1, source_target_pairs={{0,224},{4,228},{8,232},{12,236},{16,240},{20,244},{24,248},{28,25... | collective-permute-start | bytes 1572872 | tf_op jit(solution)/shard_map/ppermute | solution.py:15
  11.8 0.7 fusion.2
  12.5 21.0 %collective-permute-done.4.bm_ref = bf16[2,8,32,512]{3,2,1,0:T(8,128)(2,1)S(1)} collective-permute-done((bf16[2,8,32,512]{3,2,1,0:T(8,128)(2,1)S(1)}, bf16[2,8,32,512]{3,2,1,0:T(8,128)(2,1)S(1)}, u32[]{:S(2)}, u32[]{:S(2)}) %collective-permute-start.4) | collective-permute-done | bytes 524320 | tf_op jit(solution)/shard_map/ppermute | solution.py:15
  33.5 1.3 %collective-permute-start.5 = (bf16[2,8,32,512]{3,2,1,0:T(8,128)(2,1)S(1)}, bf16[2,8,32,512]{3,2,1,0:T(8,128)(2,1)S(1)}, u32[]{:S(2)}, u32[]{:S(2)}) collective-permute-start(bf16[2,8,32,512]{3,2,1,0:T(8,128)(2,1)S(1)} %collective-permute-done.4.bm_ref), channel_id=1, source_target_pairs={{0,1},{1,0},{2,3},{3,2},{4,5},{5,4},{6,7},{7,6},{8,9},{9,8},{10,11... | collective-permute-start | bytes 1572872 | tf_op jit(solution)/shard_map/ppermute | solution.py:30
  34.9 7.5 %collective-permute-start.9 = (bf16[2,2,32,512]{3,2,1,0:T(8,128)(2,1)}, bf16[2,2,32,512]{3,2,1,0:T(8,128)(2,1)S(1)}, u32[]{:S(2)}, u32[]{:S(2)}) collective-permute-start(bf16[2,2,32,512]{3,2,1,0:T(8,128)(2,1)} %get-tuple-element.7), channel_id=1, source_target_pairs={{0,220},{4,224},{8,228},{12,232},{16,236},{20,240},{24,244},{28,24... | collective-permute-start | bytes 393224 | tf_op jit(solution)/shard_map/ppermute | solution.py:15
  42.5 3.8 %collective-permute-start.7 = (bf16[2,2,32,512]{3,2,1,0:T(8,128)(2,1)}, bf16[2,2,32,512]{3,2,1,0:T(8,128)(2,1)}, u32[]{:S(2)}, u32[]{:S(2)}) collective-permute-start(bf16[2,2,32,512]{3,2,1,0:T(8,128)(2,1)} %get-tuple-element.7), channel_id=1, source_target_pairs={{0,28},{4,32},{8,36},{12,40},{16,44},{20,48},{24,52},{28,56},{32,6... | collective-permute-start | bytes 393224 | tf_op jit(solution)/shard_map/ppermute | solution.py:15
  46.2 4.3 %collective-permute-start.1 = (bf16[2,2,32,512]{3,2,1,0:T(8,128)(2,1)}, bf16[2,2,32,512]{3,2,1,0:T(8,128)(2,1)}, u32[]{:S(2)}, u32[]{:S(2)}) collective-permute-start(bf16[2,2,32,512]{3,2,1,0:T(8,128)(2,1)} %get-tuple-element.7), channel_id=1, source_target_pairs={{0,252},{4,0},{8,4},{12,8},{16,12},{20,16},{24,20},{28,24},{32,28}... | collective-permute-start | bytes 393224 | tf_op jit(solution)/shard_map/ppermute | solution.py:15
  50.8 6.2 %collective-permute-start.8 = (bf16[2,2,32,512]{3,2,1,0:T(8,128)(2,1)}, bf16[2,2,32,512]{3,2,1,0:T(8,128)(2,1)}, u32[]{:S(2)}, u32[]{:S(2)}) collective-permute-start(bf16[2,2,32,512]{3,2,1,0:T(8,128)(2,1)} %get-tuple-element.8), channel_id=1, source_target_pairs={{0,228},{4,232},{8,236},{12,240},{16,244},{20,248},{24,252},{28,0}... | collective-permute-start | bytes 393224 | tf_op jit(solution)/shard_map/ppermute | solution.py:15
  56.9 3.2 %collective-permute-start.6 = (bf16[2,2,32,512]{3,2,1,0:T(8,128)(2,1)}, bf16[2,2,32,512]{3,2,1,0:T(8,128)(2,1)}, u32[]{:S(2)}, u32[]{:S(2)}) collective-permute-start(bf16[2,2,32,512]{3,2,1,0:T(8,128)(2,1)} %get-tuple-element.8), channel_id=1, source_target_pairs={{0,36},{4,40},{8,44},{12,48},{16,52},{20,56},{24,60},{28,64},{32,6... | collective-permute-start | bytes 393224 | tf_op jit(solution)/shard_map/ppermute | solution.py:15
  60.2 2.7 %collective-permute-start = (bf16[2,2,32,512]{3,2,1,0:T(8,128)(2,1)}, bf16[2,2,32,512]{3,2,1,0:T(8,128)(2,1)}, u32[]{:S(2)}, u32[]{:S(2)}) collective-permute-start(bf16[2,2,32,512]{3,2,1,0:T(8,128)(2,1)} %get-tuple-element.8), channel_id=1, source_target_pairs={{0,4},{4,8},{8,12},{12,16},{16,20},{20,24},{24,28},{28,32},{32,36}... | collective-permute-start | bytes 393224 | tf_op jit(solution)/shard_map/ppermute | solution.py:15
  62.9 0.6 pad_add_fusion.place_ref
  63.5 0.7 reshape.24.keep_ref
  64.2 0.8 reshape.23.w2_ref
  65.0 0.7 pad_maximum_fusion
  65.7 2.0 %collective-permute-done.6.fa_ref = bf16[2,2,32,512]{3,2,1,0:T(8,128)(2,1)} collective-permute-done((bf16[2,2,32,512]{3,2,1,0:T(8,128)(2,1)}, bf16[2,2,32,512]{3,2,1,0:T(8,128)(2,1)}, u32[]{:S(2)}, u32[]{:S(2)}) %collective-permute-start.6) | collective-permute-done | bytes 131104 | tf_op jit(solution)/shard_map/ppermute | solution.py:15
  67.7 8.5 %collective-permute-done.above_ref = bf16[2,2,32,512]{3,2,1,0:T(8,128)(2,1)} collective-permute-done((bf16[2,2,32,512]{3,2,1,0:T(8,128)(2,1)}, bf16[2,2,32,512]{3,2,1,0:T(8,128)(2,1)}, u32[]{:S(2)}, u32[]{:S(2)}) %collective-permute-start) | collective-permute-done | bytes 131104 | tf_op jit(solution)/shard_map/ppermute | solution.py:15
  76.2 0.8 copy-done.3
  77.0 0.2 copy-done.4
  77.2 14.0 %shard_map.37 = bf16[2,16,16,512]{3,2,1,0:T(8,128)(2,1)} custom-call(s32[72]{0:T(128)} %reshape.24.keep_ref, s32[5]{0:T(128)} %pad_add_fusion.place_ref, bf16[2,16,32,512]{3,2,1,0:T(8,128)(2,1)} %bitcast.15, bf16[2,2,32,512]{3,2,1,0:T(8,128)(2,1)} %collective-permute-done.above_ref, bf16[2,2,32,512]{3,2,1,0:T(8,128)(2,1)} %collective-permute-done.1.below_ref, ...), custom_call_target="tpu_custom_call" | custom-call | tf_op jit(solution)/shard_map/pallas_call | solution.py:133
  91.2 2.1 %copy.12 = bf16[16,2,16,512]{3,2,1,0:T(8,128)(2,1)} copy(bf16[16,2,16,512]{3,0,2,1:T(8,128)(2,1)} %bitcast.16) | data formatting | bytes 1048576 | tf_op jit(solution)/shard_map/transpose | solution.py:181
  (46 shorter events, 0.8 us)
Async XLA Ops:
  1.1 33.8 %collective-permute-start.12 = (bf16[3,16,288]{2,1,0:T(8,128)(2,1)S(1)}, bf16[3,16,288]{2,1,0:T(8,128)(2,1)S(1)}, u32[]{:S(2)}, u32[]{:S(2)}) collective-permute-start(bf16[3,16,288]{2,1,0:T(8,128)(2,1)S(1)} %reshape.21), channel_id=1, source_target_pairs={{0,1},{1,2},{2,3},{3,0},{4,5},{5,6},{6,7},{7,4},{8,9},{9,10},{10,1... | collective-permute-start | bytes 82952 | tf_op jit(solution)/shard_map/ppermute | solution.py:15
  4.2 38.3 %collective-permute-start.11 = (bf16[3,16,288]{2,1,0:T(8,128)(2,1)S(1)}, bf16[3,16,288]{2,1,0:T(8,128)(2,1)S(1)}, u32[]{:S(2)}, u32[]{:S(2)}) collective-permute-start(bf16[3,16,288]{2,1,0:T(8,128)(2,1)S(1)} %reshape.21), channel_id=1, source_target_pairs={{0,2},{1,3},{2,0},{3,1},{4,6},{5,7},{6,4},{7,5},{8,10},{9,11},{10,... | collective-permute-start | bytes 82952 | tf_op jit(solution)/shard_map/ppermute | solution.py:15
  5.7 40.5 %collective-permute-start.10 = (bf16[3,16,288]{2,1,0:T(8,128)(2,1)S(1)}, bf16[3,16,288]{2,1,0:T(8,128)(2,1)S(1)}, u32[]{:S(2)}, u32[]{:S(2)}) collective-permute-start(bf16[3,16,288]{2,1,0:T(8,128)(2,1)S(1)} %reshape.21), channel_id=1, source_target_pairs={{0,3},{1,0},{2,1},{3,2},{4,7},{5,4},{6,5},{7,6},{8,11},{9,8},{10,9... | collective-permute-start | bytes 82952 | tf_op jit(solution)/shard_map/ppermute | solution.py:15
  7.5 56.7 %copy-start = (bf16[32,2,16,512]{3,0,2,1:T(8,128)(2,1)}, bf16[32,2,16,512]{3,0,2,1:T(8,128)(2,1)S(1)}, u32[]{:S(2)}) copy-start(bf16[32,2,16,512]{3,0,2,1:T(8,128)(2,1)S(1)} %copy.15) | copy-start | bytes 3145732
  7.6 25.9 %collective-permute-start.4 = (bf16[2,8,32,512]{3,2,1,0:T(8,128)(2,1)S(1)}, bf16[2,8,32,512]{3,2,1,0:T(8,128)(2,1)S(1)}, u32[]{:S(2)}, u32[]{:S(2)}) collective-permute-start(bf16[2,8,32,512]{3,2,1,0:T(8,128)(2,1)S(1)} %dynamic-slice_bitcast_fusion), channel_id=1, source_target_pairs={{0,224},{4,228},{8,232},{12,236},{16,240},{20,244},{24,248},{28,25... | collective-permute-start | bytes 1572872 | tf_op jit(solution)/shard_map/ppermute | solution.py:15
  11.7 23.0 %collective-permute-start.2 = (bf16[2,8,32,512]{3,2,1,0:T(8,128)(2,1)S(1)}, bf16[2,8,32,512]{3,2,1,0:T(8,128)(2,1)S(1)}, u32[]{:S(2)}, u32[]{:S(2)}) collective-permute-start(bf16[2,8,32,512]{3,2,1,0:T(8,128)(2,1)S(1)} %dynamic-slice_bitcast_fusion), channel_id=1, source_target_pairs={{0,32},{4,36},{8,40},{12,44},{16,48},{20,52},{24,56},{28,60},{32,6... | collective-permute-start | bytes 1572872 | tf_op jit(solution)/shard_map/ppermute | solution.py:15
  11.8 38.8 %copy-start.6 = (bf16[3,3,3,16,64]{4,3,2,1,0:T(8,128)(2,1)S(1)}, bf16[3,3,3,16,64]{4,3,2,1,0:T(8,128)(2,1)}, u32[]{:S(2)}) copy-start(bf16[3,3,3,16,64]{4,3,2,1,0:T(8,128)(2,1)} %param.5) | copy-start | bytes 165892
  33.5 42.7 %copy-start.1 = (bf16[2,8,32,512]{3,2,1,0:T(8,128)(2,1)}, bf16[2,8,32,512]{3,2,1,0:T(8,128)(2,1)S(1)}, u32[]{:S(2)}) copy-start(bf16[2,8,32,512]{3,2,1,0:T(8,128)(2,1)S(1)} %collective-permute-done.4.bm_ref) | copy-start | bytes 1572868
  33.5 42.7 %collective-permute-start.5 = (bf16[2,8,32,512]{3,2,1,0:T(8,128)(2,1)S(1)}, bf16[2,8,32,512]{3,2,1,0:T(8,128)(2,1)S(1)}, u32[]{:S(2)}, u32[]{:S(2)}) collective-permute-start(bf16[2,8,32,512]{3,2,1,0:T(8,128)(2,1)S(1)} %collective-permute-done.4.bm_ref), channel_id=1, source_target_pairs={{0,1},{1,0},{2,3},{3,2},{4,5},{5,4},{6,7},{7,6},{8,9},{9,8},{10,11... | collective-permute-start | bytes 1572872 | tf_op jit(solution)/shard_map/ppermute | solution.py:30
  34.8 41.5 %copy-start.2 = (bf16[2,8,32,512]{3,2,1,0:T(8,128)(2,1)}, bf16[2,8,32,512]{3,2,1,0:T(8,128)(2,1)S(1)}, u32[]{:S(2)}) copy-start(bf16[2,8,32,512]{3,2,1,0:T(8,128)(2,1)S(1)} %collective-permute-done.2.fm_ref) | copy-start | bytes 1572868
  34.8 41.5 %collective-permute-start.3 = (bf16[2,8,32,512]{3,2,1,0:T(8,128)(2,1)S(1)}, bf16[2,8,32,512]{3,2,1,0:T(8,128)(2,1)S(1)}, u32[]{:S(2)}, u32[]{:S(2)}) collective-permute-start(bf16[2,8,32,512]{3,2,1,0:T(8,128)(2,1)S(1)} %collective-permute-done.2.fm_ref), channel_id=1, source_target_pairs={{0,1},{1,0},{2,3},{3,2},{4,5},{5,4},{6,7},{7,6},{8,9},{9,8},{10,11... | collective-permute-start | bytes 1572872 | tf_op jit(solution)/shard_map/ppermute | solution.py:30
  34.9 15.6 %copy-start.7 = (bf16[3,16,288]{2,1,0:T(8,128)(2,1)}, bf16[3,16,288]{2,1,0:T(8,128)(2,1)S(1)}, u32[]{:S(2)}) copy-start(bf16[3,16,288]{2,1,0:T(8,128)(2,1)S(1)} %collective-permute-done.12) | copy-start | bytes 82948
  34.9 15.8 %collective-permute-start.9 = (bf16[2,2,32,512]{3,2,1,0:T(8,128)(2,1)}, bf16[2,2,32,512]{3,2,1,0:T(8,128)(2,1)S(1)}, u32[]{:S(2)}, u32[]{:S(2)}) collective-permute-start(bf16[2,2,32,512]{3,2,1,0:T(8,128)(2,1)} %get-tuple-element.7), channel_id=1, source_target_pairs={{0,220},{4,224},{8,228},{12,232},{16,236},{20,240},{24,244},{28,24... | collective-permute-start | bytes 393224 | tf_op jit(solution)/shard_map/ppermute | solution.py:15
  42.5 8.1 %copy-start.9 = (bf16[3,16,288]{2,1,0:T(8,128)(2,1)}, bf16[3,16,288]{2,1,0:T(8,128)(2,1)S(1)}, u32[]{:S(2)}) copy-start(bf16[3,16,288]{2,1,0:T(8,128)(2,1)S(1)} %collective-permute-done.11) | copy-start | bytes 82948
  42.5 14.5 %collective-permute-start.7 = (bf16[2,2,32,512]{3,2,1,0:T(8,128)(2,1)}, bf16[2,2,32,512]{3,2,1,0:T(8,128)(2,1)}, u32[]{:S(2)}, u32[]{:S(2)}) collective-permute-start(bf16[2,2,32,512]{3,2,1,0:T(8,128)(2,1)} %get-tuple-element.7), channel_id=1, source_target_pairs={{0,28},{4,32},{8,36},{12,40},{16,44},{20,48},{24,52},{28,56},{32,6... | collective-permute-start | bytes 393224 | tf_op jit(solution)/shard_map/ppermute | solution.py:15
  46.2 4.3 %copy-start.11 = (bf16[3,16,288]{2,1,0:T(8,128)(2,1)}, bf16[3,16,288]{2,1,0:T(8,128)(2,1)S(1)}, u32[]{:S(2)}) copy-start(bf16[3,16,288]{2,1,0:T(8,128)(2,1)S(1)} %collective-permute-done.10) | copy-start | bytes 82948
  46.2 13.9 %collective-permute-start.1 = (bf16[2,2,32,512]{3,2,1,0:T(8,128)(2,1)}, bf16[2,2,32,512]{3,2,1,0:T(8,128)(2,1)}, u32[]{:S(2)}, u32[]{:S(2)}) collective-permute-start(bf16[2,2,32,512]{3,2,1,0:T(8,128)(2,1)} %get-tuple-element.7), channel_id=1, source_target_pairs={{0,252},{4,0},{8,4},{12,8},{16,12},{20,16},{24,20},{28,24},{32,28}... | collective-permute-start | bytes 393224 | tf_op jit(solution)/shard_map/ppermute | solution.py:15
  50.8 12.7 %copy-start.5 = (bf16[2,2,32,512]{3,2,1,0:T(8,128)(2,1)}, bf16[2,2,32,512]{3,2,1,0:T(8,128)(2,1)S(1)}, u32[]{:S(2)}) copy-start(bf16[2,2,32,512]{3,2,1,0:T(8,128)(2,1)S(1)} %collective-permute-done.9.bb_ref) | copy-start | bytes 393220
  50.8 14.9 %collective-permute-start.8 = (bf16[2,2,32,512]{3,2,1,0:T(8,128)(2,1)}, bf16[2,2,32,512]{3,2,1,0:T(8,128)(2,1)}, u32[]{:S(2)}, u32[]{:S(2)}) collective-permute-start(bf16[2,2,32,512]{3,2,1,0:T(8,128)(2,1)} %get-tuple-element.8), channel_id=1, source_target_pairs={{0,228},{4,232},{8,236},{12,240},{16,244},{20,248},{24,252},{28,0}... | collective-permute-start | bytes 393224 | tf_op jit(solution)/shard_map/ppermute | solution.py:15
  56.9 10.7 %collective-permute-start.6 = (bf16[2,2,32,512]{3,2,1,0:T(8,128)(2,1)}, bf16[2,2,32,512]{3,2,1,0:T(8,128)(2,1)}, u32[]{:S(2)}, u32[]{:S(2)}) collective-permute-start(bf16[2,2,32,512]{3,2,1,0:T(8,128)(2,1)} %get-tuple-element.8), channel_id=1, source_target_pairs={{0,36},{4,40},{8,44},{12,48},{16,52},{20,56},{24,60},{28,64},{32,6... | collective-permute-start | bytes 393224 | tf_op jit(solution)/shard_map/ppermute | solution.py:15
  60.2 16.0 %collective-permute-start = (bf16[2,2,32,512]{3,2,1,0:T(8,128)(2,1)}, bf16[2,2,32,512]{3,2,1,0:T(8,128)(2,1)}, u32[]{:S(2)}, u32[]{:S(2)}) collective-permute-start(bf16[2,2,32,512]{3,2,1,0:T(8,128)(2,1)} %get-tuple-element.8), channel_id=1, source_target_pairs={{0,4},{4,8},{8,12},{12,16},{16,20},{20,24},{24,28},{28,32},{32,36}... | collective-permute-start | bytes 393224 | tf_op jit(solution)/shard_map/ppermute | solution.py:15
  64.2 0.8 copy-start.8
  76.2 0.8 copy-start.3
  76.2 1.0 %copy-start.4 = (bf16[2,8,32,512]{3,2,1,0:T(8,128)(2,1)}, bf16[2,8,32,512]{3,2,1,0:T(8,128)(2,1)S(1)}, u32[]{:S(2)}) copy-start(bf16[2,8,32,512]{3,2,1,0:T(8,128)(2,1)S(1)} %collective-permute-done.3.ft_ref) | copy-start | bytes 1572868
  (2 other events, 1.6 us)

commit v8 on v7

--- a/solution.py
+++ b/solution.py
@@ -21,22 +21,23 @@
     return position % GH, position // GH, tile_count // GH
 
 
-def shared_along(value, steps):
-    core = lax.axis_index("chan") % 2
-    half = value.shape[1] // 2
-    mine = lax.dynamic_slice_in_dim(value, core * half, half, 1)
+def shared_along(mine, steps):
     mine = passed_along(mine, "space", steps)
     count = lax.axis_size("chan")
     theirs = lax.ppermute(mine, "chan", [(source, source ^ 1) for source in range(count)])
     return mine, theirs
 
 
-def halo_pieces(volume_tile, rim):
+def halo_pieces(voxels, rim):
     tile_row, depth_tile, grid_depth = tile_place()
+    core = lax.axis_index("chan") % 2
+    half = voxels.shape[2] // 2
+    mine = lax.dynamic_slice_in_dim(voxels, core * half, half, 2).transpose(1, 2, 0, 3)
+    front = shared_along(mine, GH)
+    back = shared_along(mine, -GH)
+    volume_tile = voxels.transpose(1, 2, 0, 3)
     top = volume_tile[:, -rim:]
     bottom = volume_tile[:, :rim]
-    front = shared_along(volume_tile, GH)
-    back = shared_along(volume_tile, -GH)
     above = passed_along(top, "space", 1)
     below = passed_along(bottom, "space", -1)
     front_above = passed_along(top, "space", GH + 1)
@@ -173,10 +174,9 @@
 
 
 def local(voxels, first_filters, second_filters):
-    tile = voxels.transpose(1, 2, 0, 3)
-    place, pieces = halo_pieces(tile, 2)
+    place, pieces = halo_pieces(voxels, 2)
     all_first, second_filters = gathered_filters(first_filters, second_filters)
-    keep = inside_flags(tile.shape[0] + 2, tile.shape[1] + 2)
+    keep = inside_flags(voxels.shape[1] + 2, voxels.shape[2] + 2)
     out = two_layers(keep, place, pieces, all_first, tap_matrices(second_filters))
     return out.transpose(2, 0, 1, 3)
 

time: 93.5 us -> 93.5 us (level)
  no operation moved by 1% of the time
where the time goes in v8:
time: 93.5 us; the launch traced here: 93.3 us
  starting transfers between devices  37.8 us (40%)
  waiting for transfers between devices  31.5 us (34%)
  Pallas kernels  14 us (15%)
  local copies, waits for them, and re-layouts  8.26 us (9%)
  other arithmetic  1.58 us (2%)
    ppermute x11, starting transfers between devices, passed_along(): return lax.ppermute(value, axis, pairs)  36.4 us
    ppermute x11, waiting for transfers between devices, passed_along(): return lax.ppermute(value, axis, pairs)  31.5 us
    pallas_call x1, Pallas kernels, two_layers(): pl.pallas_call(two_layers_kernel, out_shape=jax.ShapeDtypeStruct((depth,...  14 us
    unnamed x27, local copies, waits for them, and re-layouts  2.8 us
    transpose x1, local copies, waits for them, and re-layouts, local(): return out.transpose(2, 0, 1, 3)  2.13 us
  transfers between devices with their start and end apart: 13, of which 3 were waited for; matrix products, arithmetic and copies ran while one was open for 6% of the time, Pallas kernels for 0%

profile of v8, /device:TPU:1, one launch (start us, length us, event | category | flops | bytes accessed | tf_op | source)
XLA Modules:
  0.0 93.3 jit_solution(629882585435398229)
XLA Ops:
  0.0 1.0 %copy.10 = bf16[3,16,3,3,32]{4,3,2,1,0:T(4,128)(2,1)S(1)} copy(bf16[3,16,3,3,32]{4,1,0,3,2:T(8,128)(2,1)} %bitcast.18) | data formatting | bytes 55296 | tf_op jit(solution)/shard_map/transpose | solution.py:166
  1.1 3.1 %collective-permute-start.12 = (bf16[3,16,288]{2,1,0:T(8,128)(2,1)S(1)}, bf16[3,16,288]{2,1,0:T(8,128)(2,1)S(1)}, u32[]{:S(2)}, u32[]{:S(2)}) collective-permute-start(bf16[3,16,288]{2,1,0:T(8,128)(2,1)S(1)} %reshape.21), channel_id=1, source_target_pairs={{0,1},{1,2},{2,3},{3,0},{4,5},{5,6},{6,7},{7,4},{8,9},{9,10},{10,1... | collective-permute-start | bytes 82952 | tf_op jit(solution)/shard_map/ppermute | solution.py:15
  4.2 1.5 %collective-permute-start.11 = (bf16[3,16,288]{2,1,0:T(8,128)(2,1)S(1)}, bf16[3,16,288]{2,1,0:T(8,128)(2,1)S(1)}, u32[]{:S(2)}, u32[]{:S(2)}) collective-permute-start(bf16[3,16,288]{2,1,0:T(8,128)(2,1)S(1)} %reshape.21), channel_id=1, source_target_pairs={{0,2},{1,3},{2,0},{3,1},{4,6},{5,7},{6,4},{7,5},{8,10},{9,11},{10,... | collective-permute-start | bytes 82952 | tf_op jit(solution)/shard_map/ppermute | solution.py:15
  5.7 1.8 %copy.15 = bf16[32,2,16,512]{3,0,2,1:T(8,128)(2,1)S(1)} copy(bf16[32,2,16,512]{3,2,1,0:T(8,128)(2,1)} %param.3) | data formatting | bytes 2097152 | tf_op args[0]
  7.6 4.1 %collective-permute-start.4 = (bf16[2,8,32,512]{3,2,1,0:T(8,128)(2,1)S(1)}, bf16[2,8,32,512]{3,2,1,0:T(8,128)(2,1)S(1)}, u32[]{:S(2)}, u32[]{:S(2)}) collective-permute-start(bf16[2,8,32,512]{3,2,1,0:T(8,128)(2,1)S(1)} %dynamic-slice_bitcast_fusion), channel_id=1, source_target_pairs={{0,224},{4,228},{8,232},{12,236},{16,240},{20,244},{24,248},{28,25... | collective-permute-start | bytes 1572872 | tf_op jit(solution)/shard_map/ppermute | solution.py:15
  11.8 0.7 fusion.2
  12.5 21.0 %collective-permute-done.4.bm_ref = bf16[2,8,32,512]{3,2,1,0:T(8,128)(2,1)S(1)} collective-permute-done((bf16[2,8,32,512]{3,2,1,0:T(8,128)(2,1)S(1)}, bf16[2,8,32,512]{3,2,1,0:T(8,128)(2,1)S(1)}, u32[]{:S(2)}, u32[]{:S(2)}) %collective-permute-start.4) | collective-permute-done | bytes 524320 | tf_op jit(solution)/shard_map/ppermute | solution.py:15
  33.5 1.3 %collective-permute-start.5 = (bf16[2,8,32,512]{3,2,1,0:T(8,128)(2,1)S(1)}, bf16[2,8,32,512]{3,2,1,0:T(8,128)(2,1)S(1)}, u32[]{:S(2)}, u32[]{:S(2)}) collective-permute-start(bf16[2,8,32,512]{3,2,1,0:T(8,128)(2,1)S(1)} %collective-permute-done.4.bm_ref), channel_id=1, source_target_pairs={{0,1},{1,0},{2,3},{3,2},{4,5},{5,4},{6,7},{7,6},{8,9},{9,8},{10,11... | collective-permute-start | bytes 1572872 | tf_op jit(solution)/shard_map/ppermute | solution.py:27
  34.9 7.5 %collective-permute-start.9 = (bf16[2,2,32,512]{3,2,1,0:T(8,128)(2,1)}, bf16[2,2,32,512]{3,2,1,0:T(8,128)(2,1)S(1)}, u32[]{:S(2)}, u32[]{:S(2)}) collective-permute-start(bf16[2,2,32,512]{3,2,1,0:T(8,128)(2,1)} %get-tuple-element.7), channel_id=1, source_target_pairs={{0,220},{4,224},{8,228},{12,232},{16,236},{20,240},{24,244},{28,24... | collective-permute-start | bytes 393224 | tf_op jit(solution)/shard_map/ppermute | solution.py:15
  42.5 3.8 %collective-permute-start.7 = (bf16[2,2,32,512]{3,2,1,0:T(8,128)(2,1)}, bf16[2,2,32,512]{3,2,1,0:T(8,128)(2,1)}, u32[]{:S(2)}, u32[]{:S(2)}) collective-permute-start(bf16[2,2,32,512]{3,2,1,0:T(8,128)(2,1)} %get-tuple-element.7), channel_id=1, source_target_pairs={{0,28},{4,32},{8,36},{12,40},{16,44},{20,48},{24,52},{28,56},{32,6... | collective-permute-start | bytes 393224 | tf_op jit(solution)/shard_map/ppermute | solution.py:15
  46.2 4.3 %collective-permute-start.1 = (bf16[2,2,32,512]{3,2,1,0:T(8,128)(2,1)}, bf16[2,2,32,512]{3,2,1,0:T(8,128)(2,1)}, u32[]{:S(2)}, u32[]{:S(2)}) collective-permute-start(bf16[2,2,32,512]{3,2,1,0:T(8,128)(2,1)} %get-tuple-element.7), channel_id=1, source_target_pairs={{0,252},{4,0},{8,4},{12,8},{16,12},{20,16},{24,20},{28,24},{32,28}... | collective-permute-start | bytes 393224 | tf_op jit(solution)/shard_map/ppermute | solution.py:15
  50.8 6.2 %collective-permute-start.8 = (bf16[2,2,32,512]{3,2,1,0:T(8,128)(2,1)}, bf16[2,2,32,512]{3,2,1,0:T(8,128)(2,1)}, u32[]{:S(2)}, u32[]{:S(2)}) collective-permute-start(bf16[2,2,32,512]{3,2,1,0:T(8,128)(2,1)} %get-tuple-element.8), channel_id=1, source_target_pairs={{0,228},{4,232},{8,236},{12,240},{16,244},{20,248},{24,252},{28,0}... | collective-permute-start | bytes 393224 | tf_op jit(solution)/shard_map/ppermute | solution.py:15
  56.9 3.2 %collective-permute-start.6 = (bf16[2,2,32,512]{3,2,1,0:T(8,128)(2,1)}, bf16[2,2,32,512]{3,2,1,0:T(8,128)(2,1)}, u32[]{:S(2)}, u32[]{:S(2)}) collective-permute-start(bf16[2,2,32,512]{3,2,1,0:T(8,128)(2,1)} %get-tuple-element.8), channel_id=1, source_target_pairs={{0,36},{4,40},{8,44},{12,48},{16,52},{20,56},{24,60},{28,64},{32,6... | collective-permute-start | bytes 393224 | tf_op jit(solution)/shard_map/ppermute | solution.py:15
  60.2 2.7 %collective-permute-start = (bf16[2,2,32,512]{3,2,1,0:T(8,128)(2,1)}, bf16[2,2,32,512]{3,2,1,0:T(8,128)(2,1)}, u32[]{:S(2)}, u32[]{:S(2)}) collective-permute-start(bf16[2,2,32,512]{3,2,1,0:T(8,128)(2,1)} %get-tuple-element.8), channel_id=1, source_target_pairs={{0,4},{4,8},{8,12},{12,16},{16,20},{20,24},{24,28},{28,32},{32,36}... | collective-permute-start | bytes 393224 | tf_op jit(solution)/shard_map/ppermute | solution.py:15
  62.9 0.6 pad_add_fusion.place_ref
  63.5 0.7 reshape.24.keep_ref
  64.2 0.8 reshape.23.w2_ref
  65.0 0.7 pad_maximum_fusion
  65.7 2.0 %collective-permute-done.6.fa_ref = bf16[2,2,32,512]{3,2,1,0:T(8,128)(2,1)} collective-permute-done((bf16[2,2,32,512]{3,2,1,0:T(8,128)(2,1)}, bf16[2,2,32,512]{3,2,1,0:T(8,128)(2,1)}, u32[]{:S(2)}, u32[]{:S(2)}) %collective-permute-start.6) | collective-permute-done | bytes 131104 | tf_op jit(solution)/shard_map/ppermute | solution.py:15
  67.7 8.5 %collective-permute-done.above_ref = bf16[2,2,32,512]{3,2,1,0:T(8,128)(2,1)} collective-permute-done((bf16[2,2,32,512]{3,2,1,0:T(8,128)(2,1)}, bf16[2,2,32,512]{3,2,1,0:T(8,128)(2,1)}, u32[]{:S(2)}, u32[]{:S(2)}) %collective-permute-start) | collective-permute-done | bytes 131104 | tf_op jit(solution)/shard_map/ppermute | solution.py:15
  76.2 0.8 copy-done.3
  77.0 0.2 copy-done.4
  77.2 14.0 %shard_map.37 = bf16[2,16,16,512]{3,2,1,0:T(8,128)(2,1)} custom-call(s32[72]{0:T(128)} %reshape.24.keep_ref, s32[5]{0:T(128)} %pad_add_fusion.place_ref, bf16[2,16,32,512]{3,2,1,0:T(8,128)(2,1)} %bitcast.15, bf16[2,2,32,512]{3,2,1,0:T(8,128)(2,1)} %collective-permute-done.above_ref, bf16[2,2,32,512]{3,2,1,0:T(8,128)(2,1)} %collective-permute-done.1.below_ref, ...), custom_call_target="tpu_custom_call" | custom-call | tf_op jit(solution)/shard_map/pallas_call | solution.py:134
  91.2 2.1 %copy.12 = bf16[16,2,16,512]{3,2,1,0:T(8,128)(2,1)} copy(bf16[16,2,16,512]{3,0,2,1:T(8,128)(2,1)} %bitcast.16) | data formatting | bytes 1048576 | tf_op jit(solution)/shard_map/transpose | solution.py:181
  (46 shorter events, 0.8 us)
Async XLA Ops:
  1.1 33.8 %collective-permute-start.12 = (bf16[3,16,288]{2,1,0:T(8,128)(2,1)S(1)}, bf16[3,16,288]{2,1,0:T(8,128)(2,1)S(1)}, u32[]{:S(2)}, u32[]{:S(2)}) collective-permute-start(bf16[3,16,288]{2,1,0:T(8,128)(2,1)S(1)} %reshape.21), channel_id=1, source_target_pairs={{0,1},{1,2},{2,3},{3,0},{4,5},{5,6},{6,7},{7,4},{8,9},{9,10},{10,1... | collective-permute-start | bytes 82952 | tf_op jit(solution)/shard_map/ppermute | solution.py:15
  4.2 38.3 %collective-permute-start.11 = (bf16[3,16,288]{2,1,0:T(8,128)(2,1)S(1)}, bf16[3,16,288]{2,1,0:T(8,128)(2,1)S(1)}, u32[]{:S(2)}, u32[]{:S(2)}) collective-permute-start(bf16[3,16,288]{2,1,0:T(8,128)(2,1)S(1)} %reshape.21), channel_id=1, source_target_pairs={{0,2},{1,3},{2,0},{3,1},{4,6},{5,7},{6,4},{7,5},{8,10},{9,11},{10,... | collective-permute-start | bytes 82952 | tf_op jit(solution)/shard_map/ppermute | solution.py:15
  5.7 40.5 %collective-permute-start.10 = (bf16[3,16,288]{2,1,0:T(8,128)(2,1)S(1)}, bf16[3,16,288]{2,1,0:T(8,128)(2,1)S(1)}, u32[]{:S(2)}, u32[]{:S(2)}) collective-permute-start(bf16[3,16,288]{2,1,0:T(8,128)(2,1)S(1)} %reshape.21), channel_id=1, source_target_pairs={{0,3},{1,0},{2,1},{3,2},{4,7},{5,4},{6,5},{7,6},{8,11},{9,8},{10,9... | collective-permute-start | bytes 82952 | tf_op jit(solution)/shard_map/ppermute | solution.py:15
  7.5 56.7 %copy-start = (bf16[32,2,16,512]{3,0,2,1:T(8,128)(2,1)}, bf16[32,2,16,512]{3,0,2,1:T(8,128)(2,1)S(1)}, u32[]{:S(2)}) copy-start(bf16[32,2,16,512]{3,0,2,1:T(8,128)(2,1)S(1)} %copy.15) | copy-start | bytes 3145732
  7.6 25.9 %collective-permute-start.4 = (bf16[2,8,32,512]{3,2,1,0:T(8,128)(2,1)S(1)}, bf16[2,8,32,512]{3,2,1,0:T(8,128)(2,1)S(1)}, u32[]{:S(2)}, u32[]{:S(2)}) collective-permute-start(bf16[2,8,32,512]{3,2,1,0:T(8,128)(2,1)S(1)} %dynamic-slice_bitcast_fusion), channel_id=1, source_target_pairs={{0,224},{4,228},{8,232},{12,236},{16,240},{20,244},{24,248},{28,25... | collective-permute-start | bytes 1572872 | tf_op jit(solution)/shard_map/ppermute | solution.py:15
  11.7 23.0 %collective-permute-start.2 = (bf16[2,8,32,512]{3,2,1,0:T(8,128)(2,1)S(1)}, bf16[2,8,32,512]{3,2,1,0:T(8,128)(2,1)S(1)}, u32[]{:S(2)}, u32[]{:S(2)}) collective-permute-start(bf16[2,8,32,512]{3,2,1,0:T(8,128)(2,1)S(1)} %dynamic-slice_bitcast_fusion), channel_id=1, source_target_pairs={{0,32},{4,36},{8,40},{12,44},{16,48},{20,52},{24,56},{28,60},{32,6... | collective-permute-start | bytes 1572872 | tf_op jit(solution)/shard_map/ppermute | solution.py:15
  11.8 38.8 %copy-start.6 = (bf16[3,3,3,16,64]{4,3,2,1,0:T(8,128)(2,1)S(1)}, bf16[3,3,3,16,64]{4,3,2,1,0:T(8,128)(2,1)}, u32[]{:S(2)}) copy-start(bf16[3,3,3,16,64]{4,3,2,1,0:T(8,128)(2,1)} %param.5) | copy-start | bytes 165892
  33.5 42.7 %copy-start.1 = (bf16[2,8,32,512]{3,2,1,0:T(8,128)(2,1)}, bf16[2,8,32,512]{3,2,1,0:T(8,128)(2,1)S(1)}, u32[]{:S(2)}) copy-start(bf16[2,8,32,512]{3,2,1,0:T(8,128)(2,1)S(1)} %collective-permute-done.4.bm_ref) | copy-start | bytes 1572868
  33.5 42.7 %collective-permute-start.5 = (bf16[2,8,32,512]{3,2,1,0:T(8,128)(2,1)S(1)}, bf16[2,8,32,512]{3,2,1,0:T(8,128)(2,1)S(1)}, u32[]{:S(2)}, u32[]{:S(2)}) collective-permute-start(bf16[2,8,32,512]{3,2,1,0:T(8,128)(2,1)S(1)} %collective-permute-done.4.bm_ref), channel_id=1, source_target_pairs={{0,1},{1,0},{2,3},{3,2},{4,5},{5,4},{6,7},{7,6},{8,9},{9,8},{10,11... | collective-permute-start | bytes 1572872 | tf_op jit(solution)/shard_map/ppermute | solution.py:27
  34.8 41.5 %copy-start.2 = (bf16[2,8,32,512]{3,2,1,0:T(8,128)(2,1)}, bf16[2,8,32,512]{3,2,1,0:T(8,128)(2,1)S(1)}, u32[]{:S(2)}) copy-start(bf16[2,8,32,512]{3,2,1,0:T(8,128)(2,1)S(1)} %collective-permute-done.2.fm_ref) | copy-start | bytes 1572868
  34.8 41.5 %collective-permute-start.3 = (bf16[2,8,32,512]{3,2,1,0:T(8,128)(2,1)S(1)}, bf16[2,8,32,512]{3,2,1,0:T(8,128)(2,1)S(1)}, u32[]{:S(2)}, u32[]{:S(2)}) collective-permute-start(bf16[2,8,32,512]{3,2,1,0:T(8,128)(2,1)S(1)} %collective-permute-done.2.fm_ref), channel_id=1, source_target_pairs={{0,1},{1,0},{2,3},{3,2},{4,5},{5,4},{6,7},{7,6},{8,9},{9,8},{10,11... | collective-permute-start | bytes 1572872 | tf_op jit(solution)/shard_map/ppermute | solution.py:27
  34.9 15.6 %copy-start.7 = (bf16[3,16,288]{2,1,0:T(8,128)(2,1)}, bf16[3,16,288]{2,1,0:T(8,128)(2,1)S(1)}, u32[]{:S(2)}) copy-start(bf16[3,16,288]{2,1,0:T(8,128)(2,1)S(1)} %collective-permute-done.12) | copy-start | bytes 82948
  34.9 15.8 %collective-permute-start.9 = (bf16[2,2,32,512]{3,2,1,0:T(8,128)(2,1)}, bf16[2,2,32,512]{3,2,1,0:T(8,128)(2,1)S(1)}, u32[]{:S(2)}, u32[]{:S(2)}) collective-permute-start(bf16[2,2,32,512]{3,2,1,0:T(8,128)(2,1)} %get-tuple-element.7), channel_id=1, source_target_pairs={{0,220},{4,224},{8,228},{12,232},{16,236},{20,240},{24,244},{28,24... | collective-permute-start | bytes 393224 | tf_op jit(solution)/shard_map/ppermute | solution.py:15
  42.5 8.1 %copy-start.9 = (bf16[3,16,288]{2,1,0:T(8,128)(2,1)}, bf16[3,16,288]{2,1,0:T(8,128)(2,1)S(1)}, u32[]{:S(2)}) copy-start(bf16[3,16,288]{2,1,0:T(8,128)(2,1)S(1)} %collective-permute-done.11) | copy-start | bytes 82948
  42.5 14.5 %collective-permute-start.7 = (bf16[2,2,32,512]{3,2,1,0:T(8,128)(2,1)}, bf16[2,2,32,512]{3,2,1,0:T(8,128)(2,1)}, u32[]{:S(2)}, u32[]{:S(2)}) collective-permute-start(bf16[2,2,32,512]{3,2,1,0:T(8,128)(2,1)} %get-tuple-element.7), channel_id=1, source_target_pairs={{0,28},{4,32},{8,36},{12,40},{16,44},{20,48},{24,52},{28,56},{32,6... | collective-permute-start | bytes 393224 | tf_op jit(solution)/shard_map/ppermute | solution.py:15
  46.2 4.3 %copy-start.11 = (bf16[3,16,288]{2,1,0:T(8,128)(2,1)}, bf16[3,16,288]{2,1,0:T(8,128)(2,1)S(1)}, u32[]{:S(2)}) copy-start(bf16[3,16,288]{2,1,0:T(8,128)(2,1)S(1)} %collective-permute-done.10) | copy-start | bytes 82948
  46.2 13.9 %collective-permute-start.1 = (bf16[2,2,32,512]{3,2,1,0:T(8,128)(2,1)}, bf16[2,2,32,512]{3,2,1,0:T(8,128)(2,1)}, u32[]{:S(2)}, u32[]{:S(2)}) collective-permute-start(bf16[2,2,32,512]{3,2,1,0:T(8,128)(2,1)} %get-tuple-element.7), channel_id=1, source_target_pairs={{0,252},{4,0},{8,4},{12,8},{16,12},{20,16},{24,20},{28,24},{32,28}... | collective-permute-start | bytes 393224 | tf_op jit(solution)/shard_map/ppermute | solution.py:15
  50.8 12.7 %copy-start.5 = (bf16[2,2,32,512]{3,2,1,0:T(8,128)(2,1)}, bf16[2,2,32,512]{3,2,1,0:T(8,128)(2,1)S(1)}, u32[]{:S(2)}) copy-start(bf16[2,2,32,512]{3,2,1,0:T(8,128)(2,1)S(1)} %collective-permute-done.9.bb_ref) | copy-start | bytes 393220
  50.8 14.9 %collective-permute-start.8 = (bf16[2,2,32,512]{3,2,1,0:T(8,128)(2,1)}, bf16[2,2,32,512]{3,2,1,0:T(8,128)(2,1)}, u32[]{:S(2)}, u32[]{:S(2)}) collective-permute-start(bf16[2,2,32,512]{3,2,1,0:T(8,128)(2,1)} %get-tuple-element.8), channel_id=1, source_target_pairs={{0,228},{4,232},{8,236},{12,240},{16,244},{20,248},{24,252},{28,0}... | collective-permute-start | bytes 393224 | tf_op jit(solution)/shard_map/ppermute | solution.py:15
  56.9 10.7 %collective-permute-start.6 = (bf16[2,2,32,512]{3,2,1,0:T(8,128)(2,1)}, bf16[2,2,32,512]{3,2,1,0:T(8,128)(2,1)}, u32[]{:S(2)}, u32[]{:S(2)}) collective-permute-start(bf16[2,2,32,512]{3,2,1,0:T(8,128)(2,1)} %get-tuple-element.8), channel_id=1, source_target_pairs={{0,36},{4,40},{8,44},{12,48},{16,52},{20,56},{24,60},{28,64},{32,6... | collective-permute-start | bytes 393224 | tf_op jit(solution)/shard_map/ppermute | solution.py:15
  60.2 16.0 %collective-permute-start = (bf16[2,2,32,512]{3,2,1,0:T(8,128)(2,1)}, bf16[2,2,32,512]{3,2,1,0:T(8,128)(2,1)}, u32[]{:S(2)}, u32[]{:S(2)}) collective-permute-start(bf16[2,2,32,512]{3,2,1,0:T(8,128)(2,1)} %get-tuple-element.8), channel_id=1, source_target_pairs={{0,4},{4,8},{8,12},{12,16},{16,20},{20,24},{24,28},{28,32},{32,36}... | collective-permute-start | bytes 393224 | tf_op jit(solution)/shard_map/ppermute | solution.py:15
  64.2 0.8 copy-start.8
  76.2 0.8 copy-start.3
  76.2 1.0 %copy-start.4 = (bf16[2,8,32,512]{3,2,1,0:T(8,128)(2,1)}, bf16[2,8,32,512]{3,2,1,0:T(8,128)(2,1)S(1)}, u32[]{:S(2)}) copy-start(bf16[2,8,32,512]{3,2,1,0:T(8,128)(2,1)S(1)} %collective-permute-done.3.ft_ref) | copy-start | bytes 1572868
  (2 other events, 1.6 us)

commit v9 on v8

--- a/solution.py
+++ b/solution.py
@@ -40,10 +40,11 @@
     bottom = volume_tile[:, :rim]
     above = passed_along(top, "space", 1)
     below = passed_along(bottom, "space", -1)
-    front_above = passed_along(top, "space", GH + 1)
-    front_below = passed_along(bottom, "space", GH - 1)
-    back_above = passed_along(top, "space", 1 - GH)
-    back_below = passed_along(bottom, "space", -1 - GH)
+    rims = jnp.concatenate([above, below], 1)
+    front_corners = passed_along(rims, "space", GH)
+    back_corners = passed_along(rims, "space", -GH)
+    front_above, front_below = front_corners[:, :rim], front_corners[:, rim:]
+    back_above, back_below = back_corners[:, :rim], back_corners[:, rim:]
     place = jnp.stack([
         tile_row > 0, tile_row < GH - 1, depth_tile > 0, depth_tile < grid_depth - 1,
     ]).astype(jnp.int32)

time: 93.5 us -> 69.8 us (0.75)
  starting transfers between devices: 37.8 us -> 25.2 us
  waiting for transfers between devices: 31.5 us -> 20 us
    ppermute x11 -> x9, starting transfers between devices: 36.4 us -> 24.6 us  [passed_along(): return lax.ppermute(value, axis, pairs)]
    ppermute x11 -> x9, waiting for transfers between devices: 31.5 us -> 20 us  [passed_along(): return lax.ppermute(value, axis, pairs)]
    slice x0 -> x2, local copies, waits for them, and re-layouts: none -> 1.43 us  [the longest x1 0.73 us: halo_pieces(): front_above, front_below = (front_corners[:, :rim], front_corners[:, rim:])]
    unnamed x27 -> x20, local copies, waits for them, and re-layouts: 2.8 us -> 3.41 us
  transfers between devices with their start and end apart: 13 -> 11, of which waited for: 3 -> 3; matrix products, arithmetic and copies ran while one was open for 6% -> 7% of each run, Pallas kernels for 0% -> 0%
where the time goes in v9:
time: 69.8 us; the launch traced here: 69.6 us
  starting transfers between devices  25.2 us (36%)
  waiting for transfers between devices  20 us (29%)
  Pallas kernels  14 us (20%)
  local copies, waits for them, and re-layouts  8.7 us (12%)
  other arithmetic  1.61 us (2%)
    ppermute x9, starting transfers between devices, passed_along(): return lax.ppermute(value, axis, pairs)  24.6 us
    ppermute x9, waiting for transfers between devices, passed_along(): return lax.ppermute(value, axis, pairs)  20 us
    pallas_call x1, Pallas kernels, two_layers(): pl.pallas_call(two_layers_kernel, out_shape=jax.ShapeDtypeStruct((depth,...  14 us
    unnamed x20, local copies, waits for them, and re-layouts  3.41 us
    transpose x1, local copies, waits for them, and re-layouts, local(): return out.transpose(2, 0, 1, 3)  2.13 us
  transfers between devices with their start and end apart: 11, of which 3 were waited for; matrix products, arithmetic and copies ran while one was open for 7% of the time, Pallas kernels for 0%

profile of v9, /device:TPU:1, one launch (start us, length us, event | category | flops | bytes accessed | tf_op | source)
XLA Modules:
  0.0 69.6 jit_solution(5551775032994749958)
XLA Ops:
  0.0 1.8 %copy.15 = bf16[32,2,16,512]{3,0,2,1:T(8,128)(2,1)S(1)} copy(bf16[32,2,16,512]{3,2,1,0:T(8,128)(2,1)} %param.3) | data formatting | bytes 2097152 | tf_op args[0]
  1.9 6.0 %collective-permute-start.4 = (bf16[2,8,32,512]{3,2,1,0:T(8,128)(2,1)S(1)}, bf16[2,8,32,512]{3,2,1,0:T(8,128)(2,1)S(1)}, u32[]{:S(2)}, u32[]{:S(2)}) collective-permute-start(bf16[2,8,32,512]{3,2,1,0:T(8,128)(2,1)S(1)} %dynamic-slice_bitcast_fusion), channel_id=1, source_target_pairs={{0,224},{4,228},{8,232},{12,236},{16,240},{20,244},{24,248},{28,25... | collective-permute-start | bytes 1572872 | tf_op jit(solution)/shard_map/ppermute | solution.py:15
  8.1 2.6 %collective-permute-start.10 = (bf16[3,16,288]{2,1,0:T(8,128)(2,1)S(1)}, bf16[3,16,288]{2,1,0:T(8,128)(2,1)S(1)}, u32[]{:S(2)}, u32[]{:S(2)}) collective-permute-start(bf16[3,16,288]{2,1,0:T(8,128)(2,1)S(1)} %reshape.21), channel_id=1, source_target_pairs={{0,1},{1,2},{2,3},{3,0},{4,5},{5,6},{6,7},{7,4},{8,9},{9,10},{10,1... | collective-permute-start | bytes 82952 | tf_op jit(solution)/shard_map/ppermute | solution.py:15
  10.7 10.1 %collective-permute-start.1 = (bf16[2,2,32,512]{3,2,1,0:T(8,128)(2,1)S(1)}, bf16[2,2,32,512]{3,2,1,0:T(8,128)(2,1)S(1)}, u32[]{:S(2)}, u32[]{:S(2)}) collective-permute-start(bf16[2,2,32,512]{3,2,1,0:T(8,128)(2,1)S(1)} %get-tuple-element.7), channel_id=1, source_target_pairs={{0,252},{4,0},{8,4},{12,8},{16,12},{20,16},{24,20},{28,24},{32,28}... | collective-permute-start | bytes 393224 | tf_op jit(solution)/shard_map/ppermute | solution.py:15
  20.9 0.2 fusion
  21.0 13.7 %collective-permute-done.above_ref = bf16[2,2,32,512]{3,2,1,0:T(8,128)(2,1)S(1)} collective-permute-done((bf16[2,2,32,512]{3,2,1,0:T(8,128)(2,1)S(1)}, bf16[2,2,32,512]{3,2,1,0:T(8,128)(2,1)S(1)}, u32[]{:S(2)}, u32[]{:S(2)}) %collective-permute-start) | collective-permute-done | bytes 131104 | tf_op jit(solution)/shard_map/ppermute | solution.py:15
  34.7 1.5 %collective-permute-start.9 = (bf16[3,16,288]{2,1,0:T(8,128)(2,1)S(1)}, bf16[3,16,288]{2,1,0:T(8,128)(2,1)S(1)}, u32[]{:S(2)}, u32[]{:S(2)}) collective-permute-start(bf16[3,16,288]{2,1,0:T(8,128)(2,1)S(1)} %reshape.21), channel_id=1, source_target_pairs={{0,2},{1,3},{2,0},{3,1},{4,6},{5,7},{6,4},{7,5},{8,10},{9,11},{10,... | collective-permute-start | bytes 82952 | tf_op jit(solution)/shard_map/ppermute | solution.py:15
  36.3 0.6 copy-done.5
  37.0 1.1 %collective-permute-start.8 = (bf16[3,16,288]{2,1,0:T(8,128)(2,1)S(1)}, bf16[3,16,288]{2,1,0:T(8,128)(2,1)S(1)}, u32[]{:S(2)}, u32[]{:S(2)}) collective-permute-start(bf16[3,16,288]{2,1,0:T(8,128)(2,1)S(1)} %reshape.21), channel_id=1, source_target_pairs={{0,3},{1,0},{2,1},{3,2},{4,7},{5,4},{6,5},{7,6},{8,11},{9,8},{10,9... | collective-permute-start | bytes 82952 | tf_op jit(solution)/shard_map/ppermute | solution.py:15
  38.2 0.6 pad_add_fusion.place_ref
  38.8 0.7 reshape.24.keep_ref
  39.5 0.8 %reshape.23.w2_ref = bf16[48,576]{1,0:T(8,128)(2,1)} reshape(bf16[3,16,3,3,64]{4,3,2,1,0:T(4,128)(2,1)S(1)} %copy.11) | data formatting | bytes 110592 | tf_op jit(solution)/shard_map/reshape | solution.py:149
  40.3 3.2 %collective-permute-start.6 = (bf16[2,4,32,512]{3,2,1,0:T(8,128)(2,1)S(1)}, bf16[2,4,32,512]{3,2,1,0:T(8,128)(2,1)S(1)}, u32[]{:S(2)}, u32[]{:S(2)}) collective-permute-start(bf16[2,4,32,512]{3,2,1,0:T(8,128)(2,1)S(1)} %constant_dynamic-update-slice_fusion), channel_id=1, source_target_pairs={{0,32},{4,36},{8,40},{12,44},{16,48},{20,52},{24,56},{28,60},{32,6... | collective-permute-start | bytes 786440 | tf_op jit(solution)/shard_map/ppermute | solution.py:15
  43.5 0.3 collective-permute-start.5
  43.8 0.3 collective-permute-start.3
  44.1 0.7 pad_maximum_fusion
  44.8 0.4 collective-permute-done.7
  45.2 0.7 %fusion.3 = (bf16[2,2,32,512]{3,2,1,0:T(8,128)(2,1)}, bf16[2,2,32,512]{3,2,1,0:T(8,128)(2,1)}) fusion(bf16[2,4,32,512]{3,2,1,0:T(8,128)(2,1)S(1)} %collective-permute-done.7), kind=kLoop, calls=%fused_computation.15 | loop fusion | bytes 524288 | tf_op jit(solution)/shard_map/slice | solution.py:47
  45.9 5.9 %collective-permute-done.6 = bf16[2,4,32,512]{3,2,1,0:T(8,128)(2,1)S(1)} collective-permute-done((bf16[2,4,32,512]{3,2,1,0:T(8,128)(2,1)S(1)}, bf16[2,4,32,512]{3,2,1,0:T(8,128)(2,1)S(1)}, u32[]{:S(2)}, u32[]{:S(2)}) %collective-permute-start.6) | collective-permute-done | bytes 262176 | tf_op jit(solution)/shard_map/ppermute | solution.py:15
  51.8 0.7 %fusion.4 = (bf16[2,2,32,512]{3,2,1,0:T(8,128)(2,1)}, bf16[2,2,32,512]{3,2,1,0:T(8,128)(2,1)}) fusion(bf16[2,4,32,512]{3,2,1,0:T(8,128)(2,1)S(1)} %collective-permute-done.6), kind=kLoop, calls=%fused_computation.16 | loop fusion | bytes 524288 | tf_op jit(solution)/shard_map/slice | solution.py:46
  52.5 0.8 %copy-done.3 = bf16[2,8,32,512]{3,2,1,0:T(8,128)(2,1)} copy-done((bf16[2,8,32,512]{3,2,1,0:T(8,128)(2,1)}, bf16[2,8,32,512]{3,2,1,0:T(8,128)(2,1)S(1)}, u32[]{:S(2)}) %copy-start.3) | copy-done | bytes 524312
  53.3 0.2 copy-done.4
  53.5 14.0 %shard_map.37 = bf16[2,16,16,512]{3,2,1,0:T(8,128)(2,1)} custom-call(s32[72]{0:T(128)} %reshape.24.keep_ref, s32[5]{0:T(128)} %pad_add_fusion.place_ref, bf16[2,16,32,512]{3,2,1,0:T(8,128)(2,1)} %bitcast.15, bf16[2,2,32,512]{3,2,1,0:T(8,128)(2,1)} %copy-done.6, bf16[2,2,32,512]{3,2,1,0:T(8,128)(2,1)} %copy-done.5, bf16[2,8,32,512]{3,2,1,0:T(8,128)(2,1)} %copy-done.2, ...), custom_call_target="tpu_custom_call" | custom-call | tf_op jit(solution)/shard_map/pallas_call | solution.py:135
  67.5 2.1 %copy.12 = bf16[16,2,16,512]{3,2,1,0:T(8,128)(2,1)} copy(bf16[16,2,16,512]{3,0,2,1:T(8,128)(2,1)} %bitcast.16) | data formatting | bytes 1048576 | tf_op jit(solution)/shard_map/transpose | solution.py:182
  (38 shorter events, 0.6 us)
Async XLA Ops:
  1.8 19.0 %copy-start = (bf16[32,2,16,512]{3,0,2,1:T(8,128)(2,1)}, bf16[32,2,16,512]{3,0,2,1:T(8,128)(2,1)S(1)}, u32[]{:S(2)}) copy-start(bf16[32,2,16,512]{3,0,2,1:T(8,128)(2,1)S(1)} %copy.15) | copy-start | bytes 3145732
  1.8 6.1 %copy-start.8 = (bf16[3,3,3,16,32]{4,3,2,1,0:T(8,128)(2,1)S(1)}, bf16[3,3,3,16,32]{4,3,2,1,0:T(8,128)(2,1)}, u32[]{:S(2)}) copy-start(bf16[3,3,3,16,32]{4,3,2,1,0:T(8,128)(2,1)} %param.4) | copy-start | bytes 82948
  1.9 41.6 %collective-permute-start.4 = (bf16[2,8,32,512]{3,2,1,0:T(8,128)(2,1)S(1)}, bf16[2,8,32,512]{3,2,1,0:T(8,128)(2,1)S(1)}, u32[]{:S(2)}, u32[]{:S(2)}) collective-permute-start(bf16[2,8,32,512]{3,2,1,0:T(8,128)(2,1)S(1)} %dynamic-slice_bitcast_fusion), channel_id=1, source_target_pairs={{0,224},{4,228},{8,232},{12,236},{16,240},{20,244},{24,248},{28,25... | collective-permute-start | bytes 1572872 | tf_op jit(solution)/shard_map/ppermute | solution.py:15
  7.9 35.9 %collective-permute-start.2 = (bf16[2,8,32,512]{3,2,1,0:T(8,128)(2,1)S(1)}, bf16[2,8,32,512]{3,2,1,0:T(8,128)(2,1)S(1)}, u32[]{:S(2)}, u32[]{:S(2)}) collective-permute-start(bf16[2,8,32,512]{3,2,1,0:T(8,128)(2,1)S(1)} %dynamic-slice_bitcast_fusion), channel_id=1, source_target_pairs={{0,32},{4,36},{8,40},{12,44},{16,48},{20,52},{24,56},{28,60},{32,6... | collective-permute-start | bytes 1572872 | tf_op jit(solution)/shard_map/ppermute | solution.py:15
  8.1 28.9 %collective-permute-start.10 = (bf16[3,16,288]{2,1,0:T(8,128)(2,1)S(1)}, bf16[3,16,288]{2,1,0:T(8,128)(2,1)S(1)}, u32[]{:S(2)}, u32[]{:S(2)}) collective-permute-start(bf16[3,16,288]{2,1,0:T(8,128)(2,1)S(1)} %reshape.21), channel_id=1, source_target_pairs={{0,1},{1,2},{2,3},{3,0},{4,5},{5,6},{6,7},{7,4},{8,9},{9,10},{10,1... | collective-permute-start | bytes 82952 | tf_op jit(solution)/shard_map/ppermute | solution.py:15
  10.6 10.2 %copy-start.7 = (bf16[3,3,3,16,64]{4,3,2,1,0:T(8,128)(2,1)S(1)}, bf16[3,3,3,16,64]{4,3,2,1,0:T(8,128)(2,1)}, u32[]{:S(2)}) copy-start(bf16[3,3,3,16,64]{4,3,2,1,0:T(8,128)(2,1)} %param.5) | copy-start | bytes 165892
  10.7 25.6 %collective-permute-start.1 = (bf16[2,2,32,512]{3,2,1,0:T(8,128)(2,1)S(1)}, bf16[2,2,32,512]{3,2,1,0:T(8,128)(2,1)S(1)}, u32[]{:S(2)}, u32[]{:S(2)}) collective-permute-start(bf16[2,2,32,512]{3,2,1,0:T(8,128)(2,1)S(1)} %get-tuple-element.7), channel_id=1, source_target_pairs={{0,252},{4,0},{8,4},{12,8},{16,12},{20,16},{24,20},{28,24},{32,28}... | collective-permute-start | bytes 393224 | tf_op jit(solution)/shard_map/ppermute | solution.py:15
  20.8 14.0 %collective-permute-start = (bf16[2,2,32,512]{3,2,1,0:T(8,128)(2,1)S(1)}, bf16[2,2,32,512]{3,2,1,0:T(8,128)(2,1)S(1)}, u32[]{:S(2)}, u32[]{:S(2)}) collective-permute-start(bf16[2,2,32,512]{3,2,1,0:T(8,128)(2,1)S(1)} %get-tuple-element.8), channel_id=1, source_target_pairs={{0,4},{4,8},{8,12},{12,16},{16,20},{20,24},{24,28},{28,32},{32,36}... | collective-permute-start | bytes 393224 | tf_op jit(solution)/shard_map/ppermute | solution.py:15
  34.7 1.6 %copy-start.6 = (bf16[2,2,32,512]{3,2,1,0:T(8,128)(2,1)}, bf16[2,2,32,512]{3,2,1,0:T(8,128)(2,1)S(1)}, u32[]{:S(2)}) copy-start(bf16[2,2,32,512]{3,2,1,0:T(8,128)(2,1)S(1)} %collective-permute-done.above_ref) | copy-start | bytes 393220
  34.7 5.5 %collective-permute-start.9 = (bf16[3,16,288]{2,1,0:T(8,128)(2,1)S(1)}, bf16[3,16,288]{2,1,0:T(8,128)(2,1)S(1)}, u32[]{:S(2)}, u32[]{:S(2)}) collective-permute-start(bf16[3,16,288]{2,1,0:T(8,128)(2,1)S(1)} %reshape.21), channel_id=1, source_target_pairs={{0,2},{1,3},{2,0},{3,1},{4,6},{5,7},{6,4},{7,5},{8,10},{9,11},{10,... | collective-permute-start | bytes 82952 | tf_op jit(solution)/shard_map/ppermute | solution.py:15
  36.3 0.6 copy-start.5
  37.0 8.2 %collective-permute-start.7 = (bf16[2,4,32,512]{3,2,1,0:T(8,128)(2,1)S(1)}, bf16[2,4,32,512]{3,2,1,0:T(8,128)(2,1)S(1)}, u32[]{:S(2)}, u32[]{:S(2)}) collective-permute-start(bf16[2,4,32,512]{3,2,1,0:T(8,128)(2,1)S(1)} %constant_dynamic-update-slice_fusion), channel_id=1, source_target_pairs={{0,224},{4,228},{8,232},{12,236},{16,240},{20,244},{24,248},{28,25... | collective-permute-start | bytes 786440 | tf_op jit(solution)/shard_map/ppermute | solution.py:15
  37.0 7.1 %collective-permute-start.8 = (bf16[3,16,288]{2,1,0:T(8,128)(2,1)S(1)}, bf16[3,16,288]{2,1,0:T(8,128)(2,1)S(1)}, u32[]{:S(2)}, u32[]{:S(2)}) collective-permute-start(bf16[3,16,288]{2,1,0:T(8,128)(2,1)S(1)} %reshape.21), channel_id=1, source_target_pairs={{0,3},{1,0},{2,1},{3,2},{4,7},{5,4},{6,5},{7,6},{8,11},{9,8},{10,9... | collective-permute-start | bytes 82952 | tf_op jit(solution)/shard_map/ppermute | solution.py:15
  40.3 11.5 %collective-permute-start.6 = (bf16[2,4,32,512]{3,2,1,0:T(8,128)(2,1)S(1)}, bf16[2,4,32,512]{3,2,1,0:T(8,128)(2,1)S(1)}, u32[]{:S(2)}, u32[]{:S(2)}) collective-permute-start(bf16[2,4,32,512]{3,2,1,0:T(8,128)(2,1)S(1)} %constant_dynamic-update-slice_fusion), channel_id=1, source_target_pairs={{0,32},{4,36},{8,40},{12,44},{16,48},{20,52},{24,56},{28,60},{32,6... | collective-permute-start | bytes 786440 | tf_op jit(solution)/shard_map/ppermute | solution.py:15
  43.5 9.0 %copy-start.1 = (bf16[2,8,32,512]{3,2,1,0:T(8,128)(2,1)}, bf16[2,8,32,512]{3,2,1,0:T(8,128)(2,1)S(1)}, u32[]{:S(2)}) copy-start(bf16[2,8,32,512]{3,2,1,0:T(8,128)(2,1)S(1)} %collective-permute-done.4.bm_ref) | copy-start | bytes 1572868
  43.5 9.0 %collective-permute-start.5 = (bf16[2,8,32,512]{3,2,1,0:T(8,128)(2,1)S(1)}, bf16[2,8,32,512]{3,2,1,0:T(8,128)(2,1)S(1)}, u32[]{:S(2)}, u32[]{:S(2)}) collective-permute-start(bf16[2,8,32,512]{3,2,1,0:T(8,128)(2,1)S(1)} %collective-permute-done.4.bm_ref), channel_id=1, source_target_pairs={{0,1},{1,0},{2,3},{3,2},{4,5},{5,4},{6,7},{7,6},{8,9},{9,8},{10,11... | collective-permute-start | bytes 1572872 | tf_op jit(solution)/shard_map/ppermute | solution.py:27
  43.8 8.7 %copy-start.2 = (bf16[2,8,32,512]{3,2,1,0:T(8,128)(2,1)}, bf16[2,8,32,512]{3,2,1,0:T(8,128)(2,1)S(1)}, u32[]{:S(2)}) copy-start(bf16[2,8,32,512]{3,2,1,0:T(8,128)(2,1)S(1)} %collective-permute-done.2.fm_ref) | copy-start | bytes 1572868
  43.8 8.7 %collective-permute-start.3 = (bf16[2,8,32,512]{3,2,1,0:T(8,128)(2,1)S(1)}, bf16[2,8,32,512]{3,2,1,0:T(8,128)(2,1)S(1)}, u32[]{:S(2)}, u32[]{:S(2)}) collective-permute-start(bf16[2,8,32,512]{3,2,1,0:T(8,128)(2,1)S(1)} %collective-permute-done.2.fm_ref), channel_id=1, source_target_pairs={{0,1},{1,0},{2,3},{3,2},{4,5},{5,4},{6,7},{7,6},{8,9},{9,8},{10,11... | collective-permute-start | bytes 1572872 | tf_op jit(solution)/shard_map/ppermute | solution.py:27
  52.5 0.8 %copy-start.3 = (bf16[2,8,32,512]{3,2,1,0:T(8,128)(2,1)}, bf16[2,8,32,512]{3,2,1,0:T(8,128)(2,1)S(1)}, u32[]{:S(2)}) copy-start(bf16[2,8,32,512]{3,2,1,0:T(8,128)(2,1)S(1)} %collective-permute-done.5.bt_ref) | copy-start | bytes 1572868
  52.5 1.0 %copy-start.4 = (bf16[2,8,32,512]{3,2,1,0:T(8,128)(2,1)}, bf16[2,8,32,512]{3,2,1,0:T(8,128)(2,1)S(1)}, u32[]{:S(2)}) copy-start(bf16[2,8,32,512]{3,2,1,0:T(8,128)(2,1)S(1)} %collective-permute-done.3.ft_ref) | copy-start | bytes 1572868

commit v10 on v8

--- a/solution.py
+++ b/solution.py
@@ -104,7 +104,7 @@
     mid_count = w1_ref.shape[0] // 3
     out_count = w2_ref.shape[0] // 3
     hid_depth, hid_height = hid_ref.shape[0], hid_ref.shape[1]
-    out_depth, out_height = o_ref.shape[0], o_ref.shape[1]
+    out_depth, out_height = o_ref.shape[1], o_ref.shape[2]
 
     for d in range(hid_depth):
         def first(h, carry, d=d):
@@ -118,7 +118,7 @@
     for d in range(out_depth):
         def second(h, carry, d=d):
             y = jnp.maximum(conv_rows(hid_ref, w2_ref, d, h, out_count), 0.0)
-            o_ref[d, h] = y.astype(o_ref.dtype)
+            o_ref[:, d, h, :] = y.astype(o_ref.dtype)
             return carry
 
         lax.fori_loop(0, out_height, second, 0, unroll=True)
@@ -133,7 +133,7 @@
     smem = pl.BlockSpec(memory_space=pltpu.SMEM)
     return pl.pallas_call(
         two_layers_kernel,
-        out_shape=jax.ShapeDtypeStruct((depth, height, out_count, width), jnp.bfloat16),
+        out_shape=jax.ShapeDtypeStruct((out_count, depth, height, width), jnp.bfloat16),
         in_specs=[smem, smem] + [pl.BlockSpec(memory_space=vmem)] * (len(pieces) + 2),
         out_specs=pl.BlockSpec(memory_space=vmem),
         scratch_shapes=[
@@ -178,7 +178,7 @@
     all_first, second_filters = gathered_filters(first_filters, second_filters)
     keep = inside_flags(voxels.shape[1] + 2, voxels.shape[2] + 2)
     out = two_layers(keep, place, pieces, all_first, tap_matrices(second_filters))
-    return out.transpose(2, 0, 1, 3)
+    return out
 
 
 def solution(mesh):

time: 93.5 us -> 91.4 us (0.978)
  local copies, waits for them, and re-layouts: 8.26 us -> 6.11 us
    transpose x1 -> x0, local copies, waits for them, and re-layouts: 2.13 us -> none  [local(): return out.transpose(2, 0, 1, 3)]
where the time goes in v10:
time: 91.4 us; the launch traced here: 91.1 us
  starting transfers between devices  37.8 us (41%)
  waiting for transfers between devices  31.5 us (34%)
  Pallas kernels  14 us (15%)
  local copies, waits for them, and re-layouts  6.11 us (7%)
  other arithmetic  1.58 us (2%)
    ppermute x11, starting transfers between devices, passed_along(): return lax.ppermute(value, axis, pairs)  36.4 us
    ppermute x11, waiting for transfers between devices, passed_along(): return lax.ppermute(value, axis, pairs)  31.5 us
    pallas_call x1, Pallas kernels, two_layers(): pl.pallas_call(two_layers_kernel, out_shape=jax.ShapeDtypeStruct((out_cou...  14 us
    unnamed x27, local copies, waits for them, and re-layouts  2.79 us
  transfers between devices with their start and end apart: 13, of which 3 were waited for; matrix products, arithmetic and copies ran while one was open for 6% of the time, Pallas kernels for 0%

profile of v10, /device:TPU:1, one launch (start us, length us, event | category | flops | bytes accessed | tf_op | source)
XLA Modules:
  0.0 91.1 jit_solution(1224078575755748785)
XLA Ops:
  0.0 1.0 %copy.9 = bf16[3,16,3,3,32]{4,3,2,1,0:T(4,128)(2,1)S(1)} copy(bf16[3,16,3,3,32]{4,1,0,3,2:T(8,128)(2,1)} %bitcast.16) | data formatting | bytes 55296 | tf_op jit(solution)/shard_map/transpose | solution.py:166
  1.1 3.1 %collective-permute-start.12 = (bf16[3,16,288]{2,1,0:T(8,128)(2,1)S(1)}, bf16[3,16,288]{2,1,0:T(8,128)(2,1)S(1)}, u32[]{:S(2)}, u32[]{:S(2)}) collective-permute-start(bf16[3,16,288]{2,1,0:T(8,128)(2,1)S(1)} %reshape.21), channel_id=1, source_target_pairs={{0,1},{1,2},{2,3},{3,0},{4,5},{5,6},{6,7},{7,4},{8,9},{9,10},{10,1... | collective-permute-start | bytes 82952 | tf_op jit(solution)/shard_map/ppermute | solution.py:15
  4.2 1.5 %collective-permute-start.11 = (bf16[3,16,288]{2,1,0:T(8,128)(2,1)S(1)}, bf16[3,16,288]{2,1,0:T(8,128)(2,1)S(1)}, u32[]{:S(2)}, u32[]{:S(2)}) collective-permute-start(bf16[3,16,288]{2,1,0:T(8,128)(2,1)S(1)} %reshape.21), channel_id=1, source_target_pairs={{0,2},{1,3},{2,0},{3,1},{4,6},{5,7},{6,4},{7,5},{8,10},{9,11},{10,... | collective-permute-start | bytes 82952 | tf_op jit(solution)/shard_map/ppermute | solution.py:15
  5.7 1.8 %copy.13 = bf16[32,2,16,512]{3,0,2,1:T(8,128)(2,1)S(1)} copy(bf16[32,2,16,512]{3,2,1,0:T(8,128)(2,1)} %param.3) | data formatting | bytes 2097152 | tf_op args[0]
  7.6 4.1 %collective-permute-start.4 = (bf16[2,8,32,512]{3,2,1,0:T(8,128)(2,1)S(1)}, bf16[2,8,32,512]{3,2,1,0:T(8,128)(2,1)S(1)}, u32[]{:S(2)}, u32[]{:S(2)}) collective-permute-start(bf16[2,8,32,512]{3,2,1,0:T(8,128)(2,1)S(1)} %dynamic-slice_bitcast_fusion), channel_id=1, source_target_pairs={{0,224},{4,228},{8,232},{12,236},{16,240},{20,244},{24,248},{28,25... | collective-permute-start | bytes 1572872 | tf_op jit(solution)/shard_map/ppermute | solution.py:15
  11.8 0.7 fusion.2
  12.5 21.0 %collective-permute-done.4.bm_ref = bf16[2,8,32,512]{3,2,1,0:T(8,128)(2,1)S(1)} collective-permute-done((bf16[2,8,32,512]{3,2,1,0:T(8,128)(2,1)S(1)}, bf16[2,8,32,512]{3,2,1,0:T(8,128)(2,1)S(1)}, u32[]{:S(2)}, u32[]{:S(2)}) %collective-permute-start.4) | collective-permute-done | bytes 524320 | tf_op jit(solution)/shard_map/ppermute | solution.py:15
  33.5 1.3 %collective-permute-start.5 = (bf16[2,8,32,512]{3,2,1,0:T(8,128)(2,1)S(1)}, bf16[2,8,32,512]{3,2,1,0:T(8,128)(2,1)S(1)}, u32[]{:S(2)}, u32[]{:S(2)}) collective-permute-start(bf16[2,8,32,512]{3,2,1,0:T(8,128)(2,1)S(1)} %collective-permute-done.4.bm_ref), channel_id=1, source_target_pairs={{0,1},{1,0},{2,3},{3,2},{4,5},{5,4},{6,7},{7,6},{8,9},{9,8},{10,11... | collective-permute-start | bytes 1572872 | tf_op jit(solution)/shard_map/ppermute | solution.py:27
  34.9 7.5 %collective-permute-start.9 = (bf16[2,2,32,512]{3,2,1,0:T(8,128)(2,1)}, bf16[2,2,32,512]{3,2,1,0:T(8,128)(2,1)S(1)}, u32[]{:S(2)}, u32[]{:S(2)}) collective-permute-start(bf16[2,2,32,512]{3,2,1,0:T(8,128)(2,1)} %get-tuple-element.7), channel_id=1, source_target_pairs={{0,220},{4,224},{8,228},{12,232},{16,236},{20,240},{24,244},{28,24... | collective-permute-start | bytes 393224 | tf_op jit(solution)/shard_map/ppermute | solution.py:15
  42.5 3.8 %collective-permute-start.7 = (bf16[2,2,32,512]{3,2,1,0:T(8,128)(2,1)}, bf16[2,2,32,512]{3,2,1,0:T(8,128)(2,1)}, u32[]{:S(2)}, u32[]{:S(2)}) collective-permute-start(bf16[2,2,32,512]{3,2,1,0:T(8,128)(2,1)} %get-tuple-element.7), channel_id=1, source_target_pairs={{0,28},{4,32},{8,36},{12,40},{16,44},{20,48},{24,52},{28,56},{32,6... | collective-permute-start | bytes 393224 | tf_op jit(solution)/shard_map/ppermute | solution.py:15
  46.2 4.3 %collective-permute-start.1 = (bf16[2,2,32,512]{3,2,1,0:T(8,128)(2,1)}, bf16[2,2,32,512]{3,2,1,0:T(8,128)(2,1)}, u32[]{:S(2)}, u32[]{:S(2)}) collective-permute-start(bf16[2,2,32,512]{3,2,1,0:T(8,128)(2,1)} %get-tuple-element.7), channel_id=1, source_target_pairs={{0,252},{4,0},{8,4},{12,8},{16,12},{20,16},{24,20},{28,24},{32,28}... | collective-permute-start | bytes 393224 | tf_op jit(solution)/shard_map/ppermute | solution.py:15
  50.6 0.2 fusion
  50.8 6.2 %collective-permute-start.8 = (bf16[2,2,32,512]{3,2,1,0:T(8,128)(2,1)}, bf16[2,2,32,512]{3,2,1,0:T(8,128)(2,1)}, u32[]{:S(2)}, u32[]{:S(2)}) collective-permute-start(bf16[2,2,32,512]{3,2,1,0:T(8,128)(2,1)} %get-tuple-element.8), channel_id=1, source_target_pairs={{0,228},{4,232},{8,236},{12,240},{16,244},{20,248},{24,252},{28,0}... | collective-permute-start | bytes 393224 | tf_op jit(solution)/shard_map/ppermute | solution.py:15
  57.0 3.2 %collective-permute-start.6 = (bf16[2,2,32,512]{3,2,1,0:T(8,128)(2,1)}, bf16[2,2,32,512]{3,2,1,0:T(8,128)(2,1)}, u32[]{:S(2)}, u32[]{:S(2)}) collective-permute-start(bf16[2,2,32,512]{3,2,1,0:T(8,128)(2,1)} %get-tuple-element.8), channel_id=1, source_target_pairs={{0,36},{4,40},{8,44},{12,48},{16,52},{20,56},{24,60},{28,64},{32,6... | collective-permute-start | bytes 393224 | tf_op jit(solution)/shard_map/ppermute | solution.py:15
  60.2 2.7 %collective-permute-start = (bf16[2,2,32,512]{3,2,1,0:T(8,128)(2,1)}, bf16[2,2,32,512]{3,2,1,0:T(8,128)(2,1)}, u32[]{:S(2)}, u32[]{:S(2)}) collective-permute-start(bf16[2,2,32,512]{3,2,1,0:T(8,128)(2,1)} %get-tuple-element.8), channel_id=1, source_target_pairs={{0,4},{4,8},{8,12},{12,16},{16,20},{20,24},{24,28},{28,32},{32,36}... | collective-permute-start | bytes 393224 | tf_op jit(solution)/shard_map/ppermute | solution.py:15
  62.9 0.6 pad_add_fusion.place_ref
  63.5 0.7 reshape.24.keep_ref
  64.3 0.8 reshape.23.w2_ref
  65.0 0.7 pad_maximum_fusion
  65.7 2.0 %collective-permute-done.6.fa_ref = bf16[2,2,32,512]{3,2,1,0:T(8,128)(2,1)} collective-permute-done((bf16[2,2,32,512]{3,2,1,0:T(8,128)(2,1)}, bf16[2,2,32,512]{3,2,1,0:T(8,128)(2,1)}, u32[]{:S(2)}, u32[]{:S(2)}) %collective-permute-start.6) | collective-permute-done | bytes 131104 | tf_op jit(solution)/shard_map/ppermute | solution.py:15
  67.7 8.5 %collective-permute-done.above_ref = bf16[2,2,32,512]{3,2,1,0:T(8,128)(2,1)} collective-permute-done((bf16[2,2,32,512]{3,2,1,0:T(8,128)(2,1)}, bf16[2,2,32,512]{3,2,1,0:T(8,128)(2,1)}, u32[]{:S(2)}, u32[]{:S(2)}) %collective-permute-start) | collective-permute-done | bytes 131104 | tf_op jit(solution)/shard_map/ppermute | solution.py:15
  76.2 0.8 copy-done.3
  77.0 0.2 copy-done.4
  77.2 14.0 %shard_map.37 = bf16[16,2,16,512]{3,2,1,0:T(8,128)(2,1)} custom-call(s32[72]{0:T(128)} %reshape.24.keep_ref, s32[5]{0:T(128)} %pad_add_fusion.place_ref, bf16[2,16,32,512]{3,2,1,0:T(8,128)(2,1)} %bitcast.14, bf16[2,2,32,512]{3,2,1,0:T(8,128)(2,1)} %collective-permute-done.above_ref, bf16[2,2,32,512]{3,2,1,0:T(8,128)(2,1)} %collective-permute-done.1.below_ref, ...), custom_call_target="tpu_custom_call" | custom-call | tf_op jit(solution)/shard_map/pallas_call | solution.py:134
  (45 shorter events, 0.6 us)
Async XLA Ops:
  1.1 33.8 %collective-permute-start.12 = (bf16[3,16,288]{2,1,0:T(8,128)(2,1)S(1)}, bf16[3,16,288]{2,1,0:T(8,128)(2,1)S(1)}, u32[]{:S(2)}, u32[]{:S(2)}) collective-permute-start(bf16[3,16,288]{2,1,0:T(8,128)(2,1)S(1)} %reshape.21), channel_id=1, source_target_pairs={{0,1},{1,2},{2,3},{3,0},{4,5},{5,6},{6,7},{7,4},{8,9},{9,10},{10,1... | collective-permute-start | bytes 82952 | tf_op jit(solution)/shard_map/ppermute | solution.py:15
  4.2 38.3 %collective-permute-start.11 = (bf16[3,16,288]{2,1,0:T(8,128)(2,1)S(1)}, bf16[3,16,288]{2,1,0:T(8,128)(2,1)S(1)}, u32[]{:S(2)}, u32[]{:S(2)}) collective-permute-start(bf16[3,16,288]{2,1,0:T(8,128)(2,1)S(1)} %reshape.21), channel_id=1, source_target_pairs={{0,2},{1,3},{2,0},{3,1},{4,6},{5,7},{6,4},{7,5},{8,10},{9,11},{10,... | collective-permute-start | bytes 82952 | tf_op jit(solution)/shard_map/ppermute | solution.py:15
  5.7 40.5 %collective-permute-start.10 = (bf16[3,16,288]{2,1,0:T(8,128)(2,1)S(1)}, bf16[3,16,288]{2,1,0:T(8,128)(2,1)S(1)}, u32[]{:S(2)}, u32[]{:S(2)}) collective-permute-start(bf16[3,16,288]{2,1,0:T(8,128)(2,1)S(1)} %reshape.21), channel_id=1, source_target_pairs={{0,3},{1,0},{2,1},{3,2},{4,7},{5,4},{6,5},{7,6},{8,11},{9,8},{10,9... | collective-permute-start | bytes 82952 | tf_op jit(solution)/shard_map/ppermute | solution.py:15
  7.5 56.7 %copy-start = (bf16[32,2,16,512]{3,0,2,1:T(8,128)(2,1)}, bf16[32,2,16,512]{3,0,2,1:T(8,128)(2,1)S(1)}, u32[]{:S(2)}) copy-start(bf16[32,2,16,512]{3,0,2,1:T(8,128)(2,1)S(1)} %copy.13) | copy-start | bytes 3145732
  7.6 25.9 %collective-permute-start.4 = (bf16[2,8,32,512]{3,2,1,0:T(8,128)(2,1)S(1)}, bf16[2,8,32,512]{3,2,1,0:T(8,128)(2,1)S(1)}, u32[]{:S(2)}, u32[]{:S(2)}) collective-permute-start(bf16[2,8,32,512]{3,2,1,0:T(8,128)(2,1)S(1)} %dynamic-slice_bitcast_fusion), channel_id=1, source_target_pairs={{0,224},{4,228},{8,232},{12,236},{16,240},{20,244},{24,248},{28,25... | collective-permute-start | bytes 1572872 | tf_op jit(solution)/shard_map/ppermute | solution.py:15
  11.7 23.0 %collective-permute-start.2 = (bf16[2,8,32,512]{3,2,1,0:T(8,128)(2,1)S(1)}, bf16[2,8,32,512]{3,2,1,0:T(8,128)(2,1)S(1)}, u32[]{:S(2)}, u32[]{:S(2)}) collective-permute-start(bf16[2,8,32,512]{3,2,1,0:T(8,128)(2,1)S(1)} %dynamic-slice_bitcast_fusion), channel_id=1, source_target_pairs={{0,32},{4,36},{8,40},{12,44},{16,48},{20,52},{24,56},{28,60},{32,6... | collective-permute-start | bytes 1572872 | tf_op jit(solution)/shard_map/ppermute | solution.py:15
  11.8 38.8 %copy-start.6 = (bf16[3,3,3,16,64]{4,3,2,1,0:T(8,128)(2,1)S(1)}, bf16[3,3,3,16,64]{4,3,2,1,0:T(8,128)(2,1)}, u32[]{:S(2)}) copy-start(bf16[3,3,3,16,64]{4,3,2,1,0:T(8,128)(2,1)} %param.5) | copy-start | bytes 165892
  33.5 42.7 %copy-start.1 = (bf16[2,8,32,512]{3,2,1,0:T(8,128)(2,1)}, bf16[2,8,32,512]{3,2,1,0:T(8,128)(2,1)S(1)}, u32[]{:S(2)}) copy-start(bf16[2,8,32,512]{3,2,1,0:T(8,128)(2,1)S(1)} %collective-permute-done.4.bm_ref) | copy-start | bytes 1572868
  33.5 42.7 %collective-permute-start.5 = (bf16[2,8,32,512]{3,2,1,0:T(8,128)(2,1)S(1)}, bf16[2,8,32,512]{3,2,1,0:T(8,128)(2,1)S(1)}, u32[]{:S(2)}, u32[]{:S(2)}) collective-permute-start(bf16[2,8,32,512]{3,2,1,0:T(8,128)(2,1)S(1)} %collective-permute-done.4.bm_ref), channel_id=1, source_target_pairs={{0,1},{1,0},{2,3},{3,2},{4,5},{5,4},{6,7},{7,6},{8,9},{9,8},{10,11... | collective-permute-start | bytes 1572872 | tf_op jit(solution)/shard_map/ppermute | solution.py:27
  34.8 41.5 %copy-start.2 = (bf16[2,8,32,512]{3,2,1,0:T(8,128)(2,1)}, bf16[2,8,32,512]{3,2,1,0:T(8,128)(2,1)S(1)}, u32[]{:S(2)}) copy-start(bf16[2,8,32,512]{3,2,1,0:T(8,128)(2,1)S(1)} %collective-permute-done.2.fm_ref) | copy-start | bytes 1572868
  34.8 41.5 %collective-permute-start.3 = (bf16[2,8,32,512]{3,2,1,0:T(8,128)(2,1)S(1)}, bf16[2,8,32,512]{3,2,1,0:T(8,128)(2,1)S(1)}, u32[]{:S(2)}, u32[]{:S(2)}) collective-permute-start(bf16[2,8,32,512]{3,2,1,0:T(8,128)(2,1)S(1)} %collective-permute-done.2.fm_ref), channel_id=1, source_target_pairs={{0,1},{1,0},{2,3},{3,2},{4,5},{5,4},{6,7},{7,6},{8,9},{9,8},{10,11... | collective-permute-start | bytes 1572872 | tf_op jit(solution)/shard_map/ppermute | solution.py:27
  34.9 15.6 %copy-start.7 = (bf16[3,16,288]{2,1,0:T(8,128)(2,1)}, bf16[3,16,288]{2,1,0:T(8,128)(2,1)S(1)}, u32[]{:S(2)}) copy-start(bf16[3,16,288]{2,1,0:T(8,128)(2,1)S(1)} %collective-permute-done.12) | copy-start | bytes 82948
  34.9 15.8 %collective-permute-start.9 = (bf16[2,2,32,512]{3,2,1,0:T(8,128)(2,1)}, bf16[2,2,32,512]{3,2,1,0:T(8,128)(2,1)S(1)}, u32[]{:S(2)}, u32[]{:S(2)}) collective-permute-start(bf16[2,2,32,512]{3,2,1,0:T(8,128)(2,1)} %get-tuple-element.7), channel_id=1, source_target_pairs={{0,220},{4,224},{8,228},{12,232},{16,236},{20,240},{24,244},{28,24... | collective-permute-start | bytes 393224 | tf_op jit(solution)/shard_map/ppermute | solution.py:15
  42.5 8.1 %copy-start.9 = (bf16[3,16,288]{2,1,0:T(8,128)(2,1)}, bf16[3,16,288]{2,1,0:T(8,128)(2,1)S(1)}, u32[]{:S(2)}) copy-start(bf16[3,16,288]{2,1,0:T(8,128)(2,1)S(1)} %collective-permute-done.11) | copy-start | bytes 82948
  42.5 14.5 %collective-permute-start.7 = (bf16[2,2,32,512]{3,2,1,0:T(8,128)(2,1)}, bf16[2,2,32,512]{3,2,1,0:T(8,128)(2,1)}, u32[]{:S(2)}, u32[]{:S(2)}) collective-permute-start(bf16[2,2,32,512]{3,2,1,0:T(8,128)(2,1)} %get-tuple-element.7), channel_id=1, source_target_pairs={{0,28},{4,32},{8,36},{12,40},{16,44},{20,48},{24,52},{28,56},{32,6... | collective-permute-start | bytes 393224 | tf_op jit(solution)/shard_map/ppermute | solution.py:15
  46.2 4.3 %copy-start.11 = (bf16[3,16,288]{2,1,0:T(8,128)(2,1)}, bf16[3,16,288]{2,1,0:T(8,128)(2,1)S(1)}, u32[]{:S(2)}) copy-start(bf16[3,16,288]{2,1,0:T(8,128)(2,1)S(1)} %collective-permute-done.10) | copy-start | bytes 82948
  46.2 13.9 %collective-permute-start.1 = (bf16[2,2,32,512]{3,2,1,0:T(8,128)(2,1)}, bf16[2,2,32,512]{3,2,1,0:T(8,128)(2,1)}, u32[]{:S(2)}, u32[]{:S(2)}) collective-permute-start(bf16[2,2,32,512]{3,2,1,0:T(8,128)(2,1)} %get-tuple-element.7), channel_id=1, source_target_pairs={{0,252},{4,0},{8,4},{12,8},{16,12},{20,16},{24,20},{28,24},{32,28}... | collective-permute-start | bytes 393224 | tf_op jit(solution)/shard_map/ppermute | solution.py:15
  50.8 12.7 %copy-start.5 = (bf16[2,2,32,512]{3,2,1,0:T(8,128)(2,1)}, bf16[2,2,32,512]{3,2,1,0:T(8,128)(2,1)S(1)}, u32[]{:S(2)}) copy-start(bf16[2,2,32,512]{3,2,1,0:T(8,128)(2,1)S(1)} %collective-permute-done.9.bb_ref) | copy-start | bytes 393220
  50.8 14.9 %collective-permute-start.8 = (bf16[2,2,32,512]{3,2,1,0:T(8,128)(2,1)}, bf16[2,2,32,512]{3,2,1,0:T(8,128)(2,1)}, u32[]{:S(2)}, u32[]{:S(2)}) collective-permute-start(bf16[2,2,32,512]{3,2,1,0:T(8,128)(2,1)} %get-tuple-element.8), channel_id=1, source_target_pairs={{0,228},{4,232},{8,236},{12,240},{16,244},{20,248},{24,252},{28,0}... | collective-permute-start | bytes 393224 | tf_op jit(solution)/shard_map/ppermute | solution.py:15
  57.0 10.7 %collective-permute-start.6 = (bf16[2,2,32,512]{3,2,1,0:T(8,128)(2,1)}, bf16[2,2,32,512]{3,2,1,0:T(8,128)(2,1)}, u32[]{:S(2)}, u32[]{:S(2)}) collective-permute-start(bf16[2,2,32,512]{3,2,1,0:T(8,128)(2,1)} %get-tuple-element.8), channel_id=1, source_target_pairs={{0,36},{4,40},{8,44},{12,48},{16,52},{20,56},{24,60},{28,64},{32,6... | collective-permute-start | bytes 393224 | tf_op jit(solution)/shard_map/ppermute | solution.py:15
  60.2 16.0 %collective-permute-start = (bf16[2,2,32,512]{3,2,1,0:T(8,128)(2,1)}, bf16[2,2,32,512]{3,2,1,0:T(8,128)(2,1)}, u32[]{:S(2)}, u32[]{:S(2)}) collective-permute-start(bf16[2,2,32,512]{3,2,1,0:T(8,128)(2,1)} %get-tuple-element.8), channel_id=1, source_target_pairs={{0,4},{4,8},{8,12},{12,16},{16,20},{20,24},{24,28},{28,32},{32,36}... | collective-permute-start | bytes 393224 | tf_op jit(solution)/shard_map/ppermute | solution.py:15
  64.2 0.8 copy-start.8
  76.2 0.8 copy-start.3
  76.2 1.0 %copy-start.4 = (bf16[2,8,32,512]{3,2,1,0:T(8,128)(2,1)}, bf16[2,8,32,512]{3,2,1,0:T(8,128)(2,1)S(1)}, u32[]{:S(2)}) copy-start(bf16[2,8,32,512]{3,2,1,0:T(8,128)(2,1)S(1)} %collective-permute-done.3.ft_ref) | copy-start | bytes 1572868
  (2 other events, 1.6 us)

commit v11 on v10

--- a/solution.py
+++ b/solution.py
@@ -21,11 +21,13 @@
     return position % GH, position // GH, tile_count // GH
 
 
-def shared_along(mine, steps):
-    mine = passed_along(mine, "space", steps)
+def shared_along(mine):
+    front = passed_along(mine, "space", GH)
+    back = passed_along(mine, "space", -GH)
+    both = jnp.stack([front, back])
     count = lax.axis_size("chan")
-    theirs = lax.ppermute(mine, "chan", [(source, source ^ 1) for source in range(count)])
-    return mine, theirs
+    theirs = lax.ppermute(both, "chan", [(source, source ^ 1) for source in range(count)])
+    return (front, theirs[0]), (back, theirs[1])
 
 
 def halo_pieces(voxels, rim):
@@ -33,8 +35,7 @@
     core = lax.axis_index("chan") % 2
     half = voxels.shape[2] // 2
     mine = lax.dynamic_slice_in_dim(voxels, core * half, half, 2).transpose(1, 2, 0, 3)
-    front = shared_along(mine, GH)
-    back = shared_along(mine, -GH)
+    front, back = shared_along(mine)
     volume_tile = voxels.transpose(1, 2, 0, 3)
     top = volume_tile[:, -rim:]
     bottom = volume_tile[:, :rim]

time: 91.4 us -> 79.4 us (0.87)
  starting transfers between devices: 37.8 us -> 28.7 us
  waiting for transfers between devices: 31.5 us -> 27.8 us
  other arithmetic: 1.58 us -> 2.79 us
    ppermute x11, starting transfers between devices: 36.4 us -> 28.2 us  [passed_along(): return lax.ppermute(value, axis, pairs)]
    ppermute x11, waiting for transfers between devices: 31.5 us -> 27.8 us  [passed_along(): return lax.ppermute(value, axis, pairs)]
    another operation x0 -> x1, other arithmetic: none -> 1.14 us  [shared_along(): both = jnp.stack([front, back])]
    squeeze x0 -> x1, local copies, waits for them, and re-layouts: none -> 1.05 us  [shared_along(): return ((front, theirs[0]), (back, theirs[1]))]
    unnamed x27 -> x23, local copies, waits for them, and re-layouts: 2.79 us -> 2.47 us
  transfers between devices with their start and end apart: 13 -> 12, of which waited for: 3 -> 5; matrix products, arithmetic and copies ran while one was open for 6% -> 7% of each run, Pallas kernels for 0% -> 0%
where the time goes in v11:
time: 79.4 us; the launch traced here: 78.6 us
  starting transfers between devices  28.7 us (36%)
  waiting for transfers between devices  27.8 us (35%)
  Pallas kernels  14 us (18%)
  local copies, waits for them, and re-layouts  5.26 us (7%)
  other arithmetic  2.79 us (4%)
    ppermute x11, starting transfers between devices, passed_along(): return lax.ppermute(value, axis, pairs)  28.2 us
    ppermute x11, waiting for transfers between devices, passed_along(): return lax.ppermute(value, axis, pairs)  27.8 us
    pallas_call x1, Pallas kernels, two_layers(): pl.pallas_call(two_layers_kernel, out_shape=jax.ShapeDtypeStruct((out_cou...  14 us
    unnamed x23, local copies, waits for them, and re-layouts  2.47 us
  transfers between devices with their start and end apart: 12, of which 5 were waited for; matrix products, arithmetic and copies ran while one was open for 7% of the time, Pallas kernels for 0%

profile of v11, /device:TPU:1, one launch (start us, length us, event | category | flops | bytes accessed | tf_op | source)
XLA Modules:
  0.0 78.6 jit_solution(15714636965817119889)
XLA Ops:
  0.0 1.8 %copy.13 = bf16[32,2,16,512]{3,0,2,1:T(8,128)(2,1)S(1)} copy(bf16[32,2,16,512]{3,2,1,0:T(8,128)(2,1)} %param.3) | data formatting | bytes 2097152 | tf_op args[0]
  1.9 3.8 %collective-permute-start.2 = (bf16[2,8,32,512]{3,2,1,0:T(8,128)(2,1)S(1)}, bf16[2,8,32,512]{3,2,1,0:T(8,128)(2,1)S(1)}, u32[]{:S(2)}, u32[]{:S(2)}) collective-permute-start(bf16[2,8,32,512]{3,2,1,0:T(8,128)(2,1)S(1)} %dynamic-slice_bitcast_fusion), channel_id=1, source_target_pairs={{0,32},{4,36},{8,40},{12,44},{16,48},{20,52},{24,56},{28,60},{32,6... | collective-permute-start | bytes 1572872 | tf_op jit(solution)/shard_map/ppermute | solution.py:15
  5.7 2.3 %collective-permute-start.3 = (bf16[2,8,32,512]{3,2,1,0:T(8,128)(2,1)S(1)}, bf16[2,8,32,512]{3,2,1,0:T(8,128)(2,1)S(1)}, u32[]{:S(2)}, u32[]{:S(2)}) collective-permute-start(bf16[2,8,32,512]{3,2,1,0:T(8,128)(2,1)S(1)} %dynamic-slice_bitcast_fusion), channel_id=1, source_target_pairs={{0,224},{4,228},{8,232},{12,236},{16,240},{20,244},{24,248},{28,25... | collective-permute-start | bytes 1572872 | tf_op jit(solution)/shard_map/ppermute | solution.py:15
  8.2 1.7 %collective-permute-start.10 = (bf16[3,16,288]{2,1,0:T(8,128)(2,1)S(1)}, bf16[3,16,288]{2,1,0:T(8,128)(2,1)S(1)}, u32[]{:S(2)}, u32[]{:S(2)}) collective-permute-start(bf16[3,16,288]{2,1,0:T(8,128)(2,1)S(1)} %reshape.21), channel_id=1, source_target_pairs={{0,2},{1,3},{2,0},{3,1},{4,6},{5,7},{6,4},{7,5},{8,10},{9,11},{10,... | collective-permute-start | bytes 82952 | tf_op jit(solution)/shard_map/ppermute | solution.py:15
  9.9 2.8 %collective-permute-start.11 = (bf16[3,16,288]{2,1,0:T(8,128)(2,1)S(1)}, bf16[3,16,288]{2,1,0:T(8,128)(2,1)S(1)}, u32[]{:S(2)}, u32[]{:S(2)}) collective-permute-start(bf16[3,16,288]{2,1,0:T(8,128)(2,1)S(1)} %reshape.21), channel_id=1, source_target_pairs={{0,1},{1,2},{2,3},{3,0},{4,5},{5,6},{6,7},{7,4},{8,9},{9,10},{10,1... | collective-permute-start | bytes 82952 | tf_op jit(solution)/shard_map/ppermute | solution.py:15
  12.7 14.8 %collective-permute-done.2.fm_ref = bf16[2,8,32,512]{3,2,1,0:T(8,128)(2,1)S(1)} collective-permute-done((bf16[2,8,32,512]{3,2,1,0:T(8,128)(2,1)S(1)}, bf16[2,8,32,512]{3,2,1,0:T(8,128)(2,1)S(1)}, u32[]{:S(2)}, u32[]{:S(2)}) %collective-permute-start.2) | collective-permute-done | bytes 524320 | tf_op jit(solution)/shard_map/ppermute | solution.py:15
  27.5 4.0 %collective-permute-done.3.bm_ref = bf16[2,8,32,512]{3,2,1,0:T(8,128)(2,1)S(1)} collective-permute-done((bf16[2,8,32,512]{3,2,1,0:T(8,128)(2,1)S(1)}, bf16[2,8,32,512]{3,2,1,0:T(8,128)(2,1)S(1)}, u32[]{:S(2)}, u32[]{:S(2)}) %collective-permute-start.3) | collective-permute-done | bytes 524320 | tf_op jit(solution)/shard_map/ppermute | solution.py:15
  31.5 1.1 %pad_maximum_fusion = bf16[2,2,8,32,512]{4,3,2,1,0:T(8,128)(2,1)} fusion(bf16[1,2,8,32,512]{4,3,2,1,0:T(8,128)(2,1)S(1)} %bitcast.22, bf16[1,2,8,32,512]{4,3,2,1,0:T(8,128)(2,1)S(1)} %bitcast.21), kind=kLoop, calls=%fused_computation | loop fusion | flops 524288 | bytes 2097152 | tf_op jit(solution)/shard_map/stack | solution.py:27
  32.7 0.5 collective-permute-start.4
  33.2 3.1 %collective-permute-start = (bf16[2,2,32,512]{3,2,1,0:T(8,128)(2,1)S(1)}, bf16[2,2,32,512]{3,2,1,0:T(8,128)(2,1)S(1)}, u32[]{:S(2)}, u32[]{:S(2)}) collective-permute-start(bf16[2,2,32,512]{3,2,1,0:T(8,128)(2,1)S(1)} %get-tuple-element.10), channel_id=1, source_target_pairs={{0,4},{4,8},{8,12},{12,16},{16,20},{20,24},{24,28},{28,32},{32,36}... | collective-permute-start | bytes 393224 | tf_op jit(solution)/shard_map/ppermute | solution.py:15
  36.6 0.6 pad_add_fusion.place_ref
  37.2 0.7 reshape.24.keep_ref
  38.0 0.8 reshape.23.w2_ref
  38.7 4.8 %collective-permute-start.5 = (bf16[2,2,32,512]{3,2,1,0:T(8,128)(2,1)S(1)}, bf16[2,2,32,512]{3,2,1,0:T(8,128)(2,1)S(1)}, u32[]{:S(2)}, u32[]{:S(2)}) collective-permute-start(bf16[2,2,32,512]{3,2,1,0:T(8,128)(2,1)S(1)} %get-tuple-element.10), channel_id=1, source_target_pairs={{0,36},{4,40},{8,44},{12,48},{16,52},{20,56},{24,60},{28,64},{32,6... | collective-permute-start | bytes 393224 | tf_op jit(solution)/shard_map/ppermute | solution.py:15
  43.6 1.6 %collective-permute-start.1 = (bf16[2,2,32,512]{3,2,1,0:T(8,128)(2,1)S(1)}, bf16[2,2,32,512]{3,2,1,0:T(8,128)(2,1)S(1)}, u32[]{:S(2)}, u32[]{:S(2)}) collective-permute-start(bf16[2,2,32,512]{3,2,1,0:T(8,128)(2,1)S(1)} %get-tuple-element.9), channel_id=1, source_target_pairs={{0,252},{4,0},{8,4},{12,8},{16,12},{20,16},{24,20},{28,24},{32,28}... | collective-permute-start | bytes 393224 | tf_op jit(solution)/shard_map/ppermute | solution.py:15
  45.2 0.4 collective-permute-start.6
  45.6 0.7 pad_maximum_fusion.1
  46.4 6.4 %collective-permute-start.7 = (bf16[2,2,32,512]{3,2,1,0:T(8,128)(2,1)S(1)}, bf16[2,2,32,512]{3,2,1,0:T(8,128)(2,1)S(1)}, u32[]{:S(2)}, u32[]{:S(2)}) collective-permute-start(bf16[2,2,32,512]{3,2,1,0:T(8,128)(2,1)S(1)} %get-tuple-element.10), channel_id=1, source_target_pairs={{0,228},{4,232},{8,236},{12,240},{16,244},{20,248},{24,252},{28,0}... | collective-permute-start | bytes 393224 | tf_op jit(solution)/shard_map/ppermute | solution.py:15
  52.8 1.3 %collective-permute-start.8 = (bf16[2,2,32,512]{3,2,1,0:T(8,128)(2,1)S(1)}, bf16[2,2,32,512]{3,2,1,0:T(8,128)(2,1)S(1)}, u32[]{:S(2)}, u32[]{:S(2)}) collective-permute-start(bf16[2,2,32,512]{3,2,1,0:T(8,128)(2,1)S(1)} %get-tuple-element.9), channel_id=1, source_target_pairs={{0,220},{4,224},{8,228},{12,232},{16,236},{20,240},{24,244},{28,24... | collective-permute-start | bytes 393224 | tf_op jit(solution)/shard_map/ppermute | solution.py:15
  54.1 1.0 %slice_bitcast_fusion = (bf16[2,8,32,512]{3,2,1,0:T(8,128)(2,1)}, bf16[2,8,32,512]{3,2,1,0:T(8,128)(2,1)}) fusion(bf16[2,2,8,32,512]{4,3,2,1,0:T(8,128)(2,1)S(1)} %collective-permute-done.4), kind=kLoop, calls=%fused_computation.1 | loop fusion | bytes 2097152 | tf_op jit(solution)/shard_map/squeeze | solution.py:30
  55.1 8.1 %collective-permute-done.6.fb_ref = bf16[2,2,32,512]{3,2,1,0:T(8,128)(2,1)S(1)} collective-permute-done((bf16[2,2,32,512]{3,2,1,0:T(8,128)(2,1)S(1)}, bf16[2,2,32,512]{3,2,1,0:T(8,128)(2,1)S(1)}, u32[]{:S(2)}, u32[]{:S(2)}) %collective-permute-start.6) | collective-permute-done | bytes 131104 | tf_op jit(solution)/shard_map/ppermute | solution.py:15
  63.3 0.7 collective-permute-done.8.bb_ref
  64.0 0.6 copy-done.8
  64.6 14.0 %shard_map.37 = bf16[16,2,16,512]{3,2,1,0:T(8,128)(2,1)} custom-call(s32[72]{0:T(128)} %reshape.24.keep_ref, s32[5]{0:T(128)} %pad_add_fusion.place_ref, bf16[2,16,32,512]{3,2,1,0:T(8,128)(2,1)} %bitcast.20, bf16[2,2,32,512]{3,2,1,0:T(8,128)(2,1)} %copy-done.3, bf16[2,2,32,512]{3,2,1,0:T(8,128)(2,1)} %copy-done.5, bf16[2,8,32,512]{3,2,1,0:T(8,128)(2,1)} %copy-done.1, ...), custom_call_target="tpu_custom_call" | custom-call | tf_op jit(solution)/shard_map/pallas_call | solution.py:135
  (41 shorter events, 0.8 us)
Async XLA Ops:
  1.8 31.3 %copy-start = (bf16[32,2,16,512]{3,0,2,1:T(8,128)(2,1)}, bf16[32,2,16,512]{3,0,2,1:T(8,128)(2,1)S(1)}, u32[]{:S(2)}) copy-start(bf16[32,2,16,512]{3,0,2,1:T(8,128)(2,1)S(1)} %copy.13) | copy-start | bytes 3145732
  1.8 6.2 %copy-start.10 = (bf16[3,3,3,16,32]{4,3,2,1,0:T(8,128)(2,1)S(1)}, bf16[3,3,3,16,32]{4,3,2,1,0:T(8,128)(2,1)}, u32[]{:S(2)}) copy-start(bf16[3,3,3,16,32]{4,3,2,1,0:T(8,128)(2,1)} %param.4) | copy-start | bytes 82948
  1.9 25.7 %collective-permute-start.2 = (bf16[2,8,32,512]{3,2,1,0:T(8,128)(2,1)S(1)}, bf16[2,8,32,512]{3,2,1,0:T(8,128)(2,1)S(1)}, u32[]{:S(2)}, u32[]{:S(2)}) collective-permute-start(bf16[2,8,32,512]{3,2,1,0:T(8,128)(2,1)S(1)} %dynamic-slice_bitcast_fusion), channel_id=1, source_target_pairs={{0,32},{4,36},{8,40},{12,44},{16,48},{20,52},{24,56},{28,60},{32,6... | collective-permute-start | bytes 1572872 | tf_op jit(solution)/shard_map/ppermute | solution.py:15
  5.7 25.8 %collective-permute-start.3 = (bf16[2,8,32,512]{3,2,1,0:T(8,128)(2,1)S(1)}, bf16[2,8,32,512]{3,2,1,0:T(8,128)(2,1)S(1)}, u32[]{:S(2)}, u32[]{:S(2)}) collective-permute-start(bf16[2,8,32,512]{3,2,1,0:T(8,128)(2,1)S(1)} %dynamic-slice_bitcast_fusion), channel_id=1, source_target_pairs={{0,224},{4,228},{8,232},{12,236},{16,240},{20,244},{24,248},{28,25... | collective-permute-start | bytes 1572872 | tf_op jit(solution)/shard_map/ppermute | solution.py:15
  8.2 30.6 %collective-permute-start.10 = (bf16[3,16,288]{2,1,0:T(8,128)(2,1)S(1)}, bf16[3,16,288]{2,1,0:T(8,128)(2,1)S(1)}, u32[]{:S(2)}, u32[]{:S(2)}) collective-permute-start(bf16[3,16,288]{2,1,0:T(8,128)(2,1)S(1)} %reshape.21), channel_id=1, source_target_pairs={{0,2},{1,3},{2,0},{3,1},{4,6},{5,7},{6,4},{7,5},{8,10},{9,11},{10,... | collective-permute-start | bytes 82952 | tf_op jit(solution)/shard_map/ppermute | solution.py:15
  9.9 33.7 %collective-permute-start.11 = (bf16[3,16,288]{2,1,0:T(8,128)(2,1)S(1)}, bf16[3,16,288]{2,1,0:T(8,128)(2,1)S(1)}, u32[]{:S(2)}, u32[]{:S(2)}) collective-permute-start(bf16[3,16,288]{2,1,0:T(8,128)(2,1)S(1)} %reshape.21), channel_id=1, source_target_pairs={{0,1},{1,2},{2,3},{3,0},{4,5},{5,6},{6,7},{7,4},{8,9},{9,10},{10,1... | collective-permute-start | bytes 82952 | tf_op jit(solution)/shard_map/ppermute | solution.py:15
  12.7 32.5 %collective-permute-start.9 = (bf16[3,16,288]{2,1,0:T(8,128)(2,1)S(1)}, bf16[3,16,288]{2,1,0:T(8,128)(2,1)S(1)}, u32[]{:S(2)}, u32[]{:S(2)}) collective-permute-start(bf16[3,16,288]{2,1,0:T(8,128)(2,1)S(1)} %reshape.21), channel_id=1, source_target_pairs={{0,3},{1,0},{2,1},{3,2},{4,7},{5,4},{6,5},{7,6},{8,11},{9,8},{10,9... | collective-permute-start | bytes 82952 | tf_op jit(solution)/shard_map/ppermute | solution.py:15
  27.5 5.1 %copy-start.1 = (bf16[2,8,32,512]{3,2,1,0:T(8,128)(2,1)}, bf16[2,8,32,512]{3,2,1,0:T(8,128)(2,1)S(1)}, u32[]{:S(2)}) copy-start(bf16[2,8,32,512]{3,2,1,0:T(8,128)(2,1)S(1)} %collective-permute-done.2.fm_ref) | copy-start | bytes 1572868
  31.5 1.1 %copy-start.2 = (bf16[2,8,32,512]{3,2,1,0:T(8,128)(2,1)}, bf16[2,8,32,512]{3,2,1,0:T(8,128)(2,1)S(1)}, u32[]{:S(2)}) copy-start(bf16[2,8,32,512]{3,2,1,0:T(8,128)(2,1)S(1)} %collective-permute-done.3.bm_ref) | copy-start | bytes 1572868
  32.7 20.1 %collective-permute-start.4 = (bf16[2,2,8,32,512]{4,3,2,1,0:T(8,128)(2,1)}, bf16[2,2,8,32,512]{4,3,2,1,0:T(8,128)(2,1)S(1)}, u32[]{:S(2)}, u32[]{:S(2)}) collective-permute-start(bf16[2,2,8,32,512]{4,3,2,1,0:T(8,128)(2,1)} %pad_maximum_fusion), channel_id=1, source_target_pairs={{0,1},{1,0},{2,3},{3,2},{4,5},{5,4},{6,7},{7,6},{8,9},{9,8},{10,11... | collective-permute-start | bytes 3145736 | tf_op jit(solution)/shard_map/ppermute | solution.py:29
  33.2 3.2 %copy-start.9 = (bf16[3,3,3,16,64]{4,3,2,1,0:T(8,128)(2,1)S(1)}, bf16[3,3,3,16,64]{4,3,2,1,0:T(8,128)(2,1)}, u32[]{:S(2)}) copy-start(bf16[3,3,3,16,64]{4,3,2,1,0:T(8,128)(2,1)} %param.5) | copy-start | bytes 165892
  33.2 13.2 %collective-permute-start = (bf16[2,2,32,512]{3,2,1,0:T(8,128)(2,1)S(1)}, bf16[2,2,32,512]{3,2,1,0:T(8,128)(2,1)S(1)}, u32[]{:S(2)}, u32[]{:S(2)}) collective-permute-start(bf16[2,2,32,512]{3,2,1,0:T(8,128)(2,1)S(1)} %get-tuple-element.10), channel_id=1, source_target_pairs={{0,4},{4,8},{8,12},{12,16},{16,20},{20,24},{24,28},{28,32},{32,36}... | collective-permute-start | bytes 393224 | tf_op jit(solution)/shard_map/ppermute | solution.py:15
  38.7 16.4 %collective-permute-start.5 = (bf16[2,2,32,512]{3,2,1,0:T(8,128)(2,1)S(1)}, bf16[2,2,32,512]{3,2,1,0:T(8,128)(2,1)S(1)}, u32[]{:S(2)}, u32[]{:S(2)}) collective-permute-start(bf16[2,2,32,512]{3,2,1,0:T(8,128)(2,1)S(1)} %get-tuple-element.10), channel_id=1, source_target_pairs={{0,36},{4,40},{8,44},{12,48},{16,52},{20,56},{24,60},{28,64},{32,6... | collective-permute-start | bytes 393224 | tf_op jit(solution)/shard_map/ppermute | solution.py:15
  43.6 11.5 %collective-permute-start.1 = (bf16[2,2,32,512]{3,2,1,0:T(8,128)(2,1)S(1)}, bf16[2,2,32,512]{3,2,1,0:T(8,128)(2,1)S(1)}, u32[]{:S(2)}, u32[]{:S(2)}) collective-permute-start(bf16[2,2,32,512]{3,2,1,0:T(8,128)(2,1)S(1)} %get-tuple-element.9), channel_id=1, source_target_pairs={{0,252},{4,0},{8,4},{12,8},{16,12},{20,16},{24,20},{28,24},{32,28}... | collective-permute-start | bytes 393224 | tf_op jit(solution)/shard_map/ppermute | solution.py:15
  45.2 18.1 %collective-permute-start.6 = (bf16[2,2,32,512]{3,2,1,0:T(8,128)(2,1)S(1)}, bf16[2,2,32,512]{3,2,1,0:T(8,128)(2,1)S(1)}, u32[]{:S(2)}, u32[]{:S(2)}) collective-permute-start(bf16[2,2,32,512]{3,2,1,0:T(8,128)(2,1)S(1)} %get-tuple-element.9), channel_id=1, source_target_pairs={{0,28},{4,32},{8,36},{12,40},{16,44},{20,48},{24,52},{28,56},{32,6... | collective-permute-start | bytes 393224 | tf_op jit(solution)/shard_map/ppermute | solution.py:15
  46.4 8.7 %copy-start.3 = (bf16[2,2,32,512]{3,2,1,0:T(8,128)(2,1)}, bf16[2,2,32,512]{3,2,1,0:T(8,128)(2,1)S(1)}, u32[]{:S(2)}) copy-start(bf16[2,2,32,512]{3,2,1,0:T(8,128)(2,1)S(1)} %collective-permute-done.above_ref) | copy-start | bytes 393220
  46.4 16.9 %collective-permute-start.7 = (bf16[2,2,32,512]{3,2,1,0:T(8,128)(2,1)S(1)}, bf16[2,2,32,512]{3,2,1,0:T(8,128)(2,1)S(1)}, u32[]{:S(2)}, u32[]{:S(2)}) collective-permute-start(bf16[2,2,32,512]{3,2,1,0:T(8,128)(2,1)S(1)} %get-tuple-element.10), channel_id=1, source_target_pairs={{0,228},{4,232},{8,236},{12,240},{16,244},{20,248},{24,252},{28,0}... | collective-permute-start | bytes 393224 | tf_op jit(solution)/shard_map/ppermute | solution.py:15
  52.8 11.2 %collective-permute-start.8 = (bf16[2,2,32,512]{3,2,1,0:T(8,128)(2,1)S(1)}, bf16[2,2,32,512]{3,2,1,0:T(8,128)(2,1)S(1)}, u32[]{:S(2)}, u32[]{:S(2)}) collective-permute-start(bf16[2,2,32,512]{3,2,1,0:T(8,128)(2,1)S(1)} %get-tuple-element.9), channel_id=1, source_target_pairs={{0,220},{4,224},{8,228},{12,232},{16,236},{20,240},{24,244},{28,24... | collective-permute-start | bytes 393224 | tf_op jit(solution)/shard_map/ppermute | solution.py:15
  55.1 8.9 %copy-start.5 = (bf16[2,2,32,512]{3,2,1,0:T(8,128)(2,1)}, bf16[2,2,32,512]{3,2,1,0:T(8,128)(2,1)S(1)}, u32[]{:S(2)}) copy-start(bf16[2,2,32,512]{3,2,1,0:T(8,128)(2,1)S(1)} %collective-permute-done.1.below_ref) | copy-start | bytes 393220
  55.1 8.9 %copy-start.4 = (bf16[2,2,32,512]{3,2,1,0:T(8,128)(2,1)}, bf16[2,2,32,512]{3,2,1,0:T(8,128)(2,1)S(1)}, u32[]{:S(2)}) copy-start(bf16[2,2,32,512]{3,2,1,0:T(8,128)(2,1)S(1)} %collective-permute-done.5.fa_ref) | copy-start | bytes 393220
  63.3 0.7 copy-start.6
  63.3 0.7 copy-start.7
  64.0 0.6 copy-start.8
